TPU v7x, 768 devices: a whole 4x8x12 slice. The times are simulated.
768 devices in a mesh: section: 6 (over z_hi, core), seq: 16 (over x, z_lo), head: 8 (over y).
Axes of the slice: x: 4, y: 8, z: 12 (z_hi: 3, z_lo: 4; z = z_hi * 4 + z_lo), core: 2. Of those that a mesh axis runs over, the one named last changes fastest.
Arguments:
- hidden: bfloat16 [6, 4096, 4096], P('section', 'seq', 'head'), may hold values from -6 to 6
- gain: bfloat16 [6, 4096], P('section'), may hold values from 0.5 to 1.5
- w_query: bfloat16 [6, 4096, 2048], P('section', None, 'head'), may hold values from -0.0234375 to 0.0234375
- w_key: bfloat16 [6, 4096, 2048], P('section', None, 'head'), may hold values from -0.09375 to 0.09375
- w_value: bfloat16 [6, 4096, 2048], P('section', None, 'head'), may hold values from -0.09375 to 0.09375
- w_out: bfloat16 [6, 2048, 4096], P('section', 'head'), may hold values from -0.5 to 0.5
- memory: bfloat16 [3072, 4096], P(('section', 'seq', 'head')), may hold values from -6 to 6
- keep: int32 [3072], P(('section', 'seq', 'head')), may hold values 0 or 1
Outputs:
- next_inputs: bfloat16 [6, 4096, 4096], P('section', 'seq', 'head')
All inputs are finite; a program needn't handle non-finite values. No bound on the sum of `keep` on one device may be relied on, other than what follows from the above.
Results may differ from a plain program's by a relative error of at most 0.014.
Values may be sent and summed in bfloat16 or wider, within the bound.
No kernel may reach another device: no remote copies, remote signals or barrier semaphores. Data moves between devices by JAX's collectives and lax.ppermute only.
A program may use at most 64 MiB of HBM per device.

v0:
```python
import jax
import jax.numpy as jnp
from jax import lax
from jax.sharding import PartitionSpec as P

HEAD_DIM = 64


mask_drop = 30.0
norm_eps = 1e-06


def from_behind(x, axis, by):
    length = lax.axis_size(axis)
    return lax.ppermute(x, axis, [(i, (i + by) % length) for i in range(length)])


def attend_terms(query, key_rows, value_rows, key_flags):
    head_count = query.shape[1] // HEAD_DIM
    query_heads = query.reshape(query.shape[0], head_count, HEAD_DIM)
    key_heads = key_rows.reshape(key_rows.shape[0], head_count, HEAD_DIM)
    value_heads = value_rows.reshape(value_rows.shape[0], head_count, HEAD_DIM)
    scores = jnp.einsum("qhd,khd->hqk", query_heads, key_heads, preferred_element_type=jnp.float32)
    scores = scores + ((key_flags.astype(jnp.float32) - 1.0) * mask_drop)[None, None, :]
    weights = jnp.exp(scores)
    numerator = jnp.einsum(
        "hqk,khd->qhd",
        weights.astype(jnp.bfloat16),
        value_heads,
        preferred_element_type=jnp.float32,
    )
    denominator = jnp.sum(weights, axis=2).T
    return (numerator.reshape(query.shape[0], head_count * HEAD_DIM), denominator)


def shards(hidden, gain, w_query, w_key, w_value, w_out, memory, keep):
    features = lax.all_gather(hidden[0], "head", axis=1, tiled=True)
    widened = features.astype(jnp.float32)
    inverse = lax.rsqrt(jnp.mean(widened * widened, axis=1, keepdims=True) + norm_eps)
    normed = (widened * inverse * gain[0].astype(jnp.float32)[None, :]).astype(jnp.bfloat16)
    query = jnp.dot(normed, w_query[0], preferred_element_type=jnp.float32).astype(jnp.bfloat16)
    encoder_rows, encoder_flags = (
        lax.all_gather(memory, ("section", "head"), axis=0, tiled=True),
        lax.all_gather(keep.astype(jnp.bfloat16), ("section", "head"), axis=0, tiled=True),
    )
    key_rows = jnp.dot(encoder_rows, w_key[0], preferred_element_type=jnp.float32).astype(
        jnp.bfloat16
    )
    value_rows = jnp.dot(encoder_rows, w_value[0], preferred_element_type=jnp.float32).astype(
        jnp.bfloat16
    )
    more_num, more_den = attend_terms(
        query,
        lax.all_gather(key_rows, "seq", axis=0, tiled=True),
        lax.all_gather(value_rows, "seq", axis=0, tiled=True),
        lax.all_gather(encoder_flags, "seq", axis=0, tiled=True),
    )
    spread = jnp.repeat(more_den, HEAD_DIM, axis=1)
    attended = (more_num / spread).astype(jnp.bfloat16)
    partial_terms = jnp.dot(attended, w_out[0], preferred_element_type=jnp.float32)
    update = lax.psum_scatter(
        partial_terms.astype(jnp.bfloat16), "head", scatter_dimension=1, tiled=True
    )
    moved = from_behind(update, "section", 1)
    return moved[None]


def solution(mesh):
    in_specs = (
        P("section", "seq", "head"),
        P("section", None),
        P("section", None, "head"),
        P("section", None, "head"),
        P("section", None, "head"),
        P("section", "head", None),
        P(("section", "seq", "head"), None),
        P(("section", "seq", "head")),
    )
    out_specs = P("section", "seq", "head")
    return jax.shard_map(shards, mesh=mesh, in_specs=in_specs, out_specs=out_specs, check_vma=False)
```

profile of v0, /device:TPU:1, one launch (start us, length us, event | category | flops | bytes accessed | tf_op | source)
XLA Modules:
  0.0 436.3 jit_solution(70736580569230915)
XLA Ops:
  6.5 0.7 all-gather.13.cloned.1.call-update
  7.3 0.0 all-gather.11.cloned.1.call-start
  7.3 0.7 all-gather.11.cloned.1.call-update
  8.0 0.0 all-gather.9.cloned.1.call-start
  8.1 111.2 %all-gather.13.cloned.1.call-done = bf16[48,4,4096]{2,1,0:T(4,128)(2,1)} async-done(((bf16[1,4,4096]{2,1,0:T(4,128)(2,1)}), bf16[48,4,4096]{2,1,0:T(4,128)(2,1)}) %all-gather.13.cloned.1.call-update) | async-done | bytes 1572880 | tf_op jit(solution)/shard_map/all_gather | solution.py:43
  119.3 3.5 reshape.34
  122.8 3.3 fusion.30
  126.1 0.0 all-gather.9.cloned.1.call-update
  126.1 0.0 all-gather.7.cloned.1.call-start
  126.2 3.3 fusion.27
  129.5 0.0 all-gather.7.cloned.1.call-update
  129.5 0.0 reduce-scatter.2.cloned.1.call-start
  129.5 1.3 dynamic-slice.1
  130.9 1.3 dynamic-slice
  133.4 0.2 dynamic-update-slice
  133.6 112.5 %all-reduce = bf16[192]{0:T(256)(128)(2,1)S(1)} all-reduce(bf16[192]{0:T(256)(128)(2,1)S(1)} %dynamic-update-slice), channel_id=1, replica_groups=mesh['section'=6,'seq'=16,'head'=8] {'section','head'}, use_global_device_ids=true, to_apply=%add | all-reduce | flops 192 | bytes 768
  246.2 0.2 dynamic-update-slice.1
  246.4 37.7 %all-reduce.1 = bf16[3072]{0:T(1024)(128)(2,1)S(1)} all-reduce(bf16[3072]{0:T(1024)(128)(2,1)S(1)} %dynamic-update-slice.1), channel_id=1, replica_groups=mesh['section'=6,'seq'=16,'head'=8] {'seq'}, use_global_device_ids=true, to_apply=%add.1 | all-reduce | flops 3072 | bytes 12288
  284.2 0.0 all-gather.11.cloned.1.call-done
  284.2 2.2 fusion.5
  286.5 2.8 fusion.22
  289.3 0.0 all-gather.9.cloned.1.call-done
  289.3 2.6 copy.14
  291.9 7.2 %fusion = (f32[4,256]{1,0:T(4,128)S(1)}, f32[4,256,3072]{2,1,0:T(8,128)}) fusion(f32[3072]{0:T(1024)S(1)} %add_multiply_fusion, bf16[256,4,64]{0,2,1:T(8,128)(2,1)S(1)} %bitcast.52, bf16[3072,4,64]{0,2,1:T(8,128)(2,1)} %bitcast.49), kind=kOutput, calls=%fused_computation.1 | convolution fusion | flops 408943616 | bytes 14303232 | tf_op jit(solution)/shard_map/qhd,khd->hqk/dot_general | solution.py:23
  299.1 40.2 %all-gather.7.cloned.1.call-done = bf16[3072,256]{1,0:T(8,128)(2,1)} async-done(((bf16[192,256]{1,0:T(8,128)(2,1)}), bf16[3072,256]{1,0:T(8,128)(2,1)}) %all-gather.7.cloned.1.call-update) | async-done | bytes 1572880 | tf_op jit(solution)/shard_map/all_gather | solution.py:55
  339.3 2.6 copy.13
  341.9 7.1 %fusion.36 = bf16[256,4,64]{0,2,1:T(8,128)(2,1)S(1)} fusion(bf16[3072,4,64]{0,2,1:T(8,128)(2,1)} %bitcast.50, f32[4,256,3072]{2,1,0:T(8,128)} %get-tuple-element.6, f32[3072]{0:T(1024)S(1)} %add_multiply_fusion, f32[256,4]{0,1:T(4,128)S(1)} %bitcast.56), kind=kOutput, calls=%fused_computation.26 | convolution fusion | flops 409075712 | bytes 14303232 | tf_op jit(solution)/shard_map/hqk,khd->qhd/dot_general | solution.py:26
  349.0 2.1 convolution_convert_fusion
  351.1 53.2 %reduce-scatter.2.cloned.1.call-done = bf16[256,512]{1,0:T(8,128)(2,1)} async-done(((bf16[256,4096]{1,0:T(8,128)(2,1)}), bf16[256,512]{1,0:T(8,128)(2,1)}) %reduce-scatter.2.cloned.1.call-update) | async-done | bytes 262160 | tf_op jit(solution)/shard_map/reduce_scatter | solution.py:61
  404.3 12.8 %collective-permute-start = (bf16[256,512]{1,0:T(8,128)(2,1)}, bf16[256,512]{1,0:T(8,128)(2,1)S(1)}, u32[]{:S(2)}, u32[]{:S(2)}) collective-permute-start(bf16[256,512]{1,0:T(8,128)(2,1)} %reduce-scatter.2.cloned.1.call-done), channel_id=1, source_target_pairs={{0,128},{128,256},{256,384},{384,512},{512,640},{640,0},{1,129},{1... | collective-permute-start | bytes 786440 | tf_op jit(solution)/shard_map/ppermute | solution.py:15
  417.0 12.0 %collective-permute-done = bf16[256,512]{1,0:T(8,128)(2,1)S(1)} collective-permute-done((bf16[256,512]{1,0:T(8,128)(2,1)}, bf16[256,512]{1,0:T(8,128)(2,1)S(1)}, u32[]{:S(2)}, u32[]{:S(2)}) %collective-permute-start) | collective-permute-done | bytes 262176 | tf_op jit(solution)/shard_map/ppermute | solution.py:15
  429.1 0.7 copy.18
  (16 shorter events, 0.1 us)
Async XLA Ops:
  6.5 342.4 %copy-start = (bf16[1,256,4096]{2,1,0:T(8,128)(2,1)S(1)}, bf16[1,256,4096]{2,1,0:T(8,128)(2,1)}, u32[]{:S(2)}) copy-start(bf16[1,256,4096]{2,1,0:T(8,128)(2,1)} %param.13) | copy-start | bytes 6291460
  6.5 112.8 %all-gather.13.cloned.1.call-start = ((), (), s32[]{:S(2)}) async-start(), calls=%async_computation.5 | async-start | bytes 1605632 | tf_op jit(solution)/shard_map/all_gather | solution.py:43
  7.3 276.9 %all-gather.11.cloned.1.call-start = ((), (), s32[]{:S(2)}) async-start(), calls=%async_computation.4 | async-start | bytes 2359296 | tf_op jit(solution)/shard_map/all_gather | solution.py:37
  8.0 281.3 %all-gather.9.cloned.1.call-start = ((), (), s32[]{:S(2)}) async-start(), calls=%async_computation.2 | async-start | bytes 1671168 | tf_op jit(solution)/shard_map/all_gather | solution.py:54
  126.1 6.1 %copy-start.3 = (s32[4]{0:T(128)S(1)}, s32[4]{0:T(128)}, u32[]{:S(2)}) copy-start(s32[4]{0:T(128)} %param.15) | copy-start | bytes 52
  126.1 6.0 %copy-start.2 = (bf16[1,4096]{1,0:T(2,128)(2,1)S(1)}, bf16[1,4096]{1,0:T(2,128)(2,1)}, u32[]{:S(2)}) copy-start(bf16[1,4096]{1,0:T(2,128)(2,1)} %param.9) | copy-start | bytes 24580
  126.1 213.1 %all-gather.7.cloned.1.call-start = ((), (), s32[]{:S(2)}) async-start(), calls=%async_computation.1 | async-start | bytes 1671168 | tf_op jit(solution)/shard_map/all_gather | solution.py:55
  129.5 274.8 %reduce-scatter.2.cloned.1.call-start = ((), (), s32[]{:S(2)}) async-start(), calls=%async_computation.3 | async-start | bytes 2359296 | tf_op jit(solution)/shard_map/reduce_scatter | solution.py:61
  284.2 2.3 copy-start.1
  404.3 24.8 %collective-permute-start = (bf16[256,512]{1,0:T(8,128)(2,1)}, bf16[256,512]{1,0:T(8,128)(2,1)S(1)}, u32[]{:S(2)}, u32[]{:S(2)}) collective-permute-start(bf16[256,512]{1,0:T(8,128)(2,1)} %reduce-scatter.2.cloned.1.call-done), channel_id=1, source_target_pairs={{0,128},{128,256},{256,384},{384,512},{512,640},{640,0},{1,129},{1... | collective-permute-start | bytes 786440 | tf_op jit(solution)/shard_map/ppermute | solution.py:15
Sparse Core Ops, SparseCore 0:
  11.4 107.8 all-gather.12
  121.7 38.2 all-gather.10
  162.3 84.3 all-gather.8
  248.9 90.3 all-gather.6
  351.2 53.0 reduce-scatter.1
where the time goes:
time: 437 us; the launch traced here: 436 us
  waiting for transfers between devices  218 us (50%)
  blocking collectives  150 us (34%)
  matrix products  25.7 us (6%)
  between operations  14.4 us (3%)
  starting transfers between devices  12.9 us (3%)
  local copies, waits for them, and re-layouts  12.5 us (3%)
    unnamed x2, blocking collectives  150 us
    all_gather x1, waiting for transfers between devices, shards(): lax.all_gather(memory, ('section', 'head'), axis=0, tiled=True)  111 us
    reduce_scatter x1, waiting for transfers between devices, shards(): lax.psum_scatter(partial_terms.astype(jnp.bfloat16), 'head', scatter_dime...  53.2 us
    all_gather x1, waiting for transfers between devices, shards(): lax.all_gather(value_rows, 'seq', axis=0, tiled=True)  40.2 us
    ppermute x1, starting transfers between devices, from_behind(): lax.ppermute(x, axis, [(i, (i + by) % length) for i in range(length)])  12.8 us
    ppermute x1, waiting for transfers between devices, from_behind(): lax.ppermute(x, axis, [(i, (i + by) % length) for i in range(length)])  12 us
  transfers between devices with their start and end apart: 6, of which 4 were waited for; matrix products, arithmetic and copies ran while one was open for 6% of the time, Pallas kernels for 0%

commit v1 on v0

v1 whole, which is shorter than its diff:
```python
import jax
import jax.numpy as jnp
from jax import lax
from jax.sharding import Mesh, PartitionSpec as P

HEAD_DIM = 64
FLAG_PAD = 128

mask_drop = 30.0
norm_eps = 1e-06

SECTION = ("zh", "core")
SEQ = ("x", "zl")
HEAD = "y"


def shifted(x, axis, by):
    length = lax.axis_size(axis)
    return lax.ppermute(x, axis, [(i, (i + by) % length) for i in range(length)])


def ring_gather(x, axis):
    length = lax.axis_size(axis)
    pieces = {0: x}
    left, right = x, x
    for step in range(1, length // 2 + 1):
        left = shifted(left, axis, 1)
        pieces[-step % length] = left
        if step < length - step:
            right = shifted(right, axis, -1)
            pieces[step] = right
    ordered = jnp.stack([pieces[r] for r in range(length)])
    return jnp.roll(ordered, lax.axis_index(axis), axis=0)


def attend_terms(query, key_rows, value_rows, key_flags):
    head_count = query.shape[1] // HEAD_DIM
    query_heads = query.reshape(query.shape[0], head_count, HEAD_DIM)
    key_heads = key_rows.reshape(key_rows.shape[0], head_count, HEAD_DIM)
    value_heads = value_rows.reshape(value_rows.shape[0], head_count, HEAD_DIM)
    scores = jnp.einsum("qhd,khd->hqk", query_heads, key_heads, preferred_element_type=jnp.float32)
    scores = scores + ((key_flags.astype(jnp.float32) - 1.0) * mask_drop)[None, None, :]
    weights = jnp.exp(scores)
    numerator = jnp.einsum(
        "hqk,khd->qhd",
        weights.astype(jnp.bfloat16),
        value_heads,
        preferred_element_type=jnp.float32,
    )
    denominator = jnp.sum(weights, axis=2).T
    return (numerator.reshape(query.shape[0], head_count * HEAD_DIM), denominator)


def shards(hidden, gain, w_query, w_key, w_value, w_out, memory, keep):
    model = memory.shape[1]
    flags = jnp.zeros((memory.shape[0], FLAG_PAD), jnp.bfloat16)
    flags = flags.at[:, 0].set(keep.astype(jnp.bfloat16))
    packed = jnp.concatenate([memory, flags], axis=1)
    packed = lax.all_gather(packed, "core", axis=0, tiled=True)
    packed = lax.all_gather(packed, "zh", axis=0, tiled=True)
    packed = lax.all_gather(packed, HEAD, axis=0, tiled=True)
    encoder_rows = packed[:, :model]
    key_rows = jnp.dot(encoder_rows, w_key[0], preferred_element_type=jnp.float32).astype(jnp.bfloat16)
    value_rows = jnp.dot(encoder_rows, w_value[0], preferred_element_type=jnp.float32).astype(
        jnp.bfloat16
    )
    width = key_rows.shape[1]
    kv = jnp.concatenate([key_rows, value_rows, packed[:, model:]], axis=1)
    kv = lax.all_gather(kv, "zl", axis=0, tiled=True)
    kv = lax.all_gather(kv, "x", axis=0, tiled=True)

    local = hidden[0]
    gathered = ring_gather(local, HEAD)
    features = jnp.transpose(gathered, (1, 0, 2)).reshape(local.shape[0], -1)
    widened = features.astype(jnp.float32)
    inverse = lax.rsqrt(jnp.mean(widened * widened, axis=1, keepdims=True) + norm_eps)
    normed = (widened * inverse * gain[0].astype(jnp.float32)[None, :]).astype(jnp.bfloat16)
    query = jnp.dot(normed, w_query[0], preferred_element_type=jnp.float32).astype(jnp.bfloat16)

    more_num, more_den = attend_terms(
        query, kv[:, :width], kv[:, width : 2 * width], kv[:, 2 * width]
    )
    spread = jnp.repeat(more_den, HEAD_DIM, axis=1)
    attended = (more_num / spread).astype(jnp.bfloat16)
    partial_terms = jnp.dot(attended, w_out[0], preferred_element_type=jnp.float32)
    update = lax.psum_scatter(
        partial_terms.astype(jnp.bfloat16), HEAD, scatter_dimension=1, tiled=True
    )
    moved = shifted(update, SECTION, 1)
    return moved[None]


def solution(mesh):
    sizes = dict(mesh.shape)
    devices = mesh.devices.reshape(
        sizes["section"] // 2, 2, 4, sizes["seq"] // 4, sizes["head"]
    )
    fine = Mesh(devices, ("zh", "core", "x", "zl", "y"))
    everything = SECTION + SEQ + (HEAD,)
    in_specs = (
        P(SECTION, SEQ, HEAD),
        P(SECTION, None),
        P(SECTION, None, HEAD),
        P(SECTION, None, HEAD),
        P(SECTION, None, HEAD),
        P(SECTION, HEAD, None),
        P(everything, None),
        P(everything),
    )
    out_specs = P(SECTION, SEQ, HEAD)
    return jax.shard_map(shards, mesh=fine, in_specs=in_specs, out_specs=out_specs, check_vma=False)
```

time: 437 us -> 256 us (0.59)
  blocking collectives: 150 us -> 45.5 us
  waiting for transfers between devices: 218 us -> 117 us
  starting transfers between devices: 12.9 us -> 34.5 us
  matrix products: 25.7 us -> 12 us
  local copies, waits for them, and re-layouts: 12.5 us -> 24 us
  other arithmetic: 2.27 us -> 8.54 us
    unnamed x2 -> x0, blocking collectives: 150 us -> none
    all_gather x4 -> x2, waiting for transfers between devices: 151 us -> 45.2 us  [the longest x1 41.5 us: shards(): packed = lax.all_gather(packed, HEAD, axis=0, tiled=True)]
    all_gather x0 -> x3, blocking collectives: none -> 45.5 us  [the longest x1 19.9 us: shards(): kv = lax.all_gather(kv, 'zl', axis=0, tiled=True)]
    ppermute x1 -> x8, starting transfers between devices: 12.8 us -> 34.4 us  [shifted(): lax.ppermute(x, axis, [(i, (i + by) % length) for i in range(length)])]
    ppermute x1 -> x8, waiting for transfers between devices: 12 us -> 23.6 us  [shifted(): lax.ppermute(x, axis, [(i, (i + by) % length) for i in range(length)])]
    slice x0 -> x5, local copies, waits for them, and re-layouts: none -> 9.11 us  [the longest x2 6.42 us: shards(): kv[:, :width]]
    unnamed x16 -> x33, local copies, waits for them, and re-layouts: 7.31 us -> 14.2 us
    all_gather x2 -> x0, local copies, waits for them, and re-layouts: 5.22 us -> none  [the longest x1 2.61 us: shards(): lax.all_gather(key_rows, 'seq', axis=0, tiled=True)]
  transfers between devices with their start and end apart: 6 -> 11, of which waited for: 4 -> 8; matrix products, arithmetic and copies ran while one was open for 6% -> 7% of each run, Pallas kernels for 0% -> 0%
where the time goes in v1:
time: 256 us; the launch traced here: 255 us
  waiting for transfers between devices  117 us (46%)
  blocking collectives  45.5 us (18%)
  starting transfers between devices  34.5 us (13%)
  local copies, waits for them, and re-layouts  24 us (9%)
  between operations  13.4 us (5%)
  matrix products  12 us (5%)
  other arithmetic  8.54 us (3%)
    reduce_scatter x1, waiting for transfers between devices, shards(): lax.psum_scatter(partial_terms.astype(jnp.bfloat16), HEAD, scatter_dimens...  48.3 us
    all_gather x1, waiting for transfers between devices, shards(): packed = lax.all_gather(packed, HEAD, axis=0, tiled=True)  41.5 us
    ppermute x8, starting transfers between devices, shifted(): lax.ppermute(x, axis, [(i, (i + by) % length) for i in range(length)])  34.4 us
    ppermute x8, waiting for transfers between devices, shifted(): lax.ppermute(x, axis, [(i, (i + by) % length) for i in range(length)])  23.6 us
    all_gather x1, blocking collectives, shards(): kv = lax.all_gather(kv, 'zl', axis=0, tiled=True)  19.9 us
    unnamed x33, local copies, waits for them, and re-layouts  14.2 us
    all_gather x1, blocking collectives, shards(): packed = lax.all_gather(packed, 'zh', axis=0, tiled=True)  13.6 us
    all_gather x1, blocking collectives, shards(): packed = lax.all_gather(packed, 'core', axis=0, tiled=True)  12 us
  transfers between devices with their start and end apart: 11, of which 8 were waited for; matrix products, arithmetic and copies ran while one was open for 7% of the time, Pallas kernels for 0%

profile of v1, /device:TPU:1, one launch (start us, length us, event | category | flops | bytes accessed | tf_op | source)
XLA Modules:
  0.0 255.1 jit_solution(10632676131520685982)
XLA Ops:
  7.2 1.3 fusion.42
  9.4 12.0 %all-gather = bf16[2,4,4224]{2,1,0:T(4,128)(2,1)S(1)} all-gather(bf16[1,4,4224]{2,1,0:T(4,128)(2,1)S(1)} %fusion.41), channel_id=1, replica_groups=mesh['zh'=3,'core'=2,'x'=4,'zl'=4,'y'=8] {'core'}, dimensions={0}, use_global_device_ids=true | all-gather | bytes 101376 | tf_op jit(solution)/shard_map/all_gather | solution.py:59
  21.4 13.6 %all_gather.16 = bf16[24,4224]{1,0:T(8,128)(2,1)} all-gather(bf16[8,4224]{1,0:T(8,128)(2,1)S(1)} %reshape.79), channel_id=1, replica_groups=mesh['zh'=3,'core'=2,'x'=4,'zl'=4,'y'=8] {'zh'}, dimensions={0}, use_global_device_ids=true | all-gather | bytes 270336 | tf_op jit(solution)/shard_map/all_gather | solution.py:60
  35.1 41.5 %all-gather.4.cloned.1.call-done = bf16[192,4224]{1,0:T(8,128)(2,1)} async-done(((bf16[24,4224]{1,0:T(8,128)(2,1)}), bf16[192,4224]{1,0:T(8,128)(2,1)}) %all-gather.4.cloned.1.call-update) | async-done | bytes 1622032 | tf_op jit(solution)/shard_map/all_gather | solution.py:61
  76.6 2.8 %fusion.28 = bf16[192,256]{1,0:T(8,128)(2,1)S(1)} fusion(bf16[1,4096,256]{2,1,0:T(8,128)(2,1)} %param.14, bf16[192,4224]{1,0:T(8,128)(2,1)} %all-gather.4.cloned.1.call-done), kind=kOutput, calls=%fused_computation.24 | convolution fusion | flops 402702336 | bytes 3768320 | tf_op jit(solution)/shard_map/dot_general | solution.py:64
  80.4 19.9 %all_gather.18 = bf16[768,640]{1,0:T(8,128)(2,1)} all-gather(bf16[192,640]{1,0:T(8,128)(2,1)S(1)} %pad_maximum_fusion), channel_id=1, replica_groups=mesh['zh'=3,'core'=2,'x'=4,'zl'=4,'y'=8] {'zl'}, dimensions={0}, use_global_device_ids=true | all-gather | bytes 1228800 | tf_op jit(solution)/shard_map/all_gather | solution.py:69
  100.5 2.0 collective-permute-start.3
  102.5 4.5 %collective-permute-start = (bf16[256,512]{0,1:T(8,128)(2,1)S(1)}, bf16[256,512]{0,1:T(8,128)(2,1)S(1)}, u32[]{:S(2)}, u32[]{:S(2)}) collective-permute-start(bf16[256,512]{0,1:T(8,128)(2,1)S(1)} %bitcast.67), channel_id=1, source_target_pairs={{0,7},{1,0},{2,1},{3,2},{4,3},{5,4},{6,5},{7,6},{8,15},{9,8},{10,9... | collective-permute-start | bytes 786440 | tf_op jit(solution)/shard_map/ppermute | solution.py:19
  107.0 1.8 collective-permute-done.3
  108.8 1.9 collective-permute-start.4
  110.7 4.6 %collective-permute-start.1 = (bf16[256,512]{0,1:T(8,128)(2,1)S(1)}, bf16[256,512]{0,1:T(8,128)(2,1)}, u32[]{:S(2)}, u32[]{:S(2)}) collective-permute-start(bf16[256,512]{0,1:T(8,128)(2,1)S(1)} %collective-permute-done), channel_id=1, source_target_pairs={{0,7},{1,0},{2,1},{3,2},{4,3},{5,4},{6,5},{7,6},{8,15},{9,8},{10,9... | collective-permute-start | bytes 786440 | tf_op jit(solution)/shard_map/ppermute | solution.py:19
  116.1 1.1 collective-permute-done.4
  117.1 2.0 collective-permute-start.5
  119.3 4.6 %collective-permute-start.2 = (bf16[256,512]{0,1:T(8,128)(2,1)}, bf16[256,512]{0,1:T(8,128)(2,1)S(1)}, u32[]{:S(2)}, u32[]{:S(2)}) collective-permute-start(bf16[256,512]{0,1:T(8,128)(2,1)} %collective-permute-done.1), channel_id=1, source_target_pairs={{0,7},{1,0},{2,1},{3,2},{4,3},{5,4},{6,5},{7,6},{8,15},{9,8},{10,9... | collective-permute-start | bytes 786440 | tf_op jit(solution)/shard_map/ppermute | solution.py:19
  124.7 2.3 collective-permute-done.5
  126.9 1.9 collective-permute-start.6
  128.8 1.7 bitcast_dynamic-update-slice_fusion.10
  131.2 6.5 %collective-permute-done.6 = bf16[256,512]{0,1:T(8,128)(2,1)S(1)} collective-permute-done((bf16[256,512]{0,1:T(8,128)(2,1)S(1)}, bf16[256,512]{0,1:T(8,128)(2,1)S(1)}, u32[]{:S(2)}, u32[]{:S(2)}) %collective-permute-start.6) | collective-permute-done | bytes 262176 | tf_op jit(solution)/shard_map/ppermute | solution.py:19
  142.0 1.7 bitcast_dynamic-update-slice_fusion.11
  147.4 2.2 fusion.5
  149.5 2.0 fusion.7
  152.5 3.7 %all-gather.6.cloned.1.call-done = bf16[3072,640]{1,0:T(8,128)(2,1)} async-done(((bf16[768,640]{1,0:T(8,128)(2,1)}), bf16[3072,640]{1,0:T(8,128)(2,1)}) %all-gather.6.cloned.1.call-update) | async-done | bytes 3932176 | tf_op jit(solution)/shard_map/all_gather | solution.py:70
  156.2 3.8 %fusion.43 = (bf16[3072,256]{1,0:T(8,128)(2,1)}, bf16[3072,256]{1,0:T(8,128)(2,1)}) fusion(bf16[3072,640]{1,0:T(8,128)(2,1)} %all-gather.6.cloned.1.call-done), kind=kLoop, calls=%fused_computation.53 | loop fusion | bytes 6291456 | tf_op jit(solution)/shard_map/slice | solution.py:81
  160.0 2.6 %copy.23 = bf16[3072,256]{0,1:T(8,128)(2,1)} copy(bf16[3072,256]{1,0:T(8,128)(2,1)} %get-tuple-element.17) | data formatting | bytes 3145728 | tf_op jit(solution)/shard_map/slice | solution.py:81
  162.6 2.7 %copy.19 = bf16[3072,256]{0,1:T(8,128)(2,1)} copy(bf16[3072,256]{1,0:T(8,128)(2,1)} %get-tuple-element.18) | data formatting | bytes 3145728 | tf_op jit(solution)/shard_map/slice | solution.py:81
  165.3 1.6 multiply_reduce_fusion
  166.9 3.6 %fusion = (f32[4,256]{1,0:T(4,128)S(1)}, f32[4,256,3072]{2,1,0:T(8,128)S(1)}) fusion(f32[3072]{0:T(1024)S(1)} %multiply_reduce_fusion, bf16[256,4,64]{0,2,1:T(8,128)(2,1)S(1)} %bitcast.70, bf16[3072,4,64]{0,2,1:T(8,128)(2,1)} %bitcast.64), kind=kOutput, calls=%fused_computation.1 | convolution fusion | flops 408943616 | bytes 14303232 | tf_op jit(solution)/shard_map/qhd,khd->hqk/dot_general | solution.py:41
  170.6 2.0 fusion.36
  172.6 2.1 convolution_convert_fusion
  174.7 48.3 %reduce-scatter.2.cloned.1.call-done = bf16[256,512]{1,0:T(8,128)(2,1)} async-done(((bf16[256,4096]{1,0:T(8,128)(2,1)}), bf16[256,512]{1,0:T(8,128)(2,1)}) %reduce-scatter.2.cloned.1.call-update) | async-done | bytes 262160 | tf_op jit(solution)/shard_map/reduce_scatter | solution.py:86
  223.0 12.9 %collective-permute-start.7 = (bf16[256,512]{1,0:T(8,128)(2,1)}, bf16[256,512]{1,0:T(8,128)(2,1)S(1)}, u32[]{:S(2)}, u32[]{:S(2)}) collective-permute-start(bf16[256,512]{1,0:T(8,128)(2,1)} %reduce-scatter.2.cloned.1.call-done), channel_id=1, source_target_pairs={{0,128},{128,256},{256,384},{384,512},{512,640},{640,0},{1,129},{1... | collective-permute-start | bytes 786440 | tf_op jit(solution)/shard_map/ppermute | solution.py:19
  235.9 12.0 %collective-permute-done.7 = bf16[256,512]{1,0:T(8,128)(2,1)S(1)} collective-permute-done((bf16[256,512]{1,0:T(8,128)(2,1)}, bf16[256,512]{1,0:T(8,128)(2,1)S(1)}, u32[]{:S(2)}, u32[]{:S(2)}) %collective-permute-start.7) | collective-permute-done | bytes 262176 | tf_op jit(solution)/shard_map/ppermute | solution.py:19
  (51 shorter events, 14.7 us)
Async XLA Ops:
  6.5 166.1 %copy-start = (bf16[1,256,4096]{2,1,0:T(8,128)(2,1)S(1)}, bf16[1,256,4096]{2,1,0:T(8,128)(2,1)}, u32[]{:S(2)}) copy-start(bf16[1,256,4096]{2,1,0:T(8,128)(2,1)} %param.15) | copy-start | bytes 6291460
  6.5 70.0 %all-gather.4.cloned.1.call-start = ((), (), s32[]{:S(2)}) async-start(), calls=%async_computation.1 | async-start | bytes 1824768 | tf_op jit(solution)/shard_map/all_gather | solution.py:61
  35.0 121.2 %all-gather.6.cloned.1.call-start = ((), (), s32[]{:S(2)}) async-start(), calls=%async_computation.2 | async-start | bytes 4915200 | tf_op jit(solution)/shard_map/all_gather | solution.py:70
  76.6 2.8 %copy-start.3 = (bf16[192,4224]{1,0:T(8,128)(2,1)S(1)}, bf16[192,4224]{1,0:T(8,128)(2,1)}, u32[]{:S(2)}) copy-start(bf16[192,4224]{1,0:T(8,128)(2,1)} %all-gather.4.cloned.1.call-done) | copy-start | bytes 4866052
  76.6 3.2 %copy-start.5 = (bf16[1,4096,256]{2,1,0:T(8,128)(2,1)S(1)}, bf16[1,4096,256]{2,1,0:T(8,128)(2,1)}, u32[]{:S(2)}) copy-start(bf16[1,4096,256]{2,1,0:T(8,128)(2,1)} %param.13) | copy-start | bytes 6291460
  76.6 3.8 %slice-start = ((bf16[192,4224]{1,0:T(8,128)(2,1)}), bf16[192,128]{1,0:T(8,128)(2,1)S(1)}, s32[]{:S(2)}) async-start(bf16[192,4224]{1,0:T(8,128)(2,1)} %all-gather.4.cloned.1.call-done), calls=%async_computation.4 | async-start | bytes 98304 | tf_op jit(solution)/shard_map/slice | solution.py:68
  79.8 20.6 %copy-start.2 = (bf16[1,256,512]{2,1,0:T(8,128)(2,1)S(1)}, bf16[1,256,512]{2,1,0:T(8,128)(2,1)}, u32[]{:S(2)}) copy-start(bf16[1,256,512]{2,1,0:T(8,128)(2,1)} %param.10) | copy-start | bytes 786436
  79.8 39.4 %copy-start.4 = (bf16[1,4096]{1,0:T(2,128)(2,1)S(1)}, bf16[1,4096]{1,0:T(2,128)(2,1)}, u32[]{:S(2)}) copy-start(bf16[1,4096]{1,0:T(2,128)(2,1)} %param.11) | copy-start | bytes 24580
  100.3 122.7 %reduce-scatter.2.cloned.1.call-start = ((), (), s32[]{:S(2)}) async-start(), calls=%async_computation.3 | async-start | bytes 2359296 | tf_op jit(solution)/shard_map/reduce_scatter | solution.py:86
  100.5 8.3 %collective-permute-start.3 = (bf16[256,512]{0,1:T(8,128)(2,1)S(1)}, bf16[256,512]{0,1:T(8,128)(2,1)S(1)}, u32[]{:S(2)}, u32[]{:S(2)}) collective-permute-start(bf16[256,512]{0,1:T(8,128)(2,1)S(1)} %bitcast.66), channel_id=1, source_target_pairs={{0,1},{1,2},{2,3},{3,4},{4,5},{5,6},{6,7},{7,0},{8,9},{9,10},{10,1... | collective-permute-start | bytes 786440 | tf_op jit(solution)/shard_map/ppermute | solution.py:19
  102.5 8.2 %collective-permute-start = (bf16[256,512]{0,1:T(8,128)(2,1)S(1)}, bf16[256,512]{0,1:T(8,128)(2,1)S(1)}, u32[]{:S(2)}, u32[]{:S(2)}) collective-permute-start(bf16[256,512]{0,1:T(8,128)(2,1)S(1)} %bitcast.67), channel_id=1, source_target_pairs={{0,7},{1,0},{2,1},{3,2},{4,3},{5,4},{6,5},{7,6},{8,15},{9,8},{10,9... | collective-permute-start | bytes 786440 | tf_op jit(solution)/shard_map/ppermute | solution.py:19
  108.8 8.3 %collective-permute-start.4 = (bf16[256,512]{0,1:T(8,128)(2,1)S(1)}, bf16[256,512]{0,1:T(8,128)(2,1)S(1)}, u32[]{:S(2)}, u32[]{:S(2)}) collective-permute-start(bf16[256,512]{0,1:T(8,128)(2,1)S(1)} %collective-permute-done.3), channel_id=1, source_target_pairs={{0,1},{1,2},{2,3},{3,4},{4,5},{5,6},{6,7},{7,0},{8,9},{9,10},{10,1... | collective-permute-start | bytes 786440 | tf_op jit(solution)/shard_map/ppermute | solution.py:19
  110.7 8.5 %collective-permute-start.1 = (bf16[256,512]{0,1:T(8,128)(2,1)S(1)}, bf16[256,512]{0,1:T(8,128)(2,1)}, u32[]{:S(2)}, u32[]{:S(2)}) collective-permute-start(bf16[256,512]{0,1:T(8,128)(2,1)S(1)} %collective-permute-done), channel_id=1, source_target_pairs={{0,7},{1,0},{2,1},{3,2},{4,3},{5,4},{6,5},{7,6},{8,15},{9,8},{10,9... | collective-permute-start | bytes 786440 | tf_op jit(solution)/shard_map/ppermute | solution.py:19
  117.1 9.8 %collective-permute-start.5 = (bf16[256,512]{0,1:T(8,128)(2,1)S(1)}, bf16[256,512]{0,1:T(8,128)(2,1)S(1)}, u32[]{:S(2)}, u32[]{:S(2)}) collective-permute-start(bf16[256,512]{0,1:T(8,128)(2,1)S(1)} %collective-permute-done.4), channel_id=1, source_target_pairs={{0,1},{1,2},{2,3},{3,4},{4,5},{5,6},{6,7},{7,0},{8,9},{9,10},{10,1... | collective-permute-start | bytes 786440 | tf_op jit(solution)/shard_map/ppermute | solution.py:19
  119.3 11.2 %collective-permute-start.2 = (bf16[256,512]{0,1:T(8,128)(2,1)}, bf16[256,512]{0,1:T(8,128)(2,1)S(1)}, u32[]{:S(2)}, u32[]{:S(2)}) collective-permute-start(bf16[256,512]{0,1:T(8,128)(2,1)} %collective-permute-done.1), channel_id=1, source_target_pairs={{0,7},{1,0},{2,1},{3,2},{4,3},{5,4},{6,5},{7,6},{8,15},{9,8},{10,9... | collective-permute-start | bytes 786440 | tf_op jit(solution)/shard_map/ppermute | solution.py:19
  126.9 10.8 %collective-permute-start.6 = (bf16[256,512]{0,1:T(8,128)(2,1)S(1)}, bf16[256,512]{0,1:T(8,128)(2,1)S(1)}, u32[]{:S(2)}, u32[]{:S(2)}) collective-permute-start(bf16[256,512]{0,1:T(8,128)(2,1)S(1)} %collective-permute-done.5), channel_id=1, source_target_pairs={{0,1},{1,2},{2,3},{3,4},{4,5},{5,6},{6,7},{7,0},{8,9},{9,10},{10,1... | collective-permute-start | bytes 786440 | tf_op jit(solution)/shard_map/ppermute | solution.py:19
  144.4 7.1 %copy-start.6 = (bf16[1,4096,256]{2,1,0:T(8,128)(2,1)S(1)}, bf16[1,4096,256]{2,1,0:T(8,128)(2,1)}, u32[]{:S(2)}) copy-start(bf16[1,4096,256]{2,1,0:T(8,128)(2,1)} %param.12) | copy-start | bytes 6291460
  166.9 3.6 %copy-start.1 = (bf16[3072,256]{0,1:T(8,128)(2,1)S(1)}, bf16[3072,256]{0,1:T(8,128)(2,1)}, u32[]{:S(2)}) copy-start(bf16[3072,256]{0,1:T(8,128)(2,1)} %copy.19) | copy-start | bytes 4718596
  223.0 24.9 %collective-permute-start.7 = (bf16[256,512]{1,0:T(8,128)(2,1)}, bf16[256,512]{1,0:T(8,128)(2,1)S(1)}, u32[]{:S(2)}, u32[]{:S(2)}) collective-permute-start(bf16[256,512]{1,0:T(8,128)(2,1)} %reduce-scatter.2.cloned.1.call-done), channel_id=1, source_target_pairs={{0,128},{128,256},{256,384},{384,512},{512,640},{640,0},{1,129},{1... | collective-permute-start | bytes 786440 | tf_op jit(solution)/shard_map/ppermute | solution.py:19
Sparse Core Ops, SparseCore 0:
  35.2 41.3 all-gather.3
  100.4 55.7 all-gather.5
  174.8 48.1 reduce-scatter.1

commit v2 on v1

--- a/solution.py
+++ b/solution.py
@@ -51,23 +51,34 @@
     return (numerator.reshape(query.shape[0], head_count * HEAD_DIM), denominator)
 
 
+def gather_rows(packed):
+    packed = lax.all_gather(packed, "core", axis=0, tiled=True)
+    packed = lax.all_gather(packed, "zh", axis=0, tiled=True)
+    return lax.all_gather(packed, HEAD, axis=0, tiled=True)
+
+
+def key_value_rows(packed, w_key, w_value, model):
+    encoder_rows = packed[:, :model]
+    key_rows = jnp.dot(encoder_rows, w_key, preferred_element_type=jnp.float32).astype(jnp.bfloat16)
+    value_rows = jnp.dot(encoder_rows, w_value, preferred_element_type=jnp.float32).astype(
+        jnp.bfloat16
+    )
+    kv = jnp.concatenate([key_rows, value_rows, packed[:, model:]], axis=1)
+    kv = lax.all_gather(kv, "zl", axis=0, tiled=True)
+    return lax.all_gather(kv, "x", axis=0, tiled=True)
+
+
 def shards(hidden, gain, w_query, w_key, w_value, w_out, memory, keep):
     model = memory.shape[1]
+    width = w_key.shape[2]
     flags = jnp.zeros((memory.shape[0], FLAG_PAD), jnp.bfloat16)
     flags = flags.at[:, 0].set(keep.astype(jnp.bfloat16))
     packed = jnp.concatenate([memory, flags], axis=1)
-    packed = lax.all_gather(packed, "core", axis=0, tiled=True)
-    packed = lax.all_gather(packed, "zh", axis=0, tiled=True)
-    packed = lax.all_gather(packed, HEAD, axis=0, tiled=True)
-    encoder_rows = packed[:, :model]
-    key_rows = jnp.dot(encoder_rows, w_key[0], preferred_element_type=jnp.float32).astype(jnp.bfloat16)
-    value_rows = jnp.dot(encoder_rows, w_value[0], preferred_element_type=jnp.float32).astype(
-        jnp.bfloat16
-    )
-    width = key_rows.shape[1]
-    kv = jnp.concatenate([key_rows, value_rows, packed[:, model:]], axis=1)
-    kv = lax.all_gather(kv, "zl", axis=0, tiled=True)
-    kv = lax.all_gather(kv, "x", axis=0, tiled=True)
+    halves = packed.shape[0] // 2
+    kv_parts = [
+        key_value_rows(gather_rows(packed[i * halves : (i + 1) * halves]), w_key[0], w_value[0], model)
+        for i in range(2)
+    ]
 
     local = hidden[0]
     gathered = ring_gather(local, HEAD)
@@ -77,17 +88,28 @@
     normed = (widened * inverse * gain[0].astype(jnp.float32)[None, :]).astype(jnp.bfloat16)
     query = jnp.dot(normed, w_query[0], preferred_element_type=jnp.float32).astype(jnp.bfloat16)
 
-    more_num, more_den = attend_terms(
-        query, kv[:, :width], kv[:, width : 2 * width], kv[:, 2 * width]
-    )
+    more_num, more_den = None, None
+    for kv in kv_parts:
+        part_num, part_den = attend_terms(
+            query, kv[:, :width], kv[:, width : 2 * width], kv[:, 2 * width]
+        )
+        if more_num is None:
+            more_num, more_den = part_num, part_den
+        else:
+            more_num, more_den = more_num + part_num, more_den + part_den
     spread = jnp.repeat(more_den, HEAD_DIM, axis=1)
     attended = (more_num / spread).astype(jnp.bfloat16)
-    partial_terms = jnp.dot(attended, w_out[0], preferred_element_type=jnp.float32)
-    update = lax.psum_scatter(
-        partial_terms.astype(jnp.bfloat16), HEAD, scatter_dimension=1, tiled=True
-    )
-    moved = shifted(update, SECTION, 1)
-    return moved[None]
+    tokens = attended.shape[0] // 2
+    moved = []
+    for i in range(2):
+        partial_terms = jnp.dot(
+            attended[i * tokens : (i + 1) * tokens], w_out[0], preferred_element_type=jnp.float32
+        )
+        update = lax.psum_scatter(
+            partial_terms.astype(jnp.bfloat16), HEAD, scatter_dimension=1, tiled=True
+        )
+        moved.append(shifted(update, SECTION, 1))
+    return jnp.concatenate(moved, axis=0)[None]
 
 
 def solution(mesh):

time: 256 us -> 331 us (1.29)
  blocking collectives: 45.5 us -> 123 us
  waiting for transfers between devices: 117 us -> 89.3 us
  starting transfers between devices: 34.5 us -> 47.3 us
  matrix products: 12 us -> 17.8 us
  local copies, waits for them, and re-layouts: 24 us -> 28.4 us
    all_gather x3 -> x8, blocking collectives: 45.5 us -> 123 us  [the longest x2 49.2 us: gather_rows(): return lax.all_gather(packed, HEAD, axis=0, tiled=True)]
    all_gather x2, waiting for transfers between devices: 45.2 us -> 2.11 us  [key_value_rows(): return lax.all_gather(kv, 'x', axis=0, tiled=True)]
    reduce_scatter x1 -> x2, waiting for transfers between devices: 48.3 us -> 74.1 us  [shards(): lax.psum_scatter(partial_terms.astype(jnp.bfloat16), HEAD, scatter_dimens...]
    ppermute x8 -> x9, starting transfers between devices: 34.4 us -> 47.2 us  [shifted(): lax.ppermute(x, axis, [(i, (i + by) % length) for i in range(length)])]
    ppermute x8 -> x9, waiting for transfers between devices: 23.6 us -> 13.1 us  [shifted(): lax.ppermute(x, axis, [(i, (i + by) % length) for i in range(length)])]
    dot_general x3 -> x6, matrix products: 5.43 us -> 11.2 us  [the longest x2 4.13 us: key_value_rows(): jnp.dot(encoder_rows, w_key, preferred_element_type=jnp.float32)]
    unnamed x33 -> x38, local copies, waits for them, and re-layouts: 14.2 us -> 16 us
    slice x2 -> x4, local copies, waits for them, and re-layouts: 6.42 us -> 7.1 us  [shards(): kv[:, :width]]
  transfers between devices with their start and end apart: 11 -> 13, of which waited for: 8 -> 5; matrix products, arithmetic and copies ran while one was open for 7% -> 10% of each run, Pallas kernels for 0% -> 0%
where the time goes in v2:
time: 331 us; the launch traced here: 330 us
  blocking collectives  123 us (37%)
  waiting for transfers between devices  89.3 us (27%)
  starting transfers between devices  47.3 us (14%)
  local copies, waits for them, and re-layouts  28.4 us (9%)
  matrix products  17.8 us (5%)
  between operations  13.5 us (4%)
  other arithmetic  10.4 us (3%)
    reduce_scatter x2, waiting for transfers between devices, shards(): lax.psum_scatter(partial_terms.astype(jnp.bfloat16), HEAD, scatter_dimens...  74.1 us
    all_gather x2, blocking collectives, gather_rows(): return lax.all_gather(packed, HEAD, axis=0, tiled=True)  49.2 us
    ppermute x9, starting transfers between devices, shifted(): lax.ppermute(x, axis, [(i, (i + by) % length) for i in range(length)])  47.2 us
    all_gather x2, blocking collectives, key_value_rows(): kv = lax.all_gather(kv, 'zl', axis=0, tiled=True)  26.3 us
    all_gather x2, blocking collectives, gather_rows(): packed = lax.all_gather(packed, 'core', axis=0, tiled=True)  24.6 us
    all_gather x2, blocking collectives, gather_rows(): packed = lax.all_gather(packed, 'zh', axis=0, tiled=True)  22.9 us
    unnamed x38, local copies, waits for them, and re-layouts  16 us
    ppermute x9, waiting for transfers between devices, shifted(): lax.ppermute(x, axis, [(i, (i + by) % length) for i in range(length)])  13.1 us
  transfers between devices with their start and end apart: 13, of which 5 were waited for; matrix products, arithmetic and copies ran while one was open for 10% of the time, Pallas kernels for 0%

profile of v2, /device:TPU:1, one launch (start us, length us, event | category | flops | bytes accessed | tf_op | source)
XLA Modules:
  0.0 329.8 jit_solution(6846822986686595968)
XLA Ops:
  9.4 12.0 %all-gather.3 = bf16[2,2,4224]{2,1,0:T(2,128)(2,1)S(1)} all-gather(bf16[1,2,4224]{2,1,0:T(2,128)(2,1)S(1)} %get-tuple-element.24), channel_id=1, replica_groups=mesh['zh'=3,'core'=2,'x'=4,'zl'=4,'y'=8] {'core'}, dimensions={0}, use_global_device_ids=true | all-gather | bytes 50688 | tf_op jit(solution)/shard_map/all_gather | solution.py:55
  21.4 11.8 %all-gather.4 = bf16[3,4,4224]{2,1,0:T(4,128)(2,1)S(1)} all-gather(bf16[1,4,4224]{2,1,0:T(4,128)(2,1)S(1)} %reshape.114), channel_id=1, replica_groups=mesh['zh'=3,'core'=2,'x'=4,'zl'=4,'y'=8] {'zh'}, dimensions={0}, use_global_device_ids=true | all-gather | bytes 135168 | tf_op jit(solution)/shard_map/all_gather | solution.py:56
  33.3 25.2 %all-gather.5 = bf16[8,12,4224]{2,1,0:T(8,128)(2,1)} all-gather(bf16[1,12,4224]{2,1,0:T(8,128)(2,1)S(1)} %reshape.116), channel_id=1, replica_groups=mesh['zh'=3,'core'=2,'x'=4,'zl'=4,'y'=8] {'y'}, dimensions={0}, use_global_device_ids=true | all-gather | bytes 912384 | tf_op jit(solution)/shard_map/all_gather | solution.py:57
  60.0 2.1 fusion.49
  62.1 2.1 fusion.43
  64.2 12.6 %all_gather.38 = bf16[384,640]{1,0:T(8,128)(2,1)} all-gather(bf16[96,640]{1,0:T(8,128)(2,1)S(1)} %pad_maximum_fusion.1), channel_id=1, replica_groups=mesh['zh'=3,'core'=2,'x'=4,'zl'=4,'y'=8] {'zl'}, dimensions={0}, use_global_device_ids=true | all-gather | bytes 614400 | tf_op jit(solution)/shard_map/all_gather | solution.py:67
  77.0 4.0 %collective-permute-start = (bf16[256,512]{0,1:T(8,128)(2,1)S(1)}, bf16[256,512]{0,1:T(8,128)(2,1)}, u32[]{:S(2)}, u32[]{:S(2)}) collective-permute-start(bf16[256,512]{0,1:T(8,128)(2,1)S(1)} %bitcast.89), channel_id=1, source_target_pairs={{0,7},{1,0},{2,1},{3,2},{4,3},{5,4},{6,5},{7,6},{8,15},{9,8},{10,9... | collective-permute-start | bytes 786440 | tf_op jit(solution)/shard_map/ppermute | solution.py:19
  81.0 1.9 collective-permute-start.3
  82.9 12.6 %all-gather = bf16[2,2,4224]{2,1,0:T(2,128)(2,1)S(1)} all-gather(bf16[1,2,4224]{2,1,0:T(2,128)(2,1)S(1)} %get-tuple-element.23), channel_id=1, replica_groups=mesh['zh'=3,'core'=2,'x'=4,'zl'=4,'y'=8] {'core'}, dimensions={0}, use_global_device_ids=true | all-gather | bytes 50688 | tf_op jit(solution)/shard_map/all_gather | solution.py:55
  95.6 11.1 %all-gather.1 = bf16[3,4,4224]{2,1,0:T(4,128)(2,1)S(1)} all-gather(bf16[1,4,4224]{2,1,0:T(4,128)(2,1)S(1)} %reshape.108), channel_id=1, replica_groups=mesh['zh'=3,'core'=2,'x'=4,'zl'=4,'y'=8] {'zh'}, dimensions={0}, use_global_device_ids=true | all-gather | bytes 135168 | tf_op jit(solution)/shard_map/all_gather | solution.py:56
  106.8 24.0 %all-gather.2 = bf16[8,12,4224]{2,1,0:T(8,128)(2,1)} all-gather(bf16[1,12,4224]{2,1,0:T(8,128)(2,1)S(1)} %reshape.110), channel_id=1, replica_groups=mesh['zh'=3,'core'=2,'x'=4,'zl'=4,'y'=8] {'y'}, dimensions={0}, use_global_device_ids=true | all-gather | bytes 912384 | tf_op jit(solution)/shard_map/all_gather | solution.py:57
  132.2 2.1 fusion.46
  134.2 2.1 fusion.40
  136.3 4.9 %collective-permute-start.1 = (bf16[256,512]{0,1:T(8,128)(2,1)}, bf16[256,512]{0,1:T(8,128)(2,1)S(1)}, u32[]{:S(2)}, u32[]{:S(2)}) collective-permute-start(bf16[256,512]{0,1:T(8,128)(2,1)} %collective-permute-done), channel_id=1, source_target_pairs={{0,7},{1,0},{2,1},{3,2},{4,3},{5,4},{6,5},{7,6},{8,15},{9,8},{10,9... | collective-permute-start | bytes 786440 | tf_op jit(solution)/shard_map/ppermute | solution.py:19
  143.2 13.7 %all_gather.33 = bf16[384,640]{1,0:T(8,128)(2,1)} all-gather(bf16[96,640]{1,0:T(8,128)(2,1)S(1)} %pad_maximum_fusion), channel_id=1, replica_groups=mesh['zh'=3,'core'=2,'x'=4,'zl'=4,'y'=8] {'zl'}, dimensions={0}, use_global_device_ids=true | all-gather | bytes 614400 | tf_op jit(solution)/shard_map/all_gather | solution.py:67
  157.7 2.2 collective-permute-start.5
  160.1 4.3 %collective-permute-start.2 = (bf16[256,512]{0,1:T(8,128)(2,1)S(1)}, bf16[256,512]{0,1:T(8,128)(2,1)S(1)}, u32[]{:S(2)}, u32[]{:S(2)}) collective-permute-start(bf16[256,512]{0,1:T(8,128)(2,1)S(1)} %collective-permute-done.1), channel_id=1, source_target_pairs={{0,7},{1,0},{2,1},{3,2},{4,3},{5,4},{6,5},{7,6},{8,15},{9,8},{10,9... | collective-permute-start | bytes 786440 | tf_op jit(solution)/shard_map/ppermute | solution.py:19
  166.2 2.1 collective-permute-start.6
  169.7 6.7 %collective-permute-done.6 = bf16[256,512]{0,1:T(8,128)(2,1)S(1)} collective-permute-done((bf16[256,512]{0,1:T(8,128)(2,1)S(1)}, bf16[256,512]{0,1:T(8,128)(2,1)S(1)}, u32[]{:S(2)}, u32[]{:S(2)}) %collective-permute-start.6) | collective-permute-done | bytes 262176 | tf_op jit(solution)/shard_map/ppermute | solution.py:19
  185.9 2.2 fusion.4
  188.2 2.0 fusion.6
  191.1 2.4 fusion.60
  193.6 2.3 copy.28
  197.0 2.1 all-gather.9.cloned.1.call-done
  199.1 2.4 fusion.59
  201.5 2.3 copy.23
  206.3 2.3 fusion.2
  216.4 40.8 %reduce-scatter.5.cloned.1.call-done = bf16[128,512]{1,0:T(8,128)(2,1)} async-done(((bf16[128,4096]{1,0:T(8,128)(2,1)}), bf16[128,512]{1,0:T(8,128)(2,1)}) %reduce-scatter.5.cloned.1.call-update) | async-done | bytes 131088 | tf_op jit(solution)/shard_map/reduce_scatter | solution.py:108
  257.2 12.9 %collective-permute-start.8 = (bf16[128,512]{1,0:T(8,128)(2,1)}, bf16[128,512]{1,0:T(8,128)(2,1)S(1)}, u32[]{:S(2)}, u32[]{:S(2)}) collective-permute-start(bf16[128,512]{1,0:T(8,128)(2,1)} %reduce-scatter.5.cloned.1.call-done), channel_id=1, source_target_pairs={{0,128},{128,256},{256,384},{384,512},{512,640},{640,0},{1,129},{1... | collective-permute-start | bytes 393224 | tf_op jit(solution)/shard_map/ppermute | solution.py:19
  270.1 33.3 %reduce-scatter.3.cloned.1.call-done = bf16[128,512]{1,0:T(8,128)(2,1)} async-done(((bf16[128,4096]{1,0:T(8,128)(2,1)}), bf16[128,512]{1,0:T(8,128)(2,1)}) %reduce-scatter.3.cloned.1.call-update) | async-done | bytes 131088 | tf_op jit(solution)/shard_map/reduce_scatter | solution.py:108
  303.4 12.9 %collective-permute-start.7 = (bf16[128,512]{1,0:T(8,128)(2,1)}, bf16[128,512]{1,0:T(8,128)(2,1)S(1)}, u32[]{:S(2)}, u32[]{:S(2)}) collective-permute-start(bf16[128,512]{1,0:T(8,128)(2,1)} %reduce-scatter.3.cloned.1.call-done), channel_id=1, source_target_pairs={{0,128},{128,256},{256,384},{384,512},{512,640},{640,0},{1,129},{1... | collective-permute-start | bytes 393224 | tf_op jit(solution)/shard_map/ppermute | solution.py:19
  316.2 6.3 %collective-permute-done.7 = bf16[128,512]{1,0:T(8,128)(2,1)S(1)} collective-permute-done((bf16[128,512]{1,0:T(8,128)(2,1)}, bf16[128,512]{1,0:T(8,128)(2,1)S(1)}, u32[]{:S(2)}, u32[]{:S(2)}) %collective-permute-start.7) | collective-permute-done | bytes 131104 | tf_op jit(solution)/shard_map/ppermute | solution.py:19
  (79 shorter events, 34.7 us)
Async XLA Ops:
  6.5 206.8 %copy-start = (bf16[1,256,4096]{2,1,0:T(8,128)(2,1)S(1)}, bf16[1,256,4096]{2,1,0:T(8,128)(2,1)}, u32[]{:S(2)}) copy-start(bf16[1,256,4096]{2,1,0:T(8,128)(2,1)} %param.15) | copy-start | bytes 6291460
  6.5 184.6 %all-gather.11.cloned.1.call-start = ((), (), s32[]{:S(2)}) async-start(), calls=%async_computation.3 | async-start | bytes 2457600 | tf_op jit(solution)/shard_map/all_gather | solution.py:68
  58.6 18.3 %copy-start.4 = (bf16[1,256,512]{2,1,0:T(8,128)(2,1)S(1)}, bf16[1,256,512]{2,1,0:T(8,128)(2,1)}, u32[]{:S(2)}) copy-start(bf16[1,256,512]{2,1,0:T(8,128)(2,1)} %param.10) | copy-start | bytes 786436
  76.8 122.3 %all-gather.9.cloned.1.call-start = ((), (), s32[]{:S(2)}) async-start(), calls=%async_computation.2 | async-start | bytes 2457600 | tf_op jit(solution)/shard_map/all_gather | solution.py:68
  77.0 59.3 %collective-permute-start = (bf16[256,512]{0,1:T(8,128)(2,1)S(1)}, bf16[256,512]{0,1:T(8,128)(2,1)}, u32[]{:S(2)}, u32[]{:S(2)}) collective-permute-start(bf16[256,512]{0,1:T(8,128)(2,1)S(1)} %bitcast.89), channel_id=1, source_target_pairs={{0,7},{1,0},{2,1},{3,2},{4,3},{5,4},{6,5},{7,6},{8,15},{9,8},{10,9... | collective-permute-start | bytes 786440 | tf_op jit(solution)/shard_map/ppermute | solution.py:19
  81.0 60.3 %collective-permute-start.3 = (bf16[256,512]{0,1:T(8,128)(2,1)S(1)}, bf16[256,512]{0,1:T(8,128)(2,1)S(1)}, u32[]{:S(2)}, u32[]{:S(2)}) collective-permute-start(bf16[256,512]{0,1:T(8,128)(2,1)S(1)} %bitcast.90), channel_id=1, source_target_pairs={{0,1},{1,2},{2,3},{3,4},{4,5},{5,6},{6,7},{7,0},{8,9},{9,10},{10,1... | collective-permute-start | bytes 786440 | tf_op jit(solution)/shard_map/ppermute | solution.py:19
  132.1 27.9 %copy-start.5 = (bf16[1,4096]{1,0:T(2,128)(2,1)S(1)}, bf16[1,4096]{1,0:T(2,128)(2,1)}, u32[]{:S(2)}) copy-start(bf16[1,4096]{1,0:T(2,128)(2,1)} %param.11) | copy-start | bytes 24580
  136.3 23.8 %collective-permute-start.1 = (bf16[256,512]{0,1:T(8,128)(2,1)}, bf16[256,512]{0,1:T(8,128)(2,1)S(1)}, u32[]{:S(2)}, u32[]{:S(2)}) collective-permute-start(bf16[256,512]{0,1:T(8,128)(2,1)} %collective-permute-done), channel_id=1, source_target_pairs={{0,7},{1,0},{2,1},{3,2},{4,3},{5,4},{6,5},{7,6},{8,15},{9,8},{10,9... | collective-permute-start | bytes 786440 | tf_op jit(solution)/shard_map/ppermute | solution.py:19
  141.3 16.5 %collective-permute-start.4 = (bf16[256,512]{0,1:T(8,128)(2,1)S(1)}, bf16[256,512]{0,1:T(8,128)(2,1)S(1)}, u32[]{:S(2)}, u32[]{:S(2)}) collective-permute-start(bf16[256,512]{0,1:T(8,128)(2,1)S(1)} %collective-permute-done.3), channel_id=1, source_target_pairs={{0,1},{1,2},{2,3},{3,4},{4,5},{5,6},{6,7},{7,0},{8,9},{9,10},{10,1... | collective-permute-start | bytes 786440 | tf_op jit(solution)/shard_map/ppermute | solution.py:19
  157.0 100.2 %reduce-scatter.5.cloned.1.call-start = ((), (), s32[]{:S(2)}) async-start(), calls=%async_computation.5 | async-start | bytes 1179648 | tf_op jit(solution)/shard_map/reduce_scatter | solution.py:108
  157.7 8.4 %collective-permute-start.5 = (bf16[256,512]{0,1:T(8,128)(2,1)S(1)}, bf16[256,512]{0,1:T(8,128)(2,1)S(1)}, u32[]{:S(2)}, u32[]{:S(2)}) collective-permute-start(bf16[256,512]{0,1:T(8,128)(2,1)S(1)} %collective-permute-done.4), channel_id=1, source_target_pairs={{0,1},{1,2},{2,3},{3,4},{4,5},{5,6},{6,7},{7,0},{8,9},{9,10},{10,1... | collective-permute-start | bytes 786440 | tf_op jit(solution)/shard_map/ppermute | solution.py:19
  160.1 8.9 %collective-permute-start.2 = (bf16[256,512]{0,1:T(8,128)(2,1)S(1)}, bf16[256,512]{0,1:T(8,128)(2,1)S(1)}, u32[]{:S(2)}, u32[]{:S(2)}) collective-permute-start(bf16[256,512]{0,1:T(8,128)(2,1)S(1)} %collective-permute-done.1), channel_id=1, source_target_pairs={{0,7},{1,0},{2,1},{3,2},{4,3},{5,4},{6,5},{7,6},{8,15},{9,8},{10,9... | collective-permute-start | bytes 786440 | tf_op jit(solution)/shard_map/ppermute | solution.py:19
  166.2 10.3 %collective-permute-start.6 = (bf16[256,512]{0,1:T(8,128)(2,1)S(1)}, bf16[256,512]{0,1:T(8,128)(2,1)S(1)}, u32[]{:S(2)}, u32[]{:S(2)}) collective-permute-start(bf16[256,512]{0,1:T(8,128)(2,1)S(1)} %collective-permute-done.5), channel_id=1, source_target_pairs={{0,1},{1,2},{2,3},{3,4},{4,5},{5,6},{6,7},{7,0},{8,9},{9,10},{10,1... | collective-permute-start | bytes 786440 | tf_op jit(solution)/shard_map/ppermute | solution.py:19
  183.1 7.0 %copy-start.6 = (bf16[1,4096,256]{2,1,0:T(8,128)(2,1)S(1)}, bf16[1,4096,256]{2,1,0:T(8,128)(2,1)}, u32[]{:S(2)}) copy-start(bf16[1,4096,256]{2,1,0:T(8,128)(2,1)} %param.12) | copy-start | bytes 6291460
  204.9 3.7 %copy-start.2 = (bf16[1536,256]{0,1:T(8,128)(2,1)S(1)}, bf16[1536,256]{0,1:T(8,128)(2,1)}, u32[]{:S(2)}) copy-start(bf16[1536,256]{0,1:T(8,128)(2,1)} %copy.28) | copy-start | bytes 2359300
  208.6 2.5 copy-start.3
  209.7 2.6 copy-start.1
  214.9 88.5 %reduce-scatter.3.cloned.1.call-start = ((), (), s32[]{:S(2)}) async-start(), calls=%async_computation.4 | async-start | bytes 1179648 | tf_op jit(solution)/shard_map/reduce_scatter | solution.py:108
  257.2 59.0 %collective-permute-start.8 = (bf16[128,512]{1,0:T(8,128)(2,1)}, bf16[128,512]{1,0:T(8,128)(2,1)S(1)}, u32[]{:S(2)}, u32[]{:S(2)}) collective-permute-start(bf16[128,512]{1,0:T(8,128)(2,1)} %reduce-scatter.5.cloned.1.call-done), channel_id=1, source_target_pairs={{0,128},{128,256},{256,384},{384,512},{512,640},{640,0},{1,129},{1... | collective-permute-start | bytes 393224 | tf_op jit(solution)/shard_map/ppermute | solution.py:19
  303.4 19.2 %collective-permute-start.7 = (bf16[128,512]{1,0:T(8,128)(2,1)}, bf16[128,512]{1,0:T(8,128)(2,1)S(1)}, u32[]{:S(2)}, u32[]{:S(2)}) collective-permute-start(bf16[128,512]{1,0:T(8,128)(2,1)} %reduce-scatter.3.cloned.1.call-done), channel_id=1, source_target_pairs={{0,128},{128,256},{256,384},{384,512},{512,640},{640,0},{1,129},{1... | collective-permute-start | bytes 393224 | tf_op jit(solution)/shard_map/ppermute | solution.py:19
Sparse Core Ops, SparseCore 0:
  76.9 44.4 all-gather.10
  157.1 41.9 all-gather.8
  215.0 42.1 reduce-scatter.4
  260.2 43.1 reduce-scatter.2

commit v3 on v1

--- a/solution.py
+++ b/solution.py
@@ -82,10 +82,12 @@
     )
     spread = jnp.repeat(more_den, HEAD_DIM, axis=1)
     attended = (more_num / spread).astype(jnp.bfloat16)
-    partial_terms = jnp.dot(attended, w_out[0], preferred_element_type=jnp.float32)
-    update = lax.psum_scatter(
-        partial_terms.astype(jnp.bfloat16), HEAD, scatter_dimension=1, tiled=True
-    )
+    out_cols = w_out.shape[2] // lax.axis_size(HEAD)
+    out_block = lax.all_to_all(
+        w_out[0].reshape(w_out.shape[1], lax.axis_size(HEAD), out_cols), HEAD, 1, 0, tiled=True
+    ).reshape(-1, out_cols)
+    every_head = lax.all_gather(attended, HEAD, axis=1, tiled=True)
+    update = jnp.dot(every_head, out_block, preferred_element_type=jnp.float32).astype(jnp.bfloat16)
     moved = shifted(update, SECTION, 1)
     return moved[None]
 

time: 256 us -> 292 us (1.14)
  waiting for transfers between devices: 117 us -> 140 us
  local copies, waits for them, and re-layouts: 24 us -> 31.9 us
  starting transfers between devices: 34.5 us -> 38.9 us
    reduce_scatter x1 -> x0, waiting for transfers between devices: 48.3 us -> none  [shards(): lax.psum_scatter(partial_terms.astype(jnp.bfloat16), HEAD, scatter_dimens...]
    all_gather x0 -> x1, waiting for transfers between devices: none -> 38.3 us  [shards(): every_head = lax.all_gather(attended, HEAD, axis=1, tiled=True)]
    ppermute x8, waiting for transfers between devices: 23.6 us -> 60.2 us  [shifted(): lax.ppermute(x, axis, [(i, (i + by) % length) for i in range(length)])]
    all_to_all x0 -> x1, starting transfers between devices: none -> 4.35 us  [shards(): lax.all_to_all(w_out[0].reshape(w_out.shape[1], lax.axis_size(HEAD), out_...]
    unnamed x33 -> x32, local copies, waits for them, and re-layouts: 14.2 us -> 18.2 us
    all_to_all x0 -> x1, local copies, waits for them, and re-layouts: none -> 3.92 us  [shards(): lax.all_to_all(w_out[0].reshape(w_out.shape[1], lax.axis_size(HEAD), out_...]
    all_gather x1, waiting for transfers between devices: 3.71 us -> 0.02 us  [shards(): kv = lax.all_gather(kv, 'x', axis=0, tiled=True)]
  transfers between devices with their start and end apart: 11 -> 12, of which waited for: 8 -> 6; matrix products, arithmetic and copies ran while one was open for 7% -> 15% of each run, Pallas kernels for 0% -> 0%
where the time goes in v3:
time: 292 us
  waiting for transfers between devices  140 us (48%)
  blocking collectives  45.5 us (16%)
  starting transfers between devices  38.9 us (13%)
  local copies, waits for them, and re-layouts  31.9 us (11%)
  between operations  13.4 us (5%)
  matrix products  13.3 us (5%)
  other arithmetic  8.54 us (3%)
    ppermute x8, waiting for transfers between devices, shifted(): lax.ppermute(x, axis, [(i, (i + by) % length) for i in range(length)])  60.2 us
    all_gather x1, waiting for transfers between devices, shards(): packed = lax.all_gather(packed, HEAD, axis=0, tiled=True)  41.5 us
    all_gather x1, waiting for transfers between devices, shards(): every_head = lax.all_gather(attended, HEAD, axis=1, tiled=True)  38.3 us
    ppermute x8, starting transfers between devices, shifted(): lax.ppermute(x, axis, [(i, (i + by) % length) for i in range(length)])  34.4 us
    all_gather x1, blocking collectives, shards(): kv = lax.all_gather(kv, 'zl', axis=0, tiled=True)  19.9 us
    unnamed x32, local copies, waits for them, and re-layouts  18.2 us
    all_gather x1, blocking collectives, shards(): packed = lax.all_gather(packed, 'zh', axis=0, tiled=True)  13.6 us
    all_gather x1, blocking collectives, shards(): packed = lax.all_gather(packed, 'core', axis=0, tiled=True)  12 us
  transfers between devices with their start and end apart: 12, of which 6 were waited for; matrix products, arithmetic and copies ran while one was open for 15% of the time, Pallas kernels for 0%

profile of v3, /device:TPU:1, one launch (start us, length us, event | category | flops | bytes accessed | tf_op | source)
XLA Modules:
  0.0 291.5 jit_solution(1871741590318790716)
XLA Ops:
  9.4 12.0 %all-gather = bf16[2,4,4224]{2,1,0:T(4,128)(2,1)S(1)} all-gather(bf16[1,4,4224]{2,1,0:T(4,128)(2,1)S(1)} %fusion.40), channel_id=1, replica_groups=mesh['zh'=3,'core'=2,'x'=4,'zl'=4,'y'=8] {'core'}, dimensions={0}, use_global_device_ids=true | all-gather | bytes 101376 | tf_op jit(solution)/shard_map/all_gather | solution.py:59
  21.4 13.6 %all_gather.19 = bf16[24,4224]{1,0:T(8,128)(2,1)} all-gather(bf16[8,4224]{1,0:T(8,128)(2,1)S(1)} %reshape.87), channel_id=1, replica_groups=mesh['zh'=3,'core'=2,'x'=4,'zl'=4,'y'=8] {'zh'}, dimensions={0}, use_global_device_ids=true | all-gather | bytes 270336 | tf_op jit(solution)/shard_map/all_gather | solution.py:60
  35.1 41.5 %all-gather.5.cloned.1.call-done = bf16[192,4224]{1,0:T(8,128)(2,1)} async-done(((bf16[24,4224]{1,0:T(8,128)(2,1)}), bf16[192,4224]{1,0:T(8,128)(2,1)}) %all-gather.5.cloned.1.call-update) | async-done | bytes 1622032 | tf_op jit(solution)/shard_map/all_gather | solution.py:61
  76.6 2.8 fusion.27
  80.4 19.9 %all_gather.21 = bf16[768,640]{1,0:T(8,128)(2,1)} all-gather(bf16[192,640]{1,0:T(8,128)(2,1)S(1)} %pad_maximum_fusion), channel_id=1, replica_groups=mesh['zh'=3,'core'=2,'x'=4,'zl'=4,'y'=8] {'zl'}, dimensions={0}, use_global_device_ids=true | all-gather | bytes 1228800 | tf_op jit(solution)/shard_map/all_gather | solution.py:69
  100.4 2.0 collective-permute-start.3
  102.5 4.5 %collective-permute-start = (bf16[256,512]{0,1:T(8,128)(2,1)S(1)}, bf16[256,512]{0,1:T(8,128)(2,1)S(1)}, u32[]{:S(2)}, u32[]{:S(2)}) collective-permute-start(bf16[256,512]{0,1:T(8,128)(2,1)S(1)} %bitcast.71), channel_id=1, source_target_pairs={{0,7},{1,0},{2,1},{3,2},{4,3},{5,4},{6,5},{7,6},{8,15},{9,8},{10,9... | collective-permute-start | bytes 786440 | tf_op jit(solution)/shard_map/ppermute | solution.py:19
  106.9 1.8 collective-permute-done.3
  108.8 1.9 collective-permute-start.4
  110.7 4.6 %collective-permute-start.1 = (bf16[256,512]{0,1:T(8,128)(2,1)S(1)}, bf16[256,512]{0,1:T(8,128)(2,1)S(1)}, u32[]{:S(2)}, u32[]{:S(2)}) collective-permute-start(bf16[256,512]{0,1:T(8,128)(2,1)S(1)} %collective-permute-done), channel_id=1, source_target_pairs={{0,7},{1,0},{2,1},{3,2},{4,3},{5,4},{6,5},{7,6},{8,15},{9,8},{10,9... | collective-permute-start | bytes 786440 | tf_op jit(solution)/shard_map/ppermute | solution.py:19
  115.3 4.1 %copy.32 = bf16[1,256,4096]{1,2,0:T(8,128)(2,1)} copy(bf16[1,256,4096]{2,1,0:T(8,128)(2,1)} %param.15) | data formatting | bytes 4194304 | tf_op args[5]
  119.3 4.4 %all-to-all-start = ((bf16[256,8,512]{0,2,1:T(8,128)(2,1)}), bf16[256,8,512]{0,2,1:T(8,128)(2,1)}, u32[]{:S(2)}, u32[]{:S(2)}) async-start(bf16[256,8,512]{0,2,1:T(8,128)(2,1)} %bitcast.68), calls=%async_computation | async-start | bytes 4194304 | tf_op jit(solution)/shard_map/all_to_all | solution.py:86
  124.5 3.2 %collective-permute-start.5 = (bf16[256,512]{0,1:T(8,128)(2,1)S(1)}, bf16[256,512]{0,1:T(8,128)(2,1)}, u32[]{:S(2)}, u32[]{:S(2)}) collective-permute-start(bf16[256,512]{0,1:T(8,128)(2,1)S(1)} %collective-permute-done.4), channel_id=1, source_target_pairs={{0,1},{1,2},{2,3},{3,4},{4,5},{5,6},{6,7},{7,0},{8,9},{9,10},{10,1... | collective-permute-start | bytes 786440 | tf_op jit(solution)/shard_map/ppermute | solution.py:19
  127.8 3.3 %collective-permute-start.2 = (bf16[256,512]{0,1:T(8,128)(2,1)S(1)}, bf16[256,512]{0,1:T(8,128)(2,1)S(1)}, u32[]{:S(2)}, u32[]{:S(2)}) collective-permute-start(bf16[256,512]{0,1:T(8,128)(2,1)S(1)} %collective-permute-done.1), channel_id=1, source_target_pairs={{0,7},{1,0},{2,1},{3,2},{4,3},{5,4},{6,5},{7,6},{8,15},{9,8},{10,9... | collective-permute-start | bytes 786440 | tf_op jit(solution)/shard_map/ppermute | solution.py:19
  131.8 41.6 %collective-permute-done.5 = bf16[256,512]{0,1:T(8,128)(2,1)} collective-permute-done((bf16[256,512]{0,1:T(8,128)(2,1)S(1)}, bf16[256,512]{0,1:T(8,128)(2,1)}, u32[]{:S(2)}, u32[]{:S(2)}) %collective-permute-start.5) | collective-permute-done | bytes 262176 | tf_op jit(solution)/shard_map/ppermute | solution.py:19
  173.4 1.9 collective-permute-start.6
  176.7 5.2 %collective-permute-done.6 = bf16[256,512]{0,1:T(8,128)(2,1)S(1)} collective-permute-done((bf16[256,512]{0,1:T(8,128)(2,1)}, bf16[256,512]{0,1:T(8,128)(2,1)S(1)}, u32[]{:S(2)}, u32[]{:S(2)}) %collective-permute-start.6) | collective-permute-done | bytes 262176 | tf_op jit(solution)/shard_map/ppermute | solution.py:19
  182.6 1.7 bitcast_dynamic-update-slice_fusion.4
  189.4 1.7 bitcast_dynamic-update-slice_fusion.5
  192.5 2.2 fusion.5
  194.7 2.0 fusion.7
  197.6 3.8 %fusion.42 = (bf16[3072,256]{1,0:T(8,128)(2,1)}, bf16[3072,256]{1,0:T(8,128)(2,1)}) fusion(bf16[3072,640]{1,0:T(8,128)(2,1)} %all-gather.7.cloned.1.call-done), kind=kLoop, calls=%fused_computation.52 | loop fusion | bytes 6291456 | tf_op jit(solution)/shard_map/slice | solution.py:81
  201.4 2.6 copy.27
  204.1 2.6 copy.31
  206.7 1.6 multiply_reduce_fusion
  208.3 3.6 %fusion = (f32[4,256]{1,0:T(4,128)S(1)}, f32[4,256,3072]{2,1,0:T(8,128)S(1)}) fusion(f32[3072]{0:T(1024)S(1)} %multiply_reduce_fusion, bf16[256,4,64]{0,2,1:T(8,128)(2,1)S(1)} %bitcast.75, bf16[3072,4,64]{0,2,1:T(8,128)(2,1)} %bitcast.67), kind=kOutput, calls=%fused_computation.1 | convolution fusion | flops 408943616 | bytes 14303232 | tf_op jit(solution)/shard_map/qhd,khd->hqk/dot_general | solution.py:41
  211.9 2.7 fusion.35
  214.7 3.9 %copy.33 = bf16[8,256,1,512]{3,1,0,2:T(8,128)(2,1)} copy(bf16[8,256,1,512]{1,3,0,2:T(8,128)(2,1)} %bitcast.23) | data formatting | bytes 4194304 | tf_op jit(solution)/shard_map/all_to_all | solution.py:86
  218.6 38.3 %all-gather.9.cloned.1.call-done = bf16[256,2048]{0,1:T(8,128)(2,1)} async-done(((bf16[256,256]{0,1:T(8,128)(2,1)}), bf16[256,2048]{0,1:T(8,128)(2,1)}) %all-gather.9.cloned.1.call-update) | async-done | bytes 1048592 | tf_op jit(solution)/shard_map/all_gather | solution.py:89
  256.9 2.6 convolution_convert_fusion
  259.5 13.1 %collective-permute-start.7 = (bf16[256,512]{1,0:T(8,128)(2,1)S(1)}, bf16[256,512]{1,0:T(8,128)(2,1)S(1)}, u32[]{:S(2)}, u32[]{:S(2)}) collective-permute-start(bf16[256,512]{1,0:T(8,128)(2,1)S(1)} %convolution_convert_fusion), channel_id=1, source_target_pairs={{0,128},{128,256},{256,384},{384,512},{512,640},{640,0},{1,129},{1... | collective-permute-start | bytes 786440 | tf_op jit(solution)/shard_map/ppermute | solution.py:19
  272.6 11.7 %collective-permute-done.7 = bf16[256,512]{1,0:T(8,128)(2,1)S(1)} collective-permute-done((bf16[256,512]{1,0:T(8,128)(2,1)S(1)}, bf16[256,512]{1,0:T(8,128)(2,1)S(1)}, u32[]{:S(2)}, u32[]{:S(2)}) %collective-permute-start.7) | collective-permute-done | bytes 262176 | tf_op jit(solution)/shard_map/ppermute | solution.py:19
  (53 shorter events, 16.0 us)
Async XLA Ops:
  6.5 190.1 %copy-start = (bf16[1,4096,256]{2,1,0:T(8,128)(2,1)S(1)}, bf16[1,4096,256]{2,1,0:T(8,128)(2,1)}, u32[]{:S(2)}) copy-start(bf16[1,4096,256]{2,1,0:T(8,128)(2,1)} %param.12) | copy-start | bytes 6291460
  6.5 70.0 %all-gather.5.cloned.1.call-start = ((), (), s32[]{:S(2)}) async-start(), calls=%async_computation.1 | async-start | bytes 1824768 | tf_op jit(solution)/shard_map/all_gather | solution.py:61
  35.0 162.6 %all-gather.7.cloned.1.call-start = ((), (), s32[]{:S(2)}) async-start(), calls=%async_computation.2 | async-start | bytes 4915200 | tf_op jit(solution)/shard_map/all_gather | solution.py:70
  76.6 2.8 copy-start.3
  76.6 3.2 %copy-start.5 = (bf16[1,4096,256]{2,1,0:T(8,128)(2,1)S(1)}, bf16[1,4096,256]{2,1,0:T(8,128)(2,1)}, u32[]{:S(2)}) copy-start(bf16[1,4096,256]{2,1,0:T(8,128)(2,1)} %param.13) | copy-start | bytes 6291460
  76.6 3.8 %slice-start = ((bf16[192,4224]{1,0:T(8,128)(2,1)}), bf16[192,128]{1,0:T(8,128)(2,1)S(1)}, s32[]{:S(2)}) async-start(bf16[192,4224]{1,0:T(8,128)(2,1)} %all-gather.5.cloned.1.call-done), calls=%async_computation.4 | async-start | bytes 98304 | tf_op jit(solution)/shard_map/slice | solution.py:68
  79.8 20.5 %copy-start.2 = (bf16[1,256,512]{2,1,0:T(8,128)(2,1)S(1)}, bf16[1,256,512]{2,1,0:T(8,128)(2,1)}, u32[]{:S(2)}) copy-start(bf16[1,256,512]{2,1,0:T(8,128)(2,1)} %param.10) | copy-start | bytes 786436
  100.4 27.3 %copy-start.4 = (bf16[1,4096]{1,0:T(2,128)(2,1)S(1)}, bf16[1,4096]{1,0:T(2,128)(2,1)}, u32[]{:S(2)}) copy-start(bf16[1,4096]{1,0:T(2,128)(2,1)} %param.11) | copy-start | bytes 24580
  100.4 8.3 %collective-permute-start.3 = (bf16[256,512]{0,1:T(8,128)(2,1)S(1)}, bf16[256,512]{0,1:T(8,128)(2,1)S(1)}, u32[]{:S(2)}, u32[]{:S(2)}) collective-permute-start(bf16[256,512]{0,1:T(8,128)(2,1)S(1)} %bitcast.70), channel_id=1, source_target_pairs={{0,1},{1,2},{2,3},{3,4},{4,5},{5,6},{6,7},{7,0},{8,9},{9,10},{10,1... | collective-permute-start | bytes 786440 | tf_op jit(solution)/shard_map/ppermute | solution.py:19
  102.5 8.2 %collective-permute-start = (bf16[256,512]{0,1:T(8,128)(2,1)S(1)}, bf16[256,512]{0,1:T(8,128)(2,1)S(1)}, u32[]{:S(2)}, u32[]{:S(2)}) collective-permute-start(bf16[256,512]{0,1:T(8,128)(2,1)S(1)} %bitcast.71), channel_id=1, source_target_pairs={{0,7},{1,0},{2,1},{3,2},{4,3},{5,4},{6,5},{7,6},{8,15},{9,8},{10,9... | collective-permute-start | bytes 786440 | tf_op jit(solution)/shard_map/ppermute | solution.py:19
  108.8 15.7 %collective-permute-start.4 = (bf16[256,512]{0,1:T(8,128)(2,1)S(1)}, bf16[256,512]{0,1:T(8,128)(2,1)S(1)}, u32[]{:S(2)}, u32[]{:S(2)}) collective-permute-start(bf16[256,512]{0,1:T(8,128)(2,1)S(1)} %collective-permute-done.3), channel_id=1, source_target_pairs={{0,1},{1,2},{2,3},{3,4},{4,5},{5,6},{6,7},{7,0},{8,9},{9,10},{10,1... | collective-permute-start | bytes 786440 | tf_op jit(solution)/shard_map/ppermute | solution.py:19
  110.7 17.1 %collective-permute-start.1 = (bf16[256,512]{0,1:T(8,128)(2,1)S(1)}, bf16[256,512]{0,1:T(8,128)(2,1)S(1)}, u32[]{:S(2)}, u32[]{:S(2)}) collective-permute-start(bf16[256,512]{0,1:T(8,128)(2,1)S(1)} %collective-permute-done), channel_id=1, source_target_pairs={{0,7},{1,0},{2,1},{3,2},{4,3},{5,4},{6,5},{7,6},{8,15},{9,8},{10,9... | collective-permute-start | bytes 786440 | tf_op jit(solution)/shard_map/ppermute | solution.py:19
  119.3 95.3 %all-to-all-start = ((bf16[256,8,512]{0,2,1:T(8,128)(2,1)}), bf16[256,8,512]{0,2,1:T(8,128)(2,1)}, u32[]{:S(2)}, u32[]{:S(2)}) async-start(bf16[256,8,512]{0,2,1:T(8,128)(2,1)} %bitcast.68), calls=%async_computation | async-start | bytes 4194304 | tf_op jit(solution)/shard_map/all_to_all | solution.py:86
  123.7 133.2 %all-gather.9.cloned.1.call-start = ((), (), s32[]{:S(2)}) async-start(), calls=%async_computation.3 | async-start | bytes 1179648 | tf_op jit(solution)/shard_map/all_gather | solution.py:89
  124.5 48.9 %collective-permute-start.5 = (bf16[256,512]{0,1:T(8,128)(2,1)S(1)}, bf16[256,512]{0,1:T(8,128)(2,1)}, u32[]{:S(2)}, u32[]{:S(2)}) collective-permute-start(bf16[256,512]{0,1:T(8,128)(2,1)S(1)} %collective-permute-done.4), channel_id=1, source_target_pairs={{0,1},{1,2},{2,3},{3,4},{4,5},{5,6},{6,7},{7,0},{8,9},{9,10},{10,1... | collective-permute-start | bytes 786440 | tf_op jit(solution)/shard_map/ppermute | solution.py:19
  127.8 48.2 %collective-permute-start.2 = (bf16[256,512]{0,1:T(8,128)(2,1)S(1)}, bf16[256,512]{0,1:T(8,128)(2,1)S(1)}, u32[]{:S(2)}, u32[]{:S(2)}) collective-permute-start(bf16[256,512]{0,1:T(8,128)(2,1)S(1)} %collective-permute-done.1), channel_id=1, source_target_pairs={{0,7},{1,0},{2,1},{3,2},{4,3},{5,4},{6,5},{7,6},{8,15},{9,8},{10,9... | collective-permute-start | bytes 786440 | tf_op jit(solution)/shard_map/ppermute | solution.py:19
  173.4 8.5 %collective-permute-start.6 = (bf16[256,512]{0,1:T(8,128)(2,1)}, bf16[256,512]{0,1:T(8,128)(2,1)S(1)}, u32[]{:S(2)}, u32[]{:S(2)}) collective-permute-start(bf16[256,512]{0,1:T(8,128)(2,1)} %collective-permute-done.5), channel_id=1, source_target_pairs={{0,1},{1,2},{2,3},{3,4},{4,5},{5,6},{6,7},{7,0},{8,9},{9,10},{10,1... | collective-permute-start | bytes 786440 | tf_op jit(solution)/shard_map/ppermute | solution.py:19
  208.3 3.6 %copy-start.1 = (bf16[3072,256]{0,1:T(8,128)(2,1)S(1)}, bf16[3072,256]{0,1:T(8,128)(2,1)}, u32[]{:S(2)}) copy-start(bf16[3072,256]{0,1:T(8,128)(2,1)} %copy.27) | copy-start | bytes 4718596
  259.5 24.7 %collective-permute-start.7 = (bf16[256,512]{1,0:T(8,128)(2,1)S(1)}, bf16[256,512]{1,0:T(8,128)(2,1)S(1)}, u32[]{:S(2)}, u32[]{:S(2)}) collective-permute-start(bf16[256,512]{1,0:T(8,128)(2,1)S(1)} %convolution_convert_fusion), channel_id=1, source_target_pairs={{0,128},{128,256},{256,384},{384,512},{512,640},{640,0},{1,129},{1... | collective-permute-start | bytes 786440 | tf_op jit(solution)/shard_map/ppermute | solution.py:19
Sparse Core Ops, SparseCore 0:
  35.2 41.3 all-gather.4
  100.4 55.7 all-gather.6
  214.8 42.0 all-gather.8

commit v4 on v1

--- a/solution.py
+++ b/solution.py
@@ -29,8 +29,7 @@
         if step < length - step:
             right = shifted(right, axis, -1)
             pieces[step] = right
-    ordered = jnp.stack([pieces[r] for r in range(length)])
-    return jnp.roll(ordered, lax.axis_index(axis), axis=0)
+    return jnp.concatenate([pieces[r] for r in range(length)], axis=0)
 
 
 def attend_terms(query, key_rows, value_rows, key_flags):
@@ -57,7 +56,7 @@
     flags = flags.at[:, 0].set(keep.astype(jnp.bfloat16))
     packed = jnp.concatenate([memory, flags], axis=1)
     packed = lax.all_gather(packed, "core", axis=0, tiled=True)
-    packed = lax.all_gather(packed, "zh", axis=0, tiled=True)
+    packed = ring_gather(packed, "zh")
     packed = lax.all_gather(packed, HEAD, axis=0, tiled=True)
     encoder_rows = packed[:, :model]
     key_rows = jnp.dot(encoder_rows, w_key[0], preferred_element_type=jnp.float32).astype(jnp.bfloat16)
@@ -67,11 +66,10 @@
     width = key_rows.shape[1]
     kv = jnp.concatenate([key_rows, value_rows, packed[:, model:]], axis=1)
     kv = lax.all_gather(kv, "zl", axis=0, tiled=True)
-    kv = lax.all_gather(kv, "x", axis=0, tiled=True)
+    kv = ring_gather(kv, "x")
 
     local = hidden[0]
-    gathered = ring_gather(local, HEAD)
-    features = jnp.transpose(gathered, (1, 0, 2)).reshape(local.shape[0], -1)
+    features = lax.all_gather(local, HEAD, axis=1, tiled=True)
     widened = features.astype(jnp.float32)
     inverse = lax.rsqrt(jnp.mean(widened * widened, axis=1, keepdims=True) + norm_eps)
     normed = (widened * inverse * gain[0].astype(jnp.float32)[None, :]).astype(jnp.bfloat16)

time: 256 us -> 239 us (0.934)
  blocking collectives: 45.5 us -> 31.2 us
  waiting for transfers between devices: 117 us -> 130 us
  local copies, waits for them, and re-layouts: 24 us -> 13.6 us
  starting transfers between devices: 34.5 us -> 30.4 us
    ppermute x8 -> x6, waiting for transfers between devices: 23.6 us -> 40.6 us  [shifted(): lax.ppermute(x, axis, [(i, (i + by) % length) for i in range(length)])]
    all_gather x1 -> x0, blocking collectives: 13.6 us -> none  [shards(): packed = lax.all_gather(packed, 'zh', axis=0, tiled=True)]
    unnamed x33 -> x20, local copies, waits for them, and re-layouts: 14.2 us -> 4.99 us
    ppermute x8 -> x6, starting transfers between devices: 34.4 us -> 30.3 us  [shifted(): lax.ppermute(x, axis, [(i, (i + by) % length) for i in range(length)])]
    all_gather x1, waiting for transfers between devices: 3.71 us -> 0.01 us  [shards(): features = lax.all_gather(local, HEAD, axis=1, tiled=True)]
    reduce_scatter x1, waiting for transfers between devices: 48.3 us -> 44.6 us  [shards(): lax.psum_scatter(partial_terms.astype(jnp.bfloat16), HEAD, scatter_dimens...]
    all_gather x1, waiting for transfers between devices: 41.5 us -> 44.1 us  [shards(): packed = lax.all_gather(packed, HEAD, axis=0, tiled=True)]
  transfers between devices with their start and end apart: 11 -> 9, of which waited for: 8 -> 6; matrix products, arithmetic and copies ran while one was open for 7% -> 5% of each run, Pallas kernels for 0% -> 0%
where the time goes in v4:
time: 239 us
  waiting for transfers between devices  130 us (54%)
  blocking collectives  31.2 us (13%)
  starting transfers between devices  30.4 us (13%)
  matrix products  14 us (6%)
  local copies, waits for them, and re-layouts  13.6 us (6%)
  between operations  13.3 us (6%)
  other arithmetic  6.18 us (3%)
    reduce_scatter x1, waiting for transfers between devices, shards(): lax.psum_scatter(partial_terms.astype(jnp.bfloat16), HEAD, scatter_dimens...  44.6 us
    all_gather x1, waiting for transfers between devices, shards(): packed = lax.all_gather(packed, HEAD, axis=0, tiled=True)  44.1 us
    ppermute x6, waiting for transfers between devices, shifted(): lax.ppermute(x, axis, [(i, (i + by) % length) for i in range(length)])  40.6 us
    ppermute x6, starting transfers between devices, shifted(): lax.ppermute(x, axis, [(i, (i + by) % length) for i in range(length)])  30.3 us
    all_gather x1, blocking collectives, shards(): kv = lax.all_gather(kv, 'zl', axis=0, tiled=True)  19.3 us
    all_gather x1, blocking collectives, shards(): packed = lax.all_gather(packed, 'core', axis=0, tiled=True)  12 us
    unnamed x20, local copies, waits for them, and re-layouts  4.99 us
  transfers between devices with their start and end apart: 9, of which 6 were waited for; matrix products, arithmetic and copies ran while one was open for 5% of the time, Pallas kernels for 0%

profile of v4, /device:TPU:1, one launch (start us, length us, event | category | flops | bytes accessed | tf_op | source)
XLA Modules:
  0.0 238.7 jit_solution(523924489770743203)
XLA Ops:
  7.2 1.3 fusion.48
  8.6 0.8 fusion.47
  9.4 12.0 %all-gather.1 = bf16[2,4,4224]{2,1,0:T(4,128)(2,1)S(1)} all-gather(bf16[1,4,4224]{2,1,0:T(4,128)(2,1)S(1)} %fusion.47), channel_id=1, replica_groups=mesh['zh'=3,'core'=2,'x'=4,'zl'=4,'y'=8] {'core'}, dimensions={0}, use_global_device_ids=true | all-gather | bytes 101376 | tf_op jit(solution)/shard_map/all_gather | solution.py:58
  21.4 1.9 collective-permute-start.1
  23.3 7.3 %collective-permute-start = (bf16[8,4224]{1,0:T(8,128)(2,1)S(1)}, bf16[8,4224]{1,0:T(8,128)(2,1)S(1)}, u32[]{:S(2)}, u32[]{:S(2)}) collective-permute-start(bf16[8,4224]{1,0:T(8,128)(2,1)S(1)} %reshape.68), channel_id=1, source_target_pairs={{0,512},{256,0},{512,256},{1,513},{257,1},{513,257},{2,514},{258,2... | collective-permute-start | bytes 202760 | tf_op jit(solution)/shard_map/ppermute | solution.py:19
  30.6 2.6 %collective-permute-done = bf16[8,4224]{1,0:T(8,128)(2,1)S(1)} collective-permute-done((bf16[8,4224]{1,0:T(8,128)(2,1)S(1)}, bf16[8,4224]{1,0:T(8,128)(2,1)S(1)}, u32[]{:S(2)}, u32[]{:S(2)}) %collective-permute-start) | collective-permute-done | bytes 67616 | tf_op jit(solution)/shard_map/ppermute | solution.py:19
  33.2 0.7 pad_maximum_fusion.1
  34.0 0.7 all-gather.7.cloned.1.call-update
  34.7 44.1 %all-gather.5.cloned.1.call-done = bf16[192,4224]{1,0:T(8,128)(2,1)} async-done(((bf16[24,4224]{1,0:T(8,128)(2,1)}), bf16[192,4224]{1,0:T(8,128)(2,1)}) %all-gather.5.cloned.1.call-update) | async-done | bytes 1622032 | tf_op jit(solution)/shard_map/all_gather | solution.py:60
  78.8 2.8 %fusion.34 = bf16[192,256]{1,0:T(8,128)(2,1)S(1)} fusion(bf16[1,4096,256]{2,1,0:T(8,128)(2,1)} %param.14, bf16[192,4224]{1,0:T(8,128)(2,1)} %all-gather.5.cloned.1.call-done), kind=kOutput, calls=%fused_computation.27 | convolution fusion | flops 402702336 | bytes 3768320 | tf_op jit(solution)/shard_map/dot_general | solution.py:63
  82.8 19.3 %all_gather.14 = bf16[768,640]{1,0:T(8,128)(2,1)S(1)} all-gather(bf16[192,640]{1,0:T(8,128)(2,1)S(1)} %pad_maximum_fusion), channel_id=1, replica_groups=mesh['zh'=3,'core'=2,'x'=4,'zl'=4,'y'=8] {'zl'}, dimensions={0}, use_global_device_ids=true | all-gather | bytes 1228800 | tf_op jit(solution)/shard_map/all_gather | solution.py:68
  102.1 3.1 %collective-permute-start.3 = (bf16[768,640]{1,0:T(8,128)(2,1)S(1)}, bf16[768,640]{1,0:T(8,128)(2,1)}, u32[]{:S(2)}, u32[]{:S(2)}) collective-permute-start(bf16[768,640]{1,0:T(8,128)(2,1)S(1)} %all_gather.14), channel_id=1, source_target_pairs={{0,32},{32,64},{64,96},{96,0},{1,33},{33,65},{65,97},{97,1},{2,34}... | collective-permute-start | bytes 2949128 | tf_op jit(solution)/shard_map/ppermute | solution.py:19
  105.2 3.4 %collective-permute-start.2 = (bf16[768,640]{1,0:T(8,128)(2,1)S(1)}, bf16[768,640]{1,0:T(8,128)(2,1)}, u32[]{:S(2)}, u32[]{:S(2)}) collective-permute-start(bf16[768,640]{1,0:T(8,128)(2,1)S(1)} %all_gather.14), channel_id=1, source_target_pairs={{0,96},{32,0},{64,32},{96,64},{1,97},{33,1},{65,33},{97,65},{2,98}... | collective-permute-start | bytes 2949128 | tf_op jit(solution)/shard_map/ppermute | solution.py:19
  108.6 14.8 %collective-permute-done.3 = bf16[768,640]{1,0:T(8,128)(2,1)} collective-permute-done((bf16[768,640]{1,0:T(8,128)(2,1)S(1)}, bf16[768,640]{1,0:T(8,128)(2,1)}, u32[]{:S(2)}, u32[]{:S(2)}) %collective-permute-start.3) | collective-permute-done | bytes 983072 | tf_op jit(solution)/shard_map/ppermute | solution.py:19
  123.4 1.9 collective-permute-start.4
  125.3 1.0 constant_dynamic-update-slice_fusion.3
  126.4 2.2 fusion.5
  128.6 2.9 %fusion.24 = bf16[256,256]{0,1:T(8,128)(2,1)S(1)} fusion(bf16[1,4096,256]{2,1,0:T(8,128)(2,1)} %param.12, bf16[1,256,4096]{2,1,0:T(8,128)(2,1)S(1)} %copy-done.3, f32[4096]{0:T(1024)S(1)} %bitcast.53, f32[256]{0:T(256)S(1)} %add_rsqrt_fusion), kind=kOutput, calls=%fused_computation.25 | convolution fusion | flops 541130752 | bytes 4342784 | tf_op jit(solution)/shard_map/dot_general | solution.py:76
  131.6 1.4 constant_dynamic-update-slice_fusion.2
  133.0 11.2 %collective-permute-done.4 = bf16[768,640]{1,0:T(8,128)(2,1)} collective-permute-done((bf16[768,640]{1,0:T(8,128)(2,1)}, bf16[768,640]{1,0:T(8,128)(2,1)}, u32[]{:S(2)}, u32[]{:S(2)}) %collective-permute-start.4) | collective-permute-done | bytes 983072 | tf_op jit(solution)/shard_map/ppermute | solution.py:19
  144.1 1.4 constant_dynamic-update-slice_fusion.1
  145.5 1.4 constant_dynamic-update-slice_fusion
  147.3 1.8 fusion.49
  149.2 2.6 %copy.17 = bf16[3072,256]{0,1:T(8,128)(2,1)} copy(bf16[3072,256]{1,0:T(8,128)(2,1)} %get-tuple-element.17) | data formatting | bytes 3145728 | tf_op jit(solution)/shard_map/slice | solution.py:79
  151.8 2.6 %copy.16 = bf16[3072,256]{0,1:T(8,128)(2,1)} copy(bf16[3072,256]{1,0:T(8,128)(2,1)} %get-tuple-element.18) | data formatting | bytes 3145728 | tf_op jit(solution)/shard_map/slice | solution.py:79
  154.3 3.6 %fusion = (f32[4,256]{1,0:T(4,128)S(1)}, f32[4,256,3072]{2,1,0:T(8,128)S(1)}) fusion(f32[3072]{0:T(1024)S(1)} %multiply_reduce_fusion, bf16[256,4,64]{0,2,1:T(8,128)(2,1)S(1)} %bitcast.51, bf16[3072,4,64]{0,2,1:T(8,128)(2,1)} %bitcast.48), kind=kOutput, calls=%fused_computation.1 | convolution fusion | flops 408943616 | bytes 14303232 | tf_op jit(solution)/shard_map/qhd,khd->hqk/dot_general | solution.py:40
  158.0 2.0 fusion.42
  160.0 2.1 convolution_convert_fusion
  162.1 44.6 %reduce-scatter.2.cloned.1.call-done = bf16[256,512]{1,0:T(8,128)(2,1)} async-done(((bf16[256,4096]{1,0:T(8,128)(2,1)}), bf16[256,512]{1,0:T(8,128)(2,1)}) %reduce-scatter.2.cloned.1.call-update) | async-done | bytes 262160 | tf_op jit(solution)/shard_map/reduce_scatter | solution.py:84
  206.7 12.7 %collective-permute-start.5 = (bf16[256,512]{1,0:T(8,128)(2,1)}, bf16[256,512]{1,0:T(8,128)(2,1)S(1)}, u32[]{:S(2)}, u32[]{:S(2)}) collective-permute-start(bf16[256,512]{1,0:T(8,128)(2,1)} %reduce-scatter.2.cloned.1.call-done), channel_id=1, source_target_pairs={{0,128},{128,256},{256,384},{384,512},{512,640},{640,0},{1,129},{1... | collective-permute-start | bytes 786440 | tf_op jit(solution)/shard_map/ppermute | solution.py:19
  219.5 12.0 %collective-permute-done.5 = bf16[256,512]{1,0:T(8,128)(2,1)S(1)} collective-permute-done((bf16[256,512]{1,0:T(8,128)(2,1)}, bf16[256,512]{1,0:T(8,128)(2,1)S(1)}, u32[]{:S(2)}, u32[]{:S(2)}) %collective-permute-start.5) | collective-permute-done | bytes 262176 | tf_op jit(solution)/shard_map/ppermute | solution.py:19
  231.5 0.7 copy.23
  (32 shorter events, 2.6 us)
Async XLA Ops:
  6.5 153.5 %copy-start = (bf16[1,256,4096]{2,1,0:T(8,128)(2,1)S(1)}, bf16[1,256,4096]{2,1,0:T(8,128)(2,1)}, u32[]{:S(2)}) copy-start(bf16[1,256,4096]{2,1,0:T(8,128)(2,1)} %param.15) | copy-start | bytes 6291460
  6.5 72.2 %all-gather.5.cloned.1.call-start = ((), (), s32[]{:S(2)}) async-start(), calls=%async_computation.1 | async-start | bytes 1824768 | tf_op jit(solution)/shard_map/all_gather | solution.py:60
  21.4 9.2 %collective-permute-start.1 = (bf16[8,4224]{1,0:T(8,128)(2,1)S(1)}, bf16[8,4224]{1,0:T(8,128)(2,1)S(1)}, u32[]{:S(2)}, u32[]{:S(2)}) collective-permute-start(bf16[8,4224]{1,0:T(8,128)(2,1)S(1)} %reshape.68), channel_id=1, source_target_pairs={{0,256},{256,512},{512,0},{1,257},{257,513},{513,1},{2,258},{258,5... | collective-permute-start | bytes 202760 | tf_op jit(solution)/shard_map/ppermute | solution.py:19
  23.3 9.9 %collective-permute-start = (bf16[8,4224]{1,0:T(8,128)(2,1)S(1)}, bf16[8,4224]{1,0:T(8,128)(2,1)S(1)}, u32[]{:S(2)}, u32[]{:S(2)}) collective-permute-start(bf16[8,4224]{1,0:T(8,128)(2,1)S(1)} %reshape.68), channel_id=1, source_target_pairs={{0,512},{256,0},{512,256},{1,513},{257,1},{513,257},{2,514},{258,2... | collective-permute-start | bytes 202760 | tf_op jit(solution)/shard_map/ppermute | solution.py:19
  33.9 92.4 %all-gather.7.cloned.1.call-start = ((), (), s32[]{:S(2)}) async-start(), calls=%async_computation.3 | async-start | bytes 2359296 | tf_op jit(solution)/shard_map/all_gather | solution.py:72
  34.7 172.1 %reduce-scatter.2.cloned.1.call-start = ((), (), s32[]{:S(2)}) async-start(), calls=%async_computation.2 | async-start | bytes 2359296 | tf_op jit(solution)/shard_map/reduce_scatter | solution.py:84
  78.8 2.8 %copy-start.4 = (bf16[192,4224]{1,0:T(8,128)(2,1)S(1)}, bf16[192,4224]{1,0:T(8,128)(2,1)}, u32[]{:S(2)}) copy-start(bf16[192,4224]{1,0:T(8,128)(2,1)} %all-gather.5.cloned.1.call-done) | copy-start | bytes 4866052
  78.8 3.2 %copy-start.6 = (bf16[1,4096,256]{2,1,0:T(8,128)(2,1)S(1)}, bf16[1,4096,256]{2,1,0:T(8,128)(2,1)}, u32[]{:S(2)}) copy-start(bf16[1,4096,256]{2,1,0:T(8,128)(2,1)} %param.13) | copy-start | bytes 6291460
  82.0 0.8 slice-start
  82.0 26.6 %copy-start.5 = (bf16[1,4096]{1,0:T(2,128)(2,1)S(1)}, bf16[1,4096]{1,0:T(2,128)(2,1)}, u32[]{:S(2)}) copy-start(bf16[1,4096]{1,0:T(2,128)(2,1)} %param.11) | copy-start | bytes 24580
  102.1 21.4 %collective-permute-start.3 = (bf16[768,640]{1,0:T(8,128)(2,1)S(1)}, bf16[768,640]{1,0:T(8,128)(2,1)}, u32[]{:S(2)}, u32[]{:S(2)}) collective-permute-start(bf16[768,640]{1,0:T(8,128)(2,1)S(1)} %all_gather.14), channel_id=1, source_target_pairs={{0,32},{32,64},{64,96},{96,0},{1,33},{33,65},{65,97},{97,1},{2,34}... | collective-permute-start | bytes 2949128 | tf_op jit(solution)/shard_map/ppermute | solution.py:19
  105.2 26.4 %collective-permute-start.2 = (bf16[768,640]{1,0:T(8,128)(2,1)S(1)}, bf16[768,640]{1,0:T(8,128)(2,1)}, u32[]{:S(2)}, u32[]{:S(2)}) collective-permute-start(bf16[768,640]{1,0:T(8,128)(2,1)S(1)} %all_gather.14), channel_id=1, source_target_pairs={{0,96},{32,0},{64,32},{96,64},{1,97},{33,1},{65,33},{97,65},{2,98}... | collective-permute-start | bytes 2949128 | tf_op jit(solution)/shard_map/ppermute | solution.py:19
  123.4 20.7 %collective-permute-start.4 = (bf16[768,640]{1,0:T(8,128)(2,1)}, bf16[768,640]{1,0:T(8,128)(2,1)}, u32[]{:S(2)}, u32[]{:S(2)}) collective-permute-start(bf16[768,640]{1,0:T(8,128)(2,1)} %collective-permute-done.3), channel_id=1, source_target_pairs={{0,32},{32,64},{64,96},{96,0},{1,33},{33,65},{65,97},{97,1},{2,34}... | collective-permute-start | bytes 2949128 | tf_op jit(solution)/shard_map/ppermute | solution.py:19
  126.4 2.2 copy-start.3
  128.6 3.0 %copy-start.2 = (bf16[3072,640]{1,0:T(8,128)(2,1)S(1)}, bf16[3072,640]{1,0:T(8,128)(2,1)}, u32[]{:S(2)}) copy-start(bf16[3072,640]{1,0:T(8,128)(2,1)} %constant_dynamic-update-slice_fusion.3) | copy-start | bytes 11796484
  154.3 3.6 %copy-start.1 = (bf16[3072,256]{0,1:T(8,128)(2,1)S(1)}, bf16[3072,256]{0,1:T(8,128)(2,1)}, u32[]{:S(2)}) copy-start(bf16[3072,256]{0,1:T(8,128)(2,1)} %copy.16) | copy-start | bytes 4718596
  206.7 24.8 %collective-permute-start.5 = (bf16[256,512]{1,0:T(8,128)(2,1)}, bf16[256,512]{1,0:T(8,128)(2,1)S(1)}, u32[]{:S(2)}, u32[]{:S(2)}) collective-permute-start(bf16[256,512]{1,0:T(8,128)(2,1)} %reduce-scatter.2.cloned.1.call-done), channel_id=1, source_target_pairs={{0,128},{128,256},{256,384},{384,512},{512,640},{640,0},{1,129},{1... | collective-permute-start | bytes 786440 | tf_op jit(solution)/shard_map/ppermute | solution.py:19
Sparse Core Ops, SparseCore 0:
  34.0 44.6 all-gather.4
  81.1 44.9 all-gather.6
  162.2 44.4 reduce-scatter.1

commit v5 on v4

--- a/solution.py
+++ b/solution.py
@@ -24,6 +24,12 @@
     pieces = {0: x}
     left, right = x, x
     for step in range(1, length // 2 + 1):
+        if step == length - step:
+            half = x.shape[0] // 2
+            pieces[step] = jnp.concatenate(
+                [shifted(left[:half], axis, 1), shifted(right[half:], axis, -1)], axis=0
+            )
+            break
         left = shifted(left, axis, 1)
         pieces[-step % length] = left
         if step < length - step:
@@ -56,7 +62,7 @@
     flags = flags.at[:, 0].set(keep.astype(jnp.bfloat16))
     packed = jnp.concatenate([memory, flags], axis=1)
     packed = lax.all_gather(packed, "core", axis=0, tiled=True)
-    packed = ring_gather(packed, "zh")
+    packed = lax.all_gather(packed, "zh", axis=0, tiled=True)
     packed = lax.all_gather(packed, HEAD, axis=0, tiled=True)
     encoder_rows = packed[:, :model]
     key_rows = jnp.dot(encoder_rows, w_key[0], preferred_element_type=jnp.float32).astype(jnp.bfloat16)
@@ -64,9 +70,16 @@
         jnp.bfloat16
     )
     width = key_rows.shape[1]
-    kv = jnp.concatenate([key_rows, value_rows, packed[:, model:]], axis=1)
+    rows = key_rows.shape[0]
+    flag_rows = jnp.zeros((8, 2 * width), jnp.bfloat16)
+    flag_rows = flag_rows.at[0, :rows].set(packed[:, model])
+    kv = jnp.concatenate([key_rows, value_rows], axis=1)
+    kv = jnp.concatenate([kv, flag_rows], axis=0)
     kv = lax.all_gather(kv, "zl", axis=0, tiled=True)
     kv = ring_gather(kv, "x")
+    kv = kv.reshape(-1, rows + 8, 2 * width)
+    key_flags = kv[:, rows, :rows].reshape(-1)
+    kv = kv[:, :rows].reshape(-1, 2 * width)
 
     local = hidden[0]
     features = lax.all_gather(local, HEAD, axis=1, tiled=True)
@@ -76,7 +89,7 @@
     query = jnp.dot(normed, w_query[0], preferred_element_type=jnp.float32).astype(jnp.bfloat16)
 
     more_num, more_den = attend_terms(
-        query, kv[:, :width], kv[:, width : 2 * width], kv[:, 2 * width]
+        query, kv[:, :width], kv[:, width:], key_flags
     )
     spread = jnp.repeat(more_den, HEAD_DIM, axis=1)
     attended = (more_num / spread).astype(jnp.bfloat16)

time: 239 us -> 235 us (0.983)
  waiting for transfers between devices: 130 us -> 111 us
  blocking collectives: 31.2 us -> 42.2 us
  local copies, waits for them, and re-layouts: 13.6 us -> 22 us
  starting transfers between devices: 30.4 us -> 25.9 us
    ppermute x6 -> x5, waiting for transfers between devices: 40.6 us -> 20.9 us  [shifted(): lax.ppermute(x, axis, [(i, (i + by) % length) for i in range(length)])]
    all_gather x0 -> x1, blocking collectives: none -> 13.6 us  [shards(): packed = lax.all_gather(packed, 'zh', axis=0, tiled=True)]
    unnamed x20 -> x21, local copies, waits for them, and re-layouts: 4.99 us -> 10.9 us
    ppermute x6 -> x5, starting transfers between devices: 30.3 us -> 25.8 us  [shifted(): lax.ppermute(x, axis, [(i, (i + by) % length) for i in range(length)])]
    slice x3 -> x4, local copies, waits for them, and re-layouts: 2.81 us -> 6.34 us  [the longest x1 3.85 us: shards(): kv = kv[:, :rows].reshape(-1, 2 * width)]
    reduce_scatter x1, waiting for transfers between devices: 44.6 us -> 48.1 us  [shards(): lax.psum_scatter(partial_terms.astype(jnp.bfloat16), HEAD, scatter_dimens...]
    all_gather x1, waiting for transfers between devices: 44.1 us -> 40.7 us  [shards(): packed = lax.all_gather(packed, HEAD, axis=0, tiled=True)]
    all_gather x1, blocking collectives: 19.3 us -> 16.5 us  [shards(): kv = lax.all_gather(kv, 'zl', axis=0, tiled=True)]
  transfers between devices with their start and end apart: 9 -> 8, of which waited for: 6 -> 5; matrix products, arithmetic and copies ran while one was open for 5% -> 6% of each run, Pallas kernels for 0% -> 0%
where the time goes in v5:
time: 235 us; the launch traced here: 234 us
  waiting for transfers between devices  111 us (47%)
  blocking collectives  42.2 us (18%)
  starting transfers between devices  25.9 us (11%)
  local copies, waits for them, and re-layouts  22 us (9%)
  matrix products  13.9 us (6%)
  between operations  13.3 us (6%)
  other arithmetic  5.89 us (3%)
    reduce_scatter x1, waiting for transfers between devices, shards(): lax.psum_scatter(partial_terms.astype(jnp.bfloat16), HEAD, scatter_dimens...  48.1 us
    all_gather x1, waiting for transfers between devices, shards(): packed = lax.all_gather(packed, HEAD, axis=0, tiled=True)  40.7 us
    ppermute x5, starting transfers between devices, shifted(): lax.ppermute(x, axis, [(i, (i + by) % length) for i in range(length)])  25.8 us
    ppermute x5, waiting for transfers between devices, shifted(): lax.ppermute(x, axis, [(i, (i + by) % length) for i in range(length)])  20.9 us
    all_gather x1, blocking collectives, shards(): kv = lax.all_gather(kv, 'zl', axis=0, tiled=True)  16.5 us
    all_gather x1, blocking collectives, shards(): packed = lax.all_gather(packed, 'zh', axis=0, tiled=True)  13.6 us
    all_gather x1, blocking collectives, shards(): packed = lax.all_gather(packed, 'core', axis=0, tiled=True)  12 us
    unnamed x21, local copies, waits for them, and re-layouts  10.9 us
  transfers between devices with their start and end apart: 8, of which 5 were waited for; matrix products, arithmetic and copies ran while one was open for 6% of the time, Pallas kernels for 0%

profile of v5, /device:TPU:1, one launch (start us, length us, event | category | flops | bytes accessed | tf_op | source)
XLA Modules:
  0.0 234.3 jit_solution(9894164351194622222)
XLA Ops:
  7.2 1.3 fusion.53
  9.4 12.0 %all-gather.1 = bf16[2,4,4224]{2,1,0:T(4,128)(2,1)S(1)} all-gather(bf16[1,4,4224]{2,1,0:T(4,128)(2,1)S(1)} %fusion.49), channel_id=1, replica_groups=mesh['zh'=3,'core'=2,'x'=4,'zl'=4,'y'=8] {'core'}, dimensions={0}, use_global_device_ids=true | all-gather | bytes 101376 | tf_op jit(solution)/shard_map/all_gather | solution.py:64
  21.4 13.6 %all_gather.16 = bf16[24,4224]{1,0:T(8,128)(2,1)} all-gather(bf16[8,4224]{1,0:T(8,128)(2,1)S(1)} %reshape.107), channel_id=1, replica_groups=mesh['zh'=3,'core'=2,'x'=4,'zl'=4,'y'=8] {'zh'}, dimensions={0}, use_global_device_ids=true | all-gather | bytes 270336 | tf_op jit(solution)/shard_map/all_gather | solution.py:65
  35.8 40.7 %all-gather.5.cloned.1.call-done = bf16[192,4224]{1,0:T(8,128)(2,1)} async-done(((bf16[24,4224]{1,0:T(8,128)(2,1)}), bf16[192,4224]{1,0:T(8,128)(2,1)}) %all-gather.5.cloned.1.call-update) | async-done | bytes 1622032 | tf_op jit(solution)/shard_map/all_gather | solution.py:66
  76.6 0.9 slice_reduce_fusion
  77.5 2.8 %fusion.34 = bf16[192,256]{1,0:T(8,128)(2,1)S(1)} fusion(bf16[1,4096,256]{2,1,0:T(8,128)(2,1)} %param.16, bf16[192,4224]{1,0:T(8,128)(2,1)} %all-gather.5.cloned.1.call-done), kind=kOutput, calls=%fused_computation.26 | convolution fusion | flops 402702336 | bytes 3768320 | tf_op jit(solution)/shard_map/dot_general | solution.py:69
  81.3 16.5 %all_gather.18 = bf16[800,512]{1,0:T(8,128)(2,1)S(1)} all-gather(bf16[200,512]{1,0:T(8,128)(2,1)S(1)} %fusion.46), channel_id=1, replica_groups=mesh['zh'=3,'core'=2,'x'=4,'zl'=4,'y'=8] {'zl'}, dimensions={0}, use_global_device_ids=true | all-gather | bytes 1024000 | tf_op jit(solution)/shard_map/all_gather | solution.py:78
  97.8 3.1 %collective-permute-start.1 = (bf16[800,512]{1,0:T(8,128)(2,1)S(1)}, bf16[800,512]{1,0:T(8,128)(2,1)S(1)}, u32[]{:S(2)}, u32[]{:S(2)}) collective-permute-start(bf16[800,512]{1,0:T(8,128)(2,1)S(1)} %all_gather.18), channel_id=1, source_target_pairs={{0,32},{32,64},{64,96},{96,0},{1,33},{33,65},{65,97},{97,1},{2,34}... | collective-permute-start | bytes 2457608 | tf_op jit(solution)/shard_map/ppermute | solution.py:19
  100.9 3.4 %collective-permute-start = (bf16[800,512]{1,0:T(8,128)(2,1)S(1)}, bf16[800,512]{1,0:T(8,128)(2,1)S(1)}, u32[]{:S(2)}, u32[]{:S(2)}) collective-permute-start(bf16[800,512]{1,0:T(8,128)(2,1)S(1)} %all_gather.18), channel_id=1, source_target_pairs={{0,96},{32,0},{64,32},{96,64},{1,97},{33,1},{65,33},{97,65},{2,98}... | collective-permute-start | bytes 2457608 | tf_op jit(solution)/shard_map/ppermute | solution.py:19
  104.4 1.0 constant_dynamic-update-slice_fusion.4
  105.3 8.9 %collective-permute-done.1 = bf16[800,512]{1,0:T(8,128)(2,1)S(1)} collective-permute-done((bf16[800,512]{1,0:T(8,128)(2,1)S(1)}, bf16[800,512]{1,0:T(8,128)(2,1)S(1)}, u32[]{:S(2)}, u32[]{:S(2)}) %collective-permute-start.1) | collective-permute-done | bytes 819232 | tf_op jit(solution)/shard_map/ppermute | solution.py:19
  114.2 0.8 slice.64
  115.0 2.0 collective-permute-start.2
  117.0 0.8 slice.65
  117.8 4.5 %collective-permute-start.3 = (bf16[400,512]{1,0:T(8,128)(2,1)}, bf16[400,512]{1,0:T(8,128)(2,1)}, u32[]{:S(2)}, u32[]{:S(2)}) collective-permute-start(bf16[400,512]{1,0:T(8,128)(2,1)} %slice.65), channel_id=1, source_target_pairs={{0,96},{32,0},{64,32},{96,64},{1,97},{33,1},{65,33},{97,65},{2,98}... | collective-permute-start | bytes 1228808 | tf_op jit(solution)/shard_map/ppermute | solution.py:19
  122.3 1.0 constant_dynamic-update-slice_fusion.3
  124.0 2.2 fusion.5
  126.2 2.8 %fusion.24 = bf16[256,256]{0,1:T(8,128)(2,1)S(1)} fusion(bf16[1,4096,256]{2,1,0:T(8,128)(2,1)} %param.14, bf16[1,256,4096]{2,1,0:T(8,128)(2,1)S(1)} %copy-done.2, f32[4096]{0:T(1024)S(1)} %bitcast.56, f32[256]{0:T(256)S(1)} %add_rsqrt_fusion), kind=kOutput, calls=%fused_computation.24 | convolution fusion | flops 541130752 | bytes 4342784 | tf_op jit(solution)/shard_map/dot_general | solution.py:89
  129.0 0.8 constant_dynamic-update-slice_fusion.2
  129.8 1.8 constant_dynamic-update-slice_fusion.1
  131.6 1.0 constant_dynamic-update-slice_fusion
  132.6 0.9 fusion.52
  133.5 3.8 %slice.66 = bf16[16,192,512]{2,1,0:T(8,128)(2,1)} slice(bf16[16,200,512]{2,1,0:T(8,128)(2,1)} %bitcast.4), slice={[0:16], [0:192], [0:512]} | slice | bytes 6291456 | tf_op jit(solution)/shard_map/slice | solution.py:82
  137.4 3.7 %fusion.54 = (bf16[3072,256]{1,0:T(8,128)(2,1)}, bf16[3072,256]{1,0:T(8,128)(2,1)}) fusion(bf16[3072,512]{1,0:T(8,128)(2,1)} %bitcast.50), kind=kLoop, calls=%fused_computation.50 | loop fusion | bytes 6291456 | tf_op jit(solution)/shard_map/slice | solution.py:92
  141.1 2.6 %copy.20 = bf16[3072,256]{0,1:T(8,128)(2,1)} copy(bf16[3072,256]{1,0:T(8,128)(2,1)} %get-tuple-element.29) | data formatting | bytes 3145728
  143.7 2.6 %copy.19 = bf16[3072,256]{0,1:T(8,128)(2,1)} copy(bf16[3072,256]{1,0:T(8,128)(2,1)} %get-tuple-element.30) | data formatting | bytes 3145728
  146.3 3.6 %fusion = (f32[4,256]{1,0:T(4,128)S(1)}, f32[4,256,3072]{2,1,0:T(8,128)S(1)}) fusion(f32[3072]{0:T(1024)S(1)} %mul.46, bf16[256,4,64]{0,2,1:T(8,128)(2,1)S(1)} %bitcast.54, bf16[3072,4,64]{0,2,1:T(8,128)(2,1)} %bitcast.51), kind=kOutput, calls=%fused_computation.1 | convolution fusion | flops 408943616 | bytes 14303232 | tf_op jit(solution)/shard_map/qhd,khd->hqk/dot_general | solution.py:46
  149.9 2.0 fusion.42
  152.0 2.1 convolution_convert_fusion
  154.1 48.1 %reduce-scatter.2.cloned.1.call-done = bf16[256,512]{1,0:T(8,128)(2,1)} async-done(((bf16[256,4096]{1,0:T(8,128)(2,1)}), bf16[256,512]{1,0:T(8,128)(2,1)}) %reduce-scatter.2.cloned.1.call-update) | async-done | bytes 262160 | tf_op jit(solution)/shard_map/reduce_scatter | solution.py:97
  202.1 12.9 %collective-permute-start.4 = (bf16[256,512]{1,0:T(8,128)(2,1)}, bf16[256,512]{1,0:T(8,128)(2,1)S(1)}, u32[]{:S(2)}, u32[]{:S(2)}) collective-permute-start(bf16[256,512]{1,0:T(8,128)(2,1)} %reduce-scatter.2.cloned.1.call-done), channel_id=1, source_target_pairs={{0,128},{128,256},{256,384},{384,512},{512,640},{640,0},{1,129},{1... | collective-permute-start | bytes 786440 | tf_op jit(solution)/shard_map/ppermute | solution.py:19
  215.0 12.0 %collective-permute-done.4 = bf16[256,512]{1,0:T(8,128)(2,1)S(1)} collective-permute-done((bf16[256,512]{1,0:T(8,128)(2,1)}, bf16[256,512]{1,0:T(8,128)(2,1)S(1)}, u32[]{:S(2)}, u32[]{:S(2)}) %collective-permute-start.4) | collective-permute-done | bytes 262176 | tf_op jit(solution)/shard_map/ppermute | solution.py:19
  (33 shorter events, 4.9 us)
Async XLA Ops:
  6.5 145.4 %copy-start = (bf16[1,256,4096]{2,1,0:T(8,128)(2,1)S(1)}, bf16[1,256,4096]{2,1,0:T(8,128)(2,1)}, u32[]{:S(2)}) copy-start(bf16[1,256,4096]{2,1,0:T(8,128)(2,1)} %param.17) | copy-start | bytes 6291460
  6.5 70.0 %all-gather.5.cloned.1.call-start = ((), (), s32[]{:S(2)}) async-start(), calls=%async_computation.1 | async-start | bytes 1824768 | tf_op jit(solution)/shard_map/all_gather | solution.py:66
  35.0 89.0 %all-gather.7.cloned.1.call-start = ((), (), s32[]{:S(2)}) async-start(), calls=%async_computation.3 | async-start | bytes 2359296 | tf_op jit(solution)/shard_map/all_gather | solution.py:85
  35.8 166.4 %reduce-scatter.2.cloned.1.call-start = ((), (), s32[]{:S(2)}) async-start(), calls=%async_computation.2 | async-start | bytes 2359296 | tf_op jit(solution)/shard_map/reduce_scatter | solution.py:97
  77.5 2.8 %copy-start.4 = (bf16[192,4224]{1,0:T(8,128)(2,1)S(1)}, bf16[192,4224]{1,0:T(8,128)(2,1)}, u32[]{:S(2)}) copy-start(bf16[192,4224]{1,0:T(8,128)(2,1)} %all-gather.5.cloned.1.call-done) | copy-start | bytes 4866052
  77.5 3.2 %copy-start.5 = (bf16[1,4096,256]{2,1,0:T(8,128)(2,1)S(1)}, bf16[1,4096,256]{2,1,0:T(8,128)(2,1)}, u32[]{:S(2)}) copy-start(bf16[1,4096,256]{2,1,0:T(8,128)(2,1)} %param.15) | copy-start | bytes 6291460
  80.7 23.7 %copy-start.3 = (bf16[1,4096]{1,0:T(2,128)(2,1)S(1)}, bf16[1,4096]{1,0:T(2,128)(2,1)}, u32[]{:S(2)}) copy-start(bf16[1,4096]{1,0:T(2,128)(2,1)} %param.13) | copy-start | bytes 24580
  97.8 16.4 %collective-permute-start.1 = (bf16[800,512]{1,0:T(8,128)(2,1)S(1)}, bf16[800,512]{1,0:T(8,128)(2,1)S(1)}, u32[]{:S(2)}, u32[]{:S(2)}) collective-permute-start(bf16[800,512]{1,0:T(8,128)(2,1)S(1)} %all_gather.18), channel_id=1, source_target_pairs={{0,32},{32,64},{64,96},{96,0},{1,33},{33,65},{65,97},{97,1},{2,34}... | collective-permute-start | bytes 2457608 | tf_op jit(solution)/shard_map/ppermute | solution.py:19
  100.9 16.1 %collective-permute-start = (bf16[800,512]{1,0:T(8,128)(2,1)S(1)}, bf16[800,512]{1,0:T(8,128)(2,1)S(1)}, u32[]{:S(2)}, u32[]{:S(2)}) collective-permute-start(bf16[800,512]{1,0:T(8,128)(2,1)S(1)} %all_gather.18), channel_id=1, source_target_pairs={{0,96},{32,0},{64,32},{96,64},{1,97},{33,1},{65,33},{97,65},{2,98}... | collective-permute-start | bytes 2457608 | tf_op jit(solution)/shard_map/ppermute | solution.py:19
  115.0 14.0 %collective-permute-start.2 = (bf16[400,512]{1,0:T(8,128)(2,1)}, bf16[400,512]{1,0:T(8,128)(2,1)S(1)}, u32[]{:S(2)}, u32[]{:S(2)}) collective-permute-start(bf16[400,512]{1,0:T(8,128)(2,1)} %slice.64), channel_id=1, source_target_pairs={{0,32},{32,64},{64,96},{96,0},{1,33},{33,65},{65,97},{97,1},{2,34}... | collective-permute-start | bytes 1228808 | tf_op jit(solution)/shard_map/ppermute | solution.py:19
  117.8 12.0 %collective-permute-start.3 = (bf16[400,512]{1,0:T(8,128)(2,1)}, bf16[400,512]{1,0:T(8,128)(2,1)}, u32[]{:S(2)}, u32[]{:S(2)}) collective-permute-start(bf16[400,512]{1,0:T(8,128)(2,1)} %slice.65), channel_id=1, source_target_pairs={{0,96},{32,0},{64,32},{96,64},{1,97},{33,1},{65,33},{97,65},{2,98}... | collective-permute-start | bytes 1228808 | tf_op jit(solution)/shard_map/ppermute | solution.py:19
  124.0 2.2 copy-start.2
  146.3 3.6 %copy-start.1 = (bf16[3072,256]{0,1:T(8,128)(2,1)S(1)}, bf16[3072,256]{0,1:T(8,128)(2,1)}, u32[]{:S(2)}) copy-start(bf16[3072,256]{0,1:T(8,128)(2,1)} %copy.19) | copy-start | bytes 4718596
  202.1 24.9 %collective-permute-start.4 = (bf16[256,512]{1,0:T(8,128)(2,1)}, bf16[256,512]{1,0:T(8,128)(2,1)S(1)}, u32[]{:S(2)}, u32[]{:S(2)}) collective-permute-start(bf16[256,512]{1,0:T(8,128)(2,1)} %reduce-scatter.2.cloned.1.call-done), channel_id=1, source_target_pairs={{0,128},{128,256},{256,384},{384,512},{512,640},{640,0},{1,129},{1... | collective-permute-start | bytes 786440 | tf_op jit(solution)/shard_map/ppermute | solution.py:19
Sparse Core Ops, SparseCore 0:
  35.2 41.3 all-gather.4
  78.9 45.0 all-gather.6
  154.2 47.9 reduce-scatter.1

commit v6 on v5

--- a/solution.py
+++ b/solution.py
@@ -38,14 +38,14 @@
     return jnp.concatenate([pieces[r] for r in range(length)], axis=0)
 
 
-def attend_terms(query, key_rows, value_rows, key_flags):
+def attend_terms(query, key_rows, value_rows, key_flags, real_rows):
     head_count = query.shape[1] // HEAD_DIM
     query_heads = query.reshape(query.shape[0], head_count, HEAD_DIM)
     key_heads = key_rows.reshape(key_rows.shape[0], head_count, HEAD_DIM)
     value_heads = value_rows.reshape(value_rows.shape[0], head_count, HEAD_DIM)
     scores = jnp.einsum("qhd,khd->hqk", query_heads, key_heads, preferred_element_type=jnp.float32)
     scores = scores + ((key_flags.astype(jnp.float32) - 1.0) * mask_drop)[None, None, :]
-    weights = jnp.exp(scores)
+    weights = jnp.where(real_rows[None, None, :], jnp.exp(scores), 0.0)
     numerator = jnp.einsum(
         "hqk,khd->qhd",
         weights.astype(jnp.bfloat16),
@@ -77,9 +77,9 @@
     kv = jnp.concatenate([kv, flag_rows], axis=0)
     kv = lax.all_gather(kv, "zl", axis=0, tiled=True)
     kv = ring_gather(kv, "x")
-    kv = kv.reshape(-1, rows + 8, 2 * width)
-    key_flags = kv[:, rows, :rows].reshape(-1)
-    kv = kv[:, :rows].reshape(-1, 2 * width)
+    blocks = kv.reshape(-1, rows + 8, 2 * width)
+    key_flags = jnp.pad(blocks[:, rows, :rows], ((0, 0), (0, 8))).reshape(-1)
+    real_rows = (jnp.arange(rows + 8) < rows)[None, :].repeat(blocks.shape[0], 0).reshape(-1)
 
     local = hidden[0]
     features = lax.all_gather(local, HEAD, axis=1, tiled=True)
@@ -89,7 +89,7 @@
     query = jnp.dot(normed, w_query[0], preferred_element_type=jnp.float32).astype(jnp.bfloat16)
 
     more_num, more_den = attend_terms(
-        query, kv[:, :width], kv[:, width:], key_flags
+        query, kv[:, :width], kv[:, width:], key_flags, real_rows
     )
     spread = jnp.repeat(more_den, HEAD_DIM, axis=1)
     attended = (more_num / spread).astype(jnp.bfloat16)

time: 235 us -> 235 us (level)
    unnamed x21 -> x20, local copies, waits for them, and re-layouts: 10.9 us -> 5.83 us
    slice x1 -> x2, local copies, waits for them, and re-layouts: 3.74 us -> 7.54 us  [shards(): kv[:, :width]]
  transfers between devices with their start and end apart: 8 -> 8, of which waited for: 5 -> 4; matrix products, arithmetic and copies ran while one was open for 6% -> 7% of each run, Pallas kernels for 0% -> 0%
where the time goes in v6:
time: 235 us; the launch traced here: 234 us
  waiting for transfers between devices  109 us (46%)
  blocking collectives  42.1 us (18%)
  starting transfers between devices  25.8 us (11%)
  local copies, waits for them, and re-layouts  24 us (10%)
  matrix products  14.8 us (6%)
  between operations  13.3 us (6%)
  other arithmetic  5.01 us (2%)
    reduce_scatter x1, waiting for transfers between devices, shards(): lax.psum_scatter(partial_terms.astype(jnp.bfloat16), HEAD, scatter_dimens...  47 us
    all_gather x1, waiting for transfers between devices, shards(): packed = lax.all_gather(packed, HEAD, axis=0, tiled=True)  40.7 us
    ppermute x5, starting transfers between devices, shifted(): lax.ppermute(x, axis, [(i, (i + by) % length) for i in range(length)])  25.7 us
    ppermute x5, waiting for transfers between devices, shifted(): lax.ppermute(x, axis, [(i, (i + by) % length) for i in range(length)])  20.9 us
    all_gather x1, blocking collectives, shards(): kv = lax.all_gather(kv, 'zl', axis=0, tiled=True)  16.5 us
    all_gather x1, blocking collectives, shards(): packed = lax.all_gather(packed, 'zh', axis=0, tiled=True)  13.6 us
    all_gather x1, blocking collectives, shards(): packed = lax.all_gather(packed, 'core', axis=0, tiled=True)  12 us
    slice x2, local copies, waits for them, and re-layouts, shards(): kv[:, :width]  7.54 us
  transfers between devices with their start and end apart: 8, of which 4 were waited for; matrix products, arithmetic and copies ran while one was open for 7% of the time, Pallas kernels for 0%

profile of v6, /device:TPU:1, one launch (start us, length us, event | category | flops | bytes accessed | tf_op | source)
XLA Modules:
  0.0 234.5 jit_solution(3306137059090187450)
XLA Ops:
  7.2 1.3 fusion.50
  8.6 0.8 fusion.49
  9.4 12.0 %all-gather.1 = bf16[2,4,4224]{2,1,0:T(4,128)(2,1)S(1)} all-gather(bf16[1,4,4224]{2,1,0:T(4,128)(2,1)S(1)} %fusion.49), channel_id=1, replica_groups=mesh['zh'=3,'core'=2,'x'=4,'zl'=4,'y'=8] {'core'}, dimensions={0}, use_global_device_ids=true | all-gather | bytes 101376 | tf_op jit(solution)/shard_map/all_gather | solution.py:64
  21.4 13.6 %all_gather.16 = bf16[24,4224]{1,0:T(8,128)(2,1)} all-gather(bf16[8,4224]{1,0:T(8,128)(2,1)S(1)} %reshape.107), channel_id=1, replica_groups=mesh['zh'=3,'core'=2,'x'=4,'zl'=4,'y'=8] {'zh'}, dimensions={0}, use_global_device_ids=true | all-gather | bytes 270336 | tf_op jit(solution)/shard_map/all_gather | solution.py:65
  35.8 40.7 %all-gather.5.cloned.1.call-done = bf16[192,4224]{1,0:T(8,128)(2,1)} async-done(((bf16[24,4224]{1,0:T(8,128)(2,1)}), bf16[192,4224]{1,0:T(8,128)(2,1)}) %all-gather.5.cloned.1.call-update) | async-done | bytes 1622032 | tf_op jit(solution)/shard_map/all_gather | solution.py:66
  76.6 0.9 slice_reduce_fusion
  77.5 2.8 %fusion.34 = bf16[192,256]{1,0:T(8,128)(2,1)S(1)} fusion(bf16[1,4096,256]{2,1,0:T(8,128)(2,1)} %param.16, bf16[192,4224]{1,0:T(8,128)(2,1)} %all-gather.5.cloned.1.call-done), kind=kOutput, calls=%fused_computation.26 | convolution fusion | flops 402702336 | bytes 3768320 | tf_op jit(solution)/shard_map/dot_general | solution.py:69
  81.3 16.5 %all_gather.18 = bf16[800,512]{1,0:T(8,128)(2,1)S(1)} all-gather(bf16[200,512]{1,0:T(8,128)(2,1)S(1)} %fusion.46), channel_id=1, replica_groups=mesh['zh'=3,'core'=2,'x'=4,'zl'=4,'y'=8] {'zl'}, dimensions={0}, use_global_device_ids=true | all-gather | bytes 1024000 | tf_op jit(solution)/shard_map/all_gather | solution.py:78
  97.8 3.1 %collective-permute-start.1 = (bf16[800,512]{1,0:T(8,128)(2,1)S(1)}, bf16[800,512]{1,0:T(8,128)(2,1)}, u32[]{:S(2)}, u32[]{:S(2)}) collective-permute-start(bf16[800,512]{1,0:T(8,128)(2,1)S(1)} %all_gather.18), channel_id=1, source_target_pairs={{0,32},{32,64},{64,96},{96,0},{1,33},{33,65},{65,97},{97,1},{2,34}... | collective-permute-start | bytes 2457608 | tf_op jit(solution)/shard_map/ppermute | solution.py:19
  101.0 3.4 %collective-permute-start = (bf16[800,512]{1,0:T(8,128)(2,1)S(1)}, bf16[800,512]{1,0:T(8,128)(2,1)}, u32[]{:S(2)}, u32[]{:S(2)}) collective-permute-start(bf16[800,512]{1,0:T(8,128)(2,1)S(1)} %all_gather.18), channel_id=1, source_target_pairs={{0,96},{32,0},{64,32},{96,64},{1,97},{33,1},{65,33},{97,65},{2,98}... | collective-permute-start | bytes 2457608 | tf_op jit(solution)/shard_map/ppermute | solution.py:19
  104.5 0.9 constant_dynamic-update-slice_fusion.4
  105.5 8.9 %collective-permute-done.1 = bf16[800,512]{1,0:T(8,128)(2,1)} collective-permute-done((bf16[800,512]{1,0:T(8,128)(2,1)S(1)}, bf16[800,512]{1,0:T(8,128)(2,1)}, u32[]{:S(2)}, u32[]{:S(2)}) %collective-permute-start.1) | collective-permute-done | bytes 819232 | tf_op jit(solution)/shard_map/ppermute | solution.py:19
  114.3 1.8 slice.60
  116.1 1.9 collective-permute-start.2
  118.0 1.0 slice.61
  119.1 4.6 %collective-permute-start.3 = (bf16[400,512]{1,0:T(8,128)(2,1)S(1)}, bf16[400,512]{1,0:T(8,128)(2,1)S(1)}, u32[]{:S(2)}, u32[]{:S(2)}) collective-permute-start(bf16[400,512]{1,0:T(8,128)(2,1)S(1)} %slice.61), channel_id=1, source_target_pairs={{0,96},{32,0},{64,32},{96,64},{1,97},{33,1},{65,33},{97,65},{2,98}... | collective-permute-start | bytes 1228808 | tf_op jit(solution)/shard_map/ppermute | solution.py:19
  123.7 2.1 constant_dynamic-update-slice_fusion.3
  125.8 2.2 fusion.5
  128.0 2.8 %fusion.24 = bf16[256,256]{0,1:T(8,128)(2,1)S(1)} fusion(bf16[1,4096,256]{2,1,0:T(8,128)(2,1)} %param.14, bf16[1,256,4096]{2,1,0:T(8,128)(2,1)S(1)} %copy-done.1, f32[4096]{0:T(1024)S(1)} %bitcast.57, f32[256]{0:T(256)S(1)} %add_rsqrt_fusion), kind=kOutput, calls=%fused_computation.24 | convolution fusion | flops 541130752 | bytes 4342784 | tf_op jit(solution)/shard_map/dot_general | solution.py:89
  130.8 0.8 constant_dynamic-update-slice_fusion.2
  131.6 0.8 constant_dynamic-update-slice_fusion.1
  132.4 2.1 constant_dynamic-update-slice_fusion
  134.5 3.8 %fusion.52 = (bf16[3200,256]{1,0:T(8,128)(2,1)}, bf16[3200,256]{1,0:T(8,128)(2,1)}) fusion(bf16[3200,512]{1,0:T(8,128)(2,1)} %constant_dynamic-update-slice_fusion), kind=kLoop, calls=%fused_computation.50 | loop fusion | bytes 6553600 | tf_op jit(solution)/shard_map/slice | solution.py:92
  138.3 0.8 slice.64
  139.3 3.7 %copy.19 = bf16[3200,256]{0,1:T(8,128)(2,1)} copy(bf16[3200,256]{1,0:T(8,128)(2,1)} %get-tuple-element.29) | data formatting | bytes 3276800 | tf_op jit(solution)/shard_map/slice | solution.py:92
  143.0 3.7 %copy.18 = bf16[3200,256]{0,1:T(8,128)(2,1)} copy(bf16[3200,256]{1,0:T(8,128)(2,1)} %get-tuple-element.30) | data formatting | bytes 3276800 | tf_op jit(solution)/shard_map/slice | solution.py:92
  146.7 4.3 %fusion = (f32[4,256]{1,0:T(4,128)S(1)}, f32[4,256,3200]{2,1,0:T(8,128)S(1)}) fusion(f32[3200]{0:T(1024)S(1)} %mul.46, pred[3200]{0:T(1024)(128)(4,1)S(1)} %broadcast_in_dim.30, bf16[256,4,64]{0,2,1:T(8,128)(2,1)S(1)} %bitcast.58, bf16[3200,4,64]{0,2,1:T(8,128)(2,1)} %bitcast.53), kind=kOutput, calls=%fused_computation.1 | convolution fusion | flops 429259776 | bytes 14896768 | tf_op jit(solution)/shard_map/qhd,khd->hqk/dot_general | solution.py:46
  151.0 2.3 fusion.42
  153.3 2.1 convolution_convert_fusion
  155.4 47.0 %reduce-scatter.2.cloned.1.call-done = bf16[256,512]{1,0:T(8,128)(2,1)} async-done(((bf16[256,4096]{1,0:T(8,128)(2,1)}), bf16[256,512]{1,0:T(8,128)(2,1)}) %reduce-scatter.2.cloned.1.call-update) | async-done | bytes 262160 | tf_op jit(solution)/shard_map/reduce_scatter | solution.py:97
  202.4 12.8 %collective-permute-start.4 = (bf16[256,512]{1,0:T(8,128)(2,1)}, bf16[256,512]{1,0:T(8,128)(2,1)S(1)}, u32[]{:S(2)}, u32[]{:S(2)}) collective-permute-start(bf16[256,512]{1,0:T(8,128)(2,1)} %reduce-scatter.2.cloned.1.call-done), channel_id=1, source_target_pairs={{0,128},{128,256},{256,384},{384,512},{512,640},{640,0},{1,129},{1... | collective-permute-start | bytes 786440 | tf_op jit(solution)/shard_map/ppermute | solution.py:19
  215.2 12.0 %collective-permute-done.4 = bf16[256,512]{1,0:T(8,128)(2,1)S(1)} collective-permute-done((bf16[256,512]{1,0:T(8,128)(2,1)}, bf16[256,512]{1,0:T(8,128)(2,1)S(1)}, u32[]{:S(2)}, u32[]{:S(2)}) %collective-permute-start.4) | collective-permute-done | bytes 262176 | tf_op jit(solution)/shard_map/ppermute | solution.py:19
  (37 shorter events, 3.6 us)
Async XLA Ops:
  6.5 146.8 %copy-start = (bf16[1,256,4096]{2,1,0:T(8,128)(2,1)S(1)}, bf16[1,256,4096]{2,1,0:T(8,128)(2,1)}, u32[]{:S(2)}) copy-start(bf16[1,256,4096]{2,1,0:T(8,128)(2,1)} %param.17) | copy-start | bytes 6291460
  6.5 70.0 %all-gather.5.cloned.1.call-start = ((), (), s32[]{:S(2)}) async-start(), calls=%async_computation.1 | async-start | bytes 1824768 | tf_op jit(solution)/shard_map/all_gather | solution.py:66
  35.0 90.7 %all-gather.7.cloned.1.call-start = ((), (), s32[]{:S(2)}) async-start(), calls=%async_computation.3 | async-start | bytes 2359296 | tf_op jit(solution)/shard_map/all_gather | solution.py:85
  35.8 166.6 %reduce-scatter.2.cloned.1.call-start = ((), (), s32[]{:S(2)}) async-start(), calls=%async_computation.2 | async-start | bytes 2359296 | tf_op jit(solution)/shard_map/reduce_scatter | solution.py:97
  77.5 2.8 %copy-start.4 = (bf16[192,4224]{1,0:T(8,128)(2,1)S(1)}, bf16[192,4224]{1,0:T(8,128)(2,1)}, u32[]{:S(2)}) copy-start(bf16[192,4224]{1,0:T(8,128)(2,1)} %all-gather.5.cloned.1.call-done) | copy-start | bytes 4866052
  77.5 3.2 %copy-start.5 = (bf16[1,4096,256]{2,1,0:T(8,128)(2,1)S(1)}, bf16[1,4096,256]{2,1,0:T(8,128)(2,1)}, u32[]{:S(2)}) copy-start(bf16[1,4096,256]{2,1,0:T(8,128)(2,1)} %param.15) | copy-start | bytes 6291460
  80.7 23.8 %copy-start.3 = (bf16[1,4096]{1,0:T(2,128)(2,1)S(1)}, bf16[1,4096]{1,0:T(2,128)(2,1)}, u32[]{:S(2)}) copy-start(bf16[1,4096]{1,0:T(2,128)(2,1)} %param.13) | copy-start | bytes 24580
  97.8 16.5 %collective-permute-start.1 = (bf16[800,512]{1,0:T(8,128)(2,1)S(1)}, bf16[800,512]{1,0:T(8,128)(2,1)}, u32[]{:S(2)}, u32[]{:S(2)}) collective-permute-start(bf16[800,512]{1,0:T(8,128)(2,1)S(1)} %all_gather.18), channel_id=1, source_target_pairs={{0,32},{32,64},{64,96},{96,0},{1,33},{33,65},{65,97},{97,1},{2,34}... | collective-permute-start | bytes 2457608 | tf_op jit(solution)/shard_map/ppermute | solution.py:19
  101.0 17.1 %collective-permute-start = (bf16[800,512]{1,0:T(8,128)(2,1)S(1)}, bf16[800,512]{1,0:T(8,128)(2,1)}, u32[]{:S(2)}, u32[]{:S(2)}) collective-permute-start(bf16[800,512]{1,0:T(8,128)(2,1)S(1)} %all_gather.18), channel_id=1, source_target_pairs={{0,96},{32,0},{64,32},{96,64},{1,97},{33,1},{65,33},{97,65},{2,98}... | collective-permute-start | bytes 2457608 | tf_op jit(solution)/shard_map/ppermute | solution.py:19
  116.1 14.7 %collective-permute-start.2 = (bf16[400,512]{1,0:T(8,128)(2,1)}, bf16[400,512]{1,0:T(8,128)(2,1)S(1)}, u32[]{:S(2)}, u32[]{:S(2)}) collective-permute-start(bf16[400,512]{1,0:T(8,128)(2,1)} %slice.60), channel_id=1, source_target_pairs={{0,32},{32,64},{64,96},{96,0},{1,33},{33,65},{65,97},{97,1},{2,34}... | collective-permute-start | bytes 1228808 | tf_op jit(solution)/shard_map/ppermute | solution.py:19
  119.1 12.5 %collective-permute-start.3 = (bf16[400,512]{1,0:T(8,128)(2,1)S(1)}, bf16[400,512]{1,0:T(8,128)(2,1)S(1)}, u32[]{:S(2)}, u32[]{:S(2)}) collective-permute-start(bf16[400,512]{1,0:T(8,128)(2,1)S(1)} %slice.61), channel_id=1, source_target_pairs={{0,96},{32,0},{64,32},{96,64},{1,97},{33,1},{65,33},{97,65},{2,98}... | collective-permute-start | bytes 1228808 | tf_op jit(solution)/shard_map/ppermute | solution.py:19
  125.8 2.2 copy-start.1
  146.7 4.3 %copy-start.2 = (bf16[3200,256]{0,1:T(8,128)(2,1)S(1)}, bf16[3200,256]{0,1:T(8,128)(2,1)}, u32[]{:S(2)}) copy-start(bf16[3200,256]{0,1:T(8,128)(2,1)} %copy.18) | copy-start | bytes 4915204
  202.4 24.8 %collective-permute-start.4 = (bf16[256,512]{1,0:T(8,128)(2,1)}, bf16[256,512]{1,0:T(8,128)(2,1)S(1)}, u32[]{:S(2)}, u32[]{:S(2)}) collective-permute-start(bf16[256,512]{1,0:T(8,128)(2,1)} %reduce-scatter.2.cloned.1.call-done), channel_id=1, source_target_pairs={{0,128},{128,256},{256,384},{384,512},{512,640},{640,0},{1,129},{1... | collective-permute-start | bytes 786440 | tf_op jit(solution)/shard_map/ppermute | solution.py:19
Sparse Core Ops, SparseCore 0:
  35.2 41.3 all-gather.4
  78.9 44.8 all-gather.6
  155.5 46.8 reduce-scatter.1

commit v7 on v5

--- a/solution.py
+++ b/solution.py
@@ -20,6 +20,10 @@
 
 
 def ring_gather(x, axis):
+    return jnp.concatenate(ring_pieces(x, axis), axis=0)
+
+
+def ring_pieces(x, axis):
     length = lax.axis_size(axis)
     pieces = {0: x}
     left, right = x, x
@@ -35,7 +39,7 @@
         if step < length - step:
             right = shifted(right, axis, -1)
             pieces[step] = right
-    return jnp.concatenate([pieces[r] for r in range(length)], axis=0)
+    return [pieces[r] for r in range(length)]
 
 
 def attend_terms(query, key_rows, value_rows, key_flags):
@@ -63,17 +67,21 @@
     packed = jnp.concatenate([memory, flags], axis=1)
     packed = lax.all_gather(packed, "core", axis=0, tiled=True)
     packed = lax.all_gather(packed, "zh", axis=0, tiled=True)
-    packed = lax.all_gather(packed, HEAD, axis=0, tiled=True)
-    encoder_rows = packed[:, :model]
-    key_rows = jnp.dot(encoder_rows, w_key[0], preferred_element_type=jnp.float32).astype(jnp.bfloat16)
-    value_rows = jnp.dot(encoder_rows, w_value[0], preferred_element_type=jnp.float32).astype(
-        jnp.bfloat16
+    both = jnp.concatenate([w_key[0], w_value[0]], axis=1)
+    pieces = ring_pieces(packed, HEAD)
+    kv = jnp.concatenate(
+        [
+            jnp.dot(p[:, :model], both, preferred_element_type=jnp.float32).astype(jnp.bfloat16)
+            for p in pieces
+        ],
+        axis=0,
     )
-    width = key_rows.shape[1]
+    packed = jnp.concatenate([p[:, model:model + 1] for p in pieces], axis=0)
+    key_rows = kv
+    width = w_key.shape[2]
     rows = key_rows.shape[0]
     flag_rows = jnp.zeros((8, 2 * width), jnp.bfloat16)
-    flag_rows = flag_rows.at[0, :rows].set(packed[:, model])
-    kv = jnp.concatenate([key_rows, value_rows], axis=1)
+    flag_rows = flag_rows.at[0, :rows].set(packed[:, 0])
     kv = jnp.concatenate([kv, flag_rows], axis=0)
     kv = lax.all_gather(kv, "zl", axis=0, tiled=True)
     kv = ring_gather(kv, "x")
@@ -81,7 +89,7 @@
     key_flags = kv[:, rows, :rows].reshape(-1)
     kv = kv[:, :rows].reshape(-1, 2 * width)
 
-    local = hidden[0]
+    local, packed = lax.optimization_barrier((hidden[0], packed))
     features = lax.all_gather(local, HEAD, axis=1, tiled=True)
     widened = features.astype(jnp.float32)
     inverse = lax.rsqrt(jnp.mean(widened * widened, axis=1, keepdims=True) + norm_eps)

time: 235 us -> 234 us (level)
  waiting for transfers between devices: 111 us -> 76.8 us
  starting transfers between devices: 25.9 us -> 52.7 us
  matrix products: 13.9 us -> 24.3 us
  local copies, waits for them, and re-layouts: 22 us -> 14.5 us
  blocking collectives: 42.2 us -> 45.9 us
    all_gather x1 -> x0, waiting for transfers between devices: 40.7 us -> none  [shards(): packed = lax.all_gather(packed, HEAD, axis=0, tiled=True)]
    ppermute x5 -> x13, starting transfers between devices: 25.8 us -> 52.7 us  [shifted(): lax.ppermute(x, axis, [(i, (i + by) % length) for i in range(length)])]
    dot_general x2 -> x8, matrix products: 3.37 us -> 14.6 us  [shards(): jnp.dot(p[:, :model], both, preferred_element_type=jnp.float32)]
    ppermute x5 -> x13, waiting for transfers between devices: 20.9 us -> 30.3 us  [shifted(): lax.ppermute(x, axis, [(i, (i + by) % length) for i in range(length)])]
    all_gather x1, blocking collectives: 16.5 us -> 20 us  [shards(): kv = lax.all_gather(kv, 'zl', axis=0, tiled=True)]
    unnamed x21 -> x31, local copies, waits for them, and re-layouts: 10.9 us -> 7.58 us
  transfers between devices with their start and end apart: 8 -> 15, of which waited for: 5 -> 7; matrix products, arithmetic and copies ran while one was open for 6% -> 11% of each run, Pallas kernels for 0% -> 0%
where the time goes in v7:
time: 234 us; the launch traced here: 233 us
  waiting for transfers between devices  76.8 us (33%)
  starting transfers between devices  52.7 us (23%)
  blocking collectives  45.9 us (20%)
  matrix products  24.3 us (10%)
  local copies, waits for them, and re-layouts  14.5 us (6%)
  between operations  13.8 us (6%)
  other arithmetic  4.89 us (2%)
    ppermute x13, starting transfers between devices, shifted(): lax.ppermute(x, axis, [(i, (i + by) % length) for i in range(length)])  52.7 us
    reduce_scatter x1, waiting for transfers between devices, shards(): lax.psum_scatter(partial_terms.astype(jnp.bfloat16), HEAD, scatter_dimens...  46.5 us
    ppermute x13, waiting for transfers between devices, shifted(): lax.ppermute(x, axis, [(i, (i + by) % length) for i in range(length)])  30.3 us
    all_gather x1, blocking collectives, shards(): kv = lax.all_gather(kv, 'zl', axis=0, tiled=True)  20 us
    dot_general x8, matrix products, shards(): jnp.dot(p[:, :model], both, preferred_element_type=jnp.float32)  14.6 us
    all_gather x1, blocking collectives, shards(): packed = lax.all_gather(packed, 'zh', axis=0, tiled=True)  14 us
    all_gather x1, blocking collectives, shards(): packed = lax.all_gather(packed, 'core', axis=0, tiled=True)  12 us
    unnamed x31, local copies, waits for them, and re-layouts  7.58 us
  transfers between devices with their start and end apart: 15, of which 7 were waited for; matrix products, arithmetic and copies ran while one was open for 11% of the time, Pallas kernels for 0%

profile of v7, /device:TPU:1, one launch (start us, length us, event | category | flops | bytes accessed | tf_op | source)
XLA Modules:
  0.0 233.0 jit_solution(4664629595056350549)
XLA Ops:
  9.4 12.0 %all-gather = bf16[2,4,4224]{2,1,0:T(4,128)(2,1)S(1)} all-gather(bf16[1,4,4224]{2,1,0:T(4,128)(2,1)S(1)} %fusion.47), channel_id=1, replica_groups=mesh['zh'=3,'core'=2,'x'=4,'zl'=4,'y'=8] {'core'}, dimensions={0}, use_global_device_ids=true | all-gather | bytes 101376 | tf_op jit(solution)/shard_map/all_gather | solution.py:68
  21.4 14.0 %all_gather.13 = bf16[24,4224]{1,0:T(8,128)(2,1)S(1)} all-gather(bf16[8,4224]{1,0:T(8,128)(2,1)S(1)} %reshape.105), channel_id=1, replica_groups=mesh['zh'=3,'core'=2,'x'=4,'zl'=4,'y'=8] {'zh'}, dimensions={0}, use_global_device_ids=true | all-gather | bytes 270336 | tf_op jit(solution)/shard_map/all_gather | solution.py:69
  35.4 3.2 %collective-permute-start.3 = (bf16[24,4224]{1,0:T(8,128)(2,1)S(1)}, bf16[24,4224]{1,0:T(8,128)(2,1)S(1)}, u32[]{:S(2)}, u32[]{:S(2)}) collective-permute-start(bf16[24,4224]{1,0:T(8,128)(2,1)S(1)} %all_gather.13), channel_id=1, source_target_pairs={{0,1},{1,2},{2,3},{3,4},{4,5},{5,6},{6,7},{7,0},{8,9},{9,10},{10,1... | collective-permute-start | bytes 608264 | tf_op jit(solution)/shard_map/ppermute | solution.py:19
  38.6 3.8 %collective-permute-start = (bf16[24,4224]{1,0:T(8,128)(2,1)S(1)}, bf16[24,4224]{1,0:T(8,128)(2,1)S(1)}, u32[]{:S(2)}, u32[]{:S(2)}) collective-permute-start(bf16[24,4224]{1,0:T(8,128)(2,1)S(1)} %all_gather.13), channel_id=1, source_target_pairs={{0,7},{1,0},{2,1},{3,2},{4,3},{5,4},{6,5},{7,6},{8,15},{9,8},{10,9... | collective-permute-start | bytes 608264 | tf_op jit(solution)/shard_map/ppermute | solution.py:19
  42.5 2.9 %fusion.35 = bf16[200,512]{1,0:T(8,128)(2,1)S(1)} fusion(bf16[24,4224]{1,0:T(8,128)(2,1)S(1)} %all_gather.13, bf16[4096,256]{1,0:T(8,128)(2,1)} %bitcast.47, bf16[4096,256]{1,0:T(8,128)(2,1)} %bitcast.55), kind=kOutput, calls=%fused_computation.36 | convolution fusion | flops 109064192 | bytes 4415488 | tf_op jit(solution)/shard_map/dot_general | solution.py:74
  45.6 2.7 %collective-permute-start.4 = (bf16[24,4224]{1,0:T(8,128)(2,1)S(1)}, bf16[24,4224]{1,0:T(8,128)(2,1)S(1)}, u32[]{:S(2)}, u32[]{:S(2)}) collective-permute-start(bf16[24,4224]{1,0:T(8,128)(2,1)S(1)} %collective-permute-done.3), channel_id=1, source_target_pairs={{0,1},{1,2},{2,3},{3,4},{4,5},{5,6},{6,7},{7,0},{8,9},{9,10},{10,1... | collective-permute-start | bytes 608264 | tf_op jit(solution)/shard_map/ppermute | solution.py:19
  48.3 3.8 %collective-permute-start.1 = (bf16[24,4224]{1,0:T(8,128)(2,1)S(1)}, bf16[24,4224]{1,0:T(8,128)(2,1)S(1)}, u32[]{:S(2)}, u32[]{:S(2)}) collective-permute-start(bf16[24,4224]{1,0:T(8,128)(2,1)S(1)} %collective-permute-done), channel_id=1, source_target_pairs={{0,7},{1,0},{2,1},{3,2},{4,3},{5,4},{6,5},{7,6},{8,15},{9,8},{10,9... | collective-permute-start | bytes 608264 | tf_op jit(solution)/shard_map/ppermute | solution.py:19
  52.1 2.9 %fusion.34 = bf16[200,512]{1,0:T(8,128)(2,1)S(1)} fusion(bf16[200,512]{1,0:T(8,128)(2,1)S(1)} %fusion.35, bf16[24,4224]{1,0:T(8,128)(2,1)S(1)} %collective-permute-done, bf16[4096,256]{1,0:T(8,128)(2,1)} %bitcast.48, bf16[4096,256]{1,0:T(8,128)(2,1)} %bitcast.56), kind=kOutput, calls=%fused_computation.34 | convolution fusion | flops 109064192 | bytes 4415488 | tf_op jit(solution)/shard_map/dot_general | solution.py:74
  56.8 4.5 %collective-permute-start.5 = (bf16[24,4224]{1,0:T(8,128)(2,1)S(1)}, bf16[24,4224]{1,0:T(8,128)(2,1)S(1)}, u32[]{:S(2)}, u32[]{:S(2)}) collective-permute-start(bf16[24,4224]{1,0:T(8,128)(2,1)S(1)} %collective-permute-done.4), channel_id=1, source_target_pairs={{0,1},{1,2},{2,3},{3,4},{4,5},{5,6},{6,7},{7,0},{8,9},{9,10},{10,1... | collective-permute-start | bytes 608264 | tf_op jit(solution)/shard_map/ppermute | solution.py:19
  61.3 2.2 collective-permute-start.2
  63.6 3.0 %fusion.33 = bf16[200,512]{1,0:T(8,128)(2,1)S(1)} fusion(bf16[200,512]{1,0:T(8,128)(2,1)S(1)} %fusion.34, bf16[24,4224]{1,0:T(8,128)(2,1)} %copy-done.6, bf16[4096,256]{1,0:T(8,128)(2,1)} %bitcast.49, bf16[4096,256]{1,0:T(8,128)(2,1)} %bitcast.57), kind=kOutput, calls=%fused_computation.32 | convolution fusion | flops 109064192 | bytes 4415488 | tf_op jit(solution)/shard_map/dot_general | solution.py:74
  66.6 3.1 %collective-permute-start.6 = (bf16[12,4224]{1,0:T(8,128)(2,1)S(1)}, bf16[12,4224]{1,0:T(8,128)(2,1)S(1)}, u32[]{:S(2)}, u32[]{:S(2)}) collective-permute-start(bf16[12,4224]{1,0:T(8,128)(2,1)S(1)} %slice.130), channel_id=1, source_target_pairs={{0,1},{1,2},{2,3},{3,4},{4,5},{5,6},{6,7},{7,0},{8,9},{9,10},{10,1... | collective-permute-start | bytes 304136 | tf_op jit(solution)/shard_map/ppermute | solution.py:19
  69.7 3.4 %collective-permute-start.7 = (bf16[12,4224]{1,0:T(8,128)(2,1)S(1)}, bf16[12,4224]{1,0:T(8,128)(2,1)S(1)}, u32[]{:S(2)}, u32[]{:S(2)}) collective-permute-start(bf16[12,4224]{1,0:T(8,128)(2,1)S(1)} %slice.131), channel_id=1, source_target_pairs={{0,7},{1,0},{2,1},{3,2},{4,3},{5,4},{6,5},{7,6},{8,15},{9,8},{10,9... | collective-permute-start | bytes 304136 | tf_op jit(solution)/shard_map/ppermute | solution.py:19
  75.8 3.0 %fusion.31 = bf16[200,512]{1,0:T(8,128)(2,1)S(1)} fusion(bf16[200,512]{1,0:T(8,128)(2,1)S(1)} %fusion.32, bf16[12,4224]{1,0:T(8,128)(2,1)S(1)} %collective-permute-done.6, bf16[12,4224]{1,0:T(8,128)(2,1)S(1)} %collective-permute-done.7, bf16[4096,256]{1,0:T(8,128)(2,1)} %bitcast.50, bf16[4096,256]{1,0:T(8,128)(2,1)} %bitcast.58), kind=kOutput, calls=%fused_computation.28 | convolution fusion | flops 109457408 | bytes 4489216 | tf_op jit(solution)/shard_map/dot_general | solution.py:74
  81.6 20.0 %all_gather.14 = bf16[800,512]{1,0:T(8,128)(2,1)S(1)} all-gather(bf16[200,512]{1,0:T(8,128)(2,1)S(1)} %constant_dynamic-update-slice_fusion), channel_id=1, replica_groups=mesh['zh'=3,'core'=2,'x'=4,'zl'=4,'y'=8] {'zl'}, dimensions={0}, use_global_device_ids=true | all-gather | bytes 1024000 | tf_op jit(solution)/shard_map/all_gather | solution.py:86
  101.6 3.1 %collective-permute-start.9 = (bf16[800,512]{1,0:T(8,128)(2,1)S(1)}, bf16[800,512]{1,0:T(8,128)(2,1)S(1)}, u32[]{:S(2)}, u32[]{:S(2)}) collective-permute-start(bf16[800,512]{1,0:T(8,128)(2,1)S(1)} %all_gather.14), channel_id=1, source_target_pairs={{0,32},{32,64},{64,96},{96,0},{1,33},{33,65},{65,97},{97,1},{2,34}... | collective-permute-start | bytes 2457608 | tf_op jit(solution)/shard_map/ppermute | solution.py:19
  104.7 3.4 %collective-permute-start.8 = (bf16[800,512]{1,0:T(8,128)(2,1)S(1)}, bf16[800,512]{1,0:T(8,128)(2,1)S(1)}, u32[]{:S(2)}, u32[]{:S(2)}) collective-permute-start(bf16[800,512]{1,0:T(8,128)(2,1)S(1)} %all_gather.14), channel_id=1, source_target_pairs={{0,96},{32,0},{64,32},{96,64},{1,97},{33,1},{65,33},{97,65},{2,98}... | collective-permute-start | bytes 2457608 | tf_op jit(solution)/shard_map/ppermute | solution.py:19
  108.1 10.5 %collective-permute-done.9 = bf16[800,512]{1,0:T(8,128)(2,1)S(1)} collective-permute-done((bf16[800,512]{1,0:T(8,128)(2,1)S(1)}, bf16[800,512]{1,0:T(8,128)(2,1)S(1)}, u32[]{:S(2)}, u32[]{:S(2)}) %collective-permute-start.9) | collective-permute-done | bytes 819232 | tf_op jit(solution)/shard_map/ppermute | solution.py:19
  120.5 4.8 %collective-permute-start.11 = (bf16[400,512]{1,0:T(8,128)(2,1)S(1)}, bf16[400,512]{1,0:T(8,128)(2,1)S(1)}, u32[]{:S(2)}, u32[]{:S(2)}) collective-permute-start(bf16[400,512]{1,0:T(8,128)(2,1)S(1)} %slice.145), channel_id=1, source_target_pairs={{0,96},{32,0},{64,32},{96,64},{1,97},{33,1},{65,33},{97,65},{2,98}... | collective-permute-start | bytes 1228808 | tf_op jit(solution)/shard_map/ppermute | solution.py:19
  125.5 3.6 %collective-permute-done.10 = bf16[400,512]{1,0:T(8,128)(2,1)S(1)} collective-permute-done((bf16[400,512]{1,0:T(8,128)(2,1)S(1)}, bf16[400,512]{1,0:T(8,128)(2,1)S(1)}, u32[]{:S(2)}, u32[]{:S(2)}) %collective-permute-start.10) | collective-permute-done | bytes 409632 | tf_op jit(solution)/shard_map/ppermute | solution.py:19
  131.0 2.0 slice.146
  133.1 3.8 %fusion.53 = (bf16[3072,256]{1,0:T(8,128)(2,1)}, bf16[3072,256]{1,0:T(8,128)(2,1)}) fusion(bf16[3072,512]{1,0:T(8,128)(2,1)} %bitcast.35), kind=kLoop, calls=%fused_computation.67 | loop fusion | bytes 6291456 | tf_op jit(solution)/shard_map/slice | solution.py:100
  137.0 2.6 %copy.31 = bf16[3072,256]{0,1:T(8,128)(2,1)} copy(bf16[3072,256]{1,0:T(8,128)(2,1)} %get-tuple-element.31) | data formatting | bytes 3145728
  139.6 2.6 %copy.30 = bf16[3072,256]{0,1:T(8,128)(2,1)} copy(bf16[3072,256]{1,0:T(8,128)(2,1)} %get-tuple-element.32) | data formatting | bytes 3145728
  142.1 2.1 fusion.5
  144.2 3.5 %fusion.17 = bf16[256,256]{0,1:T(8,128)(2,1)S(1)} fusion(bf16[1,4096,256]{2,1,0:T(8,128)(2,1)} %param.14, bf16[256,4096]{1,0:T(8,128)(2,1)} %all-gather.3.cloned.1.call-done, f32[4096]{0:T(1024)S(1)} %bitcast.44, f32[256]{0:T(256)S(1)} %add_rsqrt_fusion), kind=kOutput, calls=%fused_computation.18 | convolution fusion | flops 541130752 | bytes 4342784 | tf_op jit(solution)/shard_map/dot_general | solution.py:97
  147.8 2.1 fusion
  149.9 2.0 fusion.25
  151.9 2.1 convolution_convert_fusion
  154.0 46.5 %reduce-scatter.2.cloned.1.call-done = bf16[256,512]{1,0:T(8,128)(2,1)} async-done(((bf16[256,4096]{1,0:T(8,128)(2,1)}), bf16[256,512]{1,0:T(8,128)(2,1)}) %reduce-scatter.2.cloned.1.call-update) | async-done | bytes 262160 | tf_op jit(solution)/shard_map/reduce_scatter | solution.py:105
  200.6 12.8 %collective-permute-start.12 = (bf16[256,512]{1,0:T(8,128)(2,1)}, bf16[256,512]{1,0:T(8,128)(2,1)S(1)}, u32[]{:S(2)}, u32[]{:S(2)}) collective-permute-start(bf16[256,512]{1,0:T(8,128)(2,1)} %reduce-scatter.2.cloned.1.call-done), channel_id=1, source_target_pairs={{0,128},{128,256},{256,384},{384,512},{512,640},{640,0},{1,129},{1... | collective-permute-start | bytes 786440 | tf_op jit(solution)/shard_map/ppermute | solution.py:19
  213.4 12.0 %collective-permute-done.12 = bf16[256,512]{1,0:T(8,128)(2,1)S(1)} collective-permute-done((bf16[256,512]{1,0:T(8,128)(2,1)}, bf16[256,512]{1,0:T(8,128)(2,1)S(1)}, u32[]{:S(2)}, u32[]{:S(2)}) %collective-permute-start.12) | collective-permute-done | bytes 262176 | tf_op jit(solution)/shard_map/ppermute | solution.py:19
  (79 shorter events, 15.2 us)
Async XLA Ops:
  6.5 145.4 %copy-start = (bf16[1,256,4096]{2,1,0:T(8,128)(2,1)S(1)}, bf16[1,256,4096]{2,1,0:T(8,128)(2,1)}, u32[]{:S(2)}) copy-start(bf16[1,256,4096]{2,1,0:T(8,128)(2,1)} %param.17) | copy-start | bytes 6291460
  6.5 135.6 %all-gather.3.cloned.1.call-start = ((), (), s32[]{:S(2)}) async-start(), calls=%async_computation.1 | async-start | bytes 2359296 | tf_op jit(solution)/shard_map/all_gather | solution.py:93
  35.4 10.0 %collective-permute-start.3 = (bf16[24,4224]{1,0:T(8,128)(2,1)S(1)}, bf16[24,4224]{1,0:T(8,128)(2,1)S(1)}, u32[]{:S(2)}, u32[]{:S(2)}) collective-permute-start(bf16[24,4224]{1,0:T(8,128)(2,1)S(1)} %all_gather.13), channel_id=1, source_target_pairs={{0,1},{1,2},{2,3},{3,4},{4,5},{5,6},{6,7},{7,0},{8,9},{9,10},{10,1... | collective-permute-start | bytes 608264 | tf_op jit(solution)/shard_map/ppermute | solution.py:19
  38.6 7.0 %collective-permute-start = (bf16[24,4224]{1,0:T(8,128)(2,1)S(1)}, bf16[24,4224]{1,0:T(8,128)(2,1)S(1)}, u32[]{:S(2)}, u32[]{:S(2)}) collective-permute-start(bf16[24,4224]{1,0:T(8,128)(2,1)S(1)} %all_gather.13), channel_id=1, source_target_pairs={{0,7},{1,0},{2,1},{3,2},{4,3},{5,4},{6,5},{7,6},{8,15},{9,8},{10,9... | collective-permute-start | bytes 608264 | tf_op jit(solution)/shard_map/ppermute | solution.py:19
  45.6 9.4 %collective-permute-start.4 = (bf16[24,4224]{1,0:T(8,128)(2,1)S(1)}, bf16[24,4224]{1,0:T(8,128)(2,1)S(1)}, u32[]{:S(2)}, u32[]{:S(2)}) collective-permute-start(bf16[24,4224]{1,0:T(8,128)(2,1)S(1)} %collective-permute-done.3), channel_id=1, source_target_pairs={{0,1},{1,2},{2,3},{3,4},{4,5},{5,6},{6,7},{7,0},{8,9},{9,10},{10,1... | collective-permute-start | bytes 608264 | tf_op jit(solution)/shard_map/ppermute | solution.py:19
  48.3 7.7 %collective-permute-start.1 = (bf16[24,4224]{1,0:T(8,128)(2,1)S(1)}, bf16[24,4224]{1,0:T(8,128)(2,1)S(1)}, u32[]{:S(2)}, u32[]{:S(2)}) collective-permute-start(bf16[24,4224]{1,0:T(8,128)(2,1)S(1)} %collective-permute-done), channel_id=1, source_target_pairs={{0,7},{1,0},{2,1},{3,2},{4,3},{5,4},{6,5},{7,6},{8,15},{9,8},{10,9... | collective-permute-start | bytes 608264 | tf_op jit(solution)/shard_map/ppermute | solution.py:19
  55.0 11.5 %copy-start.4 = (bf16[24,4224]{1,0:T(8,128)(2,1)}, bf16[24,4224]{1,0:T(8,128)(2,1)S(1)}, u32[]{:S(2)}) copy-start(bf16[24,4224]{1,0:T(8,128)(2,1)S(1)} %collective-permute-done.4) | copy-start | bytes 608260
  56.0 0.7 copy-start.6
  56.8 16.4 %copy-start.7 = (bf16[1,4096,256]{2,1,0:T(8,128)(2,1)S(1)}, bf16[1,4096,256]{2,1,0:T(8,128)(2,1)}, u32[]{:S(2)}) copy-start(bf16[1,4096,256]{2,1,0:T(8,128)(2,1)} %param.16) | copy-start | bytes 6291460
  56.8 16.4 %copy-start.9 = (bf16[1,4096,256]{2,1,0:T(8,128)(2,1)S(1)}, bf16[1,4096,256]{2,1,0:T(8,128)(2,1)}, u32[]{:S(2)}) copy-start(bf16[1,4096,256]{2,1,0:T(8,128)(2,1)} %param.15) | copy-start | bytes 6291460
  56.8 9.8 %collective-permute-start.5 = (bf16[24,4224]{1,0:T(8,128)(2,1)S(1)}, bf16[24,4224]{1,0:T(8,128)(2,1)S(1)}, u32[]{:S(2)}, u32[]{:S(2)}) collective-permute-start(bf16[24,4224]{1,0:T(8,128)(2,1)S(1)} %collective-permute-done.4), channel_id=1, source_target_pairs={{0,1},{1,2},{2,3},{3,4},{4,5},{5,6},{6,7},{7,0},{8,9},{9,10},{10,1... | collective-permute-start | bytes 608264 | tf_op jit(solution)/shard_map/ppermute | solution.py:19
  61.3 8.4 %collective-permute-start.2 = (bf16[24,4224]{1,0:T(8,128)(2,1)}, bf16[24,4224]{1,0:T(8,128)(2,1)S(1)}, u32[]{:S(2)}, u32[]{:S(2)}) collective-permute-start(bf16[24,4224]{1,0:T(8,128)(2,1)} %copy-done.6), channel_id=1, source_target_pairs={{0,7},{1,0},{2,1},{3,2},{4,3},{5,4},{6,5},{7,6},{8,15},{9,8},{10,9... | collective-permute-start | bytes 608264 | tf_op jit(solution)/shard_map/ppermute | solution.py:19
  66.6 7.5 %collective-permute-start.6 = (bf16[12,4224]{1,0:T(8,128)(2,1)S(1)}, bf16[12,4224]{1,0:T(8,128)(2,1)S(1)}, u32[]{:S(2)}, u32[]{:S(2)}) collective-permute-start(bf16[12,4224]{1,0:T(8,128)(2,1)S(1)} %slice.130), channel_id=1, source_target_pairs={{0,1},{1,2},{2,3},{3,4},{4,5},{5,6},{6,7},{7,0},{8,9},{9,10},{10,1... | collective-permute-start | bytes 304136 | tf_op jit(solution)/shard_map/ppermute | solution.py:19
  69.7 5.8 %collective-permute-start.7 = (bf16[12,4224]{1,0:T(8,128)(2,1)S(1)}, bf16[12,4224]{1,0:T(8,128)(2,1)S(1)}, u32[]{:S(2)}, u32[]{:S(2)}) collective-permute-start(bf16[12,4224]{1,0:T(8,128)(2,1)S(1)} %slice.131), channel_id=1, source_target_pairs={{0,7},{1,0},{2,1},{3,2},{4,3},{5,4},{6,5},{7,6},{8,15},{9,8},{10,9... | collective-permute-start | bytes 304136 | tf_op jit(solution)/shard_map/ppermute | solution.py:19
  75.7 124.9 %reduce-scatter.2.cloned.1.call-start = ((), (), s32[]{:S(2)}) async-start(), calls=%async_computation.2 | async-start | bytes 2359296 | tf_op jit(solution)/shard_map/reduce_scatter | solution.py:105
  75.8 3.1 %copy-start.8 = (bf16[1,4096,256]{2,1,0:T(8,128)(2,1)S(1)}, bf16[1,4096,256]{2,1,0:T(8,128)(2,1)}, u32[]{:S(2)}) copy-start(bf16[1,4096,256]{2,1,0:T(8,128)(2,1)} %param.16) | copy-start | bytes 6291460
  75.8 3.5 %copy-start.10 = (bf16[1,4096,256]{2,1,0:T(8,128)(2,1)S(1)}, bf16[1,4096,256]{2,1,0:T(8,128)(2,1)}, u32[]{:S(2)}) copy-start(bf16[1,4096,256]{2,1,0:T(8,128)(2,1)} %param.15) | copy-start | bytes 6291460
  79.3 0.9 copy-start.5
  80.9 44.4 %copy-start.3 = (bf16[1,4096]{1,0:T(2,128)(2,1)S(1)}, bf16[1,4096]{1,0:T(2,128)(2,1)}, u32[]{:S(2)}) copy-start(bf16[1,4096]{1,0:T(2,128)(2,1)} %param.13) | copy-start | bytes 24580
  101.6 17.0 %collective-permute-start.9 = (bf16[800,512]{1,0:T(8,128)(2,1)S(1)}, bf16[800,512]{1,0:T(8,128)(2,1)S(1)}, u32[]{:S(2)}, u32[]{:S(2)}) collective-permute-start(bf16[800,512]{1,0:T(8,128)(2,1)S(1)} %all_gather.14), channel_id=1, source_target_pairs={{0,32},{32,64},{64,96},{96,0},{1,33},{33,65},{65,97},{97,1},{2,34}... | collective-permute-start | bytes 2457608 | tf_op jit(solution)/shard_map/ppermute | solution.py:19
  104.7 15.8 %collective-permute-start.8 = (bf16[800,512]{1,0:T(8,128)(2,1)S(1)}, bf16[800,512]{1,0:T(8,128)(2,1)S(1)}, u32[]{:S(2)}, u32[]{:S(2)}) collective-permute-start(bf16[800,512]{1,0:T(8,128)(2,1)S(1)} %all_gather.14), channel_id=1, source_target_pairs={{0,96},{32,0},{64,32},{96,64},{1,97},{33,1},{65,33},{97,65},{2,98}... | collective-permute-start | bytes 2457608 | tf_op jit(solution)/shard_map/ppermute | solution.py:19
  118.6 10.5 %collective-permute-start.10 = (bf16[400,512]{1,0:T(8,128)(2,1)S(1)}, bf16[400,512]{1,0:T(8,128)(2,1)S(1)}, u32[]{:S(2)}, u32[]{:S(2)}) collective-permute-start(bf16[400,512]{1,0:T(8,128)(2,1)S(1)} %slice.144), channel_id=1, source_target_pairs={{0,32},{32,64},{64,96},{96,0},{1,33},{33,65},{65,97},{97,1},{2,34}... | collective-permute-start | bytes 1228808 | tf_op jit(solution)/shard_map/ppermute | solution.py:19
  120.5 10.4 %collective-permute-start.11 = (bf16[400,512]{1,0:T(8,128)(2,1)S(1)}, bf16[400,512]{1,0:T(8,128)(2,1)S(1)}, u32[]{:S(2)}, u32[]{:S(2)}) collective-permute-start(bf16[400,512]{1,0:T(8,128)(2,1)S(1)} %slice.145), channel_id=1, source_target_pairs={{0,96},{32,0},{64,32},{96,64},{1,97},{33,1},{65,33},{97,65},{2,98}... | collective-permute-start | bytes 1228808 | tf_op jit(solution)/shard_map/ppermute | solution.py:19
  144.2 3.5 %copy-start.1 = (bf16[3072,256]{0,1:T(8,128)(2,1)S(1)}, bf16[3072,256]{0,1:T(8,128)(2,1)}, u32[]{:S(2)}) copy-start(bf16[3072,256]{0,1:T(8,128)(2,1)} %copy.31) | copy-start | bytes 4718596
  147.8 2.1 copy-start.2
  200.6 24.8 %collective-permute-start.12 = (bf16[256,512]{1,0:T(8,128)(2,1)}, bf16[256,512]{1,0:T(8,128)(2,1)S(1)}, u32[]{:S(2)}, u32[]{:S(2)}) collective-permute-start(bf16[256,512]{1,0:T(8,128)(2,1)} %reduce-scatter.2.cloned.1.call-done), channel_id=1, source_target_pairs={{0,128},{128,256},{256,384},{384,512},{512,640},{640,0},{1,129},{1... | collective-permute-start | bytes 786440 | tf_op jit(solution)/shard_map/ppermute | solution.py:19
Sparse Core Ops, SparseCore 0:
  75.8 45.5 all-gather.2
  154.2 46.3 reduce-scatter.1

commit v8 on v7

--- a/solution.py
+++ b/solution.py
@@ -42,14 +42,14 @@
     return [pieces[r] for r in range(length)]
 
 
-def attend_terms(query, key_rows, value_rows, key_flags):
+def attend_terms(query, key_rows, value_rows, key_flags, real_rows):
     head_count = query.shape[1] // HEAD_DIM
     query_heads = query.reshape(query.shape[0], head_count, HEAD_DIM)
     key_heads = key_rows.reshape(key_rows.shape[0], head_count, HEAD_DIM)
     value_heads = value_rows.reshape(value_rows.shape[0], head_count, HEAD_DIM)
     scores = jnp.einsum("qhd,khd->hqk", query_heads, key_heads, preferred_element_type=jnp.float32)
     scores = scores + ((key_flags.astype(jnp.float32) - 1.0) * mask_drop)[None, None, :]
-    weights = jnp.exp(scores)
+    weights = jnp.where(real_rows[None, None, :], jnp.exp(scores), 0.0)
     numerator = jnp.einsum(
         "hqk,khd->qhd",
         weights.astype(jnp.bfloat16),
@@ -84,21 +84,28 @@
     flag_rows = flag_rows.at[0, :rows].set(packed[:, 0])
     kv = jnp.concatenate([kv, flag_rows], axis=0)
     kv = lax.all_gather(kv, "zl", axis=0, tiled=True)
-    kv = ring_gather(kv, "x")
-    kv = kv.reshape(-1, rows + 8, 2 * width)
-    key_flags = kv[:, rows, :rows].reshape(-1)
-    kv = kv[:, :rows].reshape(-1, 2 * width)
-
-    local, packed = lax.optimization_barrier((hidden[0], packed))
-    features = lax.all_gather(local, HEAD, axis=1, tiled=True)
+    features = lax.all_gather(hidden[0], HEAD, axis=1, tiled=True)
     widened = features.astype(jnp.float32)
     inverse = lax.rsqrt(jnp.mean(widened * widened, axis=1, keepdims=True) + norm_eps)
     normed = (widened * inverse * gain[0].astype(jnp.float32)[None, :]).astype(jnp.bfloat16)
     query = jnp.dot(normed, w_query[0], preferred_element_type=jnp.float32).astype(jnp.bfloat16)
 
-    more_num, more_den = attend_terms(
-        query, kv[:, :width], kv[:, width:], key_flags
-    )
+    kv, query = lax.optimization_barrier((kv, query))
+    kv_pieces = ring_pieces(kv, "x")
+
+
+    more_num, more_den = None, None
+    for piece in kv_pieces:
+        blocks = piece.reshape(-1, rows + 8, 2 * width)
+        key_flags = jnp.pad(blocks[:, rows, :rows], ((0, 0), (0, 8))).reshape(-1)
+        real_rows = (jnp.arange(rows + 8) < rows)[None, :].repeat(blocks.shape[0], 0).reshape(-1)
+        part_num, part_den = attend_terms(
+            query, piece[:, :width], piece[:, width:], key_flags, real_rows
+        )
+        if more_num is None:
+            more_num, more_den = part_num, part_den
+        else:
+            more_num, more_den = more_num + part_num, more_den + part_den
     spread = jnp.repeat(more_den, HEAD_DIM, axis=1)
     attended = (more_num / spread).astype(jnp.bfloat16)
     partial_terms = jnp.dot(attended, w_out[0], preferred_element_type=jnp.float32)

time: 234 us -> 248 us (1.060)
  matrix products: 24.3 us -> 35.8 us
  local copies, waits for them, and re-layouts: 14.5 us -> 23.3 us
  waiting for transfers between devices: 76.8 us -> 71.9 us
  blocking collectives: 45.9 us -> 42.8 us
    ppermute x13, waiting for transfers between devices: 30.3 us -> 23.3 us  [shifted(): lax.ppermute(x, axis, [(i, (i + by) % length) for i in range(length)])]
    slice x2 -> x16, local copies, waits for them, and re-layouts: 5.8 us -> 12.1 us  [the longest x8 7.89 us: shards(): piece[:, :width]]
    dot_general x1 -> x4, matrix products: 2.04 us -> 8.17 us  [attend_terms(): jnp.einsum('hqk,khd->qhd', weights.astype(jnp.bfloat16), value_heads, pre...]
    dot_general x1 -> x4, matrix products: 2.12 us -> 7.96 us  [attend_terms(): jnp.einsum('qhd,khd->hqk', query_heads, key_heads, preferred_element_type...]
    all_gather x1, blocking collectives: 20 us -> 16.8 us  [shards(): kv = lax.all_gather(kv, 'zl', axis=0, tiled=True)]
    unnamed x31 -> x52, local copies, waits for them, and re-layouts: 7.58 us -> 4.82 us
  transfers between devices with their start and end apart: 15 -> 15, of which waited for: 7 -> 8; matrix products, arithmetic and copies ran while one was open for 11% -> 19% of each run, Pallas kernels for 0% -> 0%
where the time goes in v8:
time: 248 us; the launch traced here: 247 us
  waiting for transfers between devices  71.9 us (29%)
  starting transfers between devices  53.6 us (22%)
  blocking collectives  42.8 us (17%)
  matrix products  35.8 us (14%)
  local copies, waits for them, and re-layouts  23.3 us (9%)
  between operations  13.9 us (6%)
  other arithmetic  5.61 us (2%)
    ppermute x13, starting transfers between devices, shifted(): lax.ppermute(x, axis, [(i, (i + by) % length) for i in range(length)])  53.5 us
    reduce_scatter x1, waiting for transfers between devices, shards(): lax.psum_scatter(partial_terms.astype(jnp.bfloat16), HEAD, scatter_dimens...  47.9 us
    ppermute x13, waiting for transfers between devices, shifted(): lax.ppermute(x, axis, [(i, (i + by) % length) for i in range(length)])  23.3 us
    all_gather x1, blocking collectives, shards(): kv = lax.all_gather(kv, 'zl', axis=0, tiled=True)  16.8 us
    dot_general x8, matrix products, shards(): jnp.dot(p[:, :model], both, preferred_element_type=jnp.float32)  14.6 us
    all_gather x1, blocking collectives, shards(): packed = lax.all_gather(packed, 'zh', axis=0, tiled=True)  14 us
    all_gather x1, blocking collectives, shards(): packed = lax.all_gather(packed, 'core', axis=0, tiled=True)  12 us
    dot_general x4, matrix products, attend_terms(): jnp.einsum('hqk,khd->qhd', weights.astype(jnp.bfloat16), value_heads, pre...  8.17 us
  transfers between devices with their start and end apart: 15, of which 8 were waited for; matrix products, arithmetic and copies ran while one was open for 19% of the time, Pallas kernels for 0%

profile of v8, /device:TPU:1, one launch (start us, length us, event | category | flops | bytes accessed | tf_op | source)
XLA Modules:
  0.0 246.9 jit_solution(430510416423669414)
XLA Ops:
  10.1 12.0 %all-gather.1 = bf16[2,4,4224]{2,1,0:T(4,128)(2,1)S(1)} all-gather(bf16[1,4,4224]{2,1,0:T(4,128)(2,1)S(1)} %fusion.80), channel_id=1, replica_groups=mesh['zh'=3,'core'=2,'x'=4,'zl'=4,'y'=8] {'core'}, dimensions={0}, use_global_device_ids=true | all-gather | bytes 101376 | tf_op jit(solution)/shard_map/all_gather | solution.py:68
  22.1 14.0 %all_gather.13 = bf16[24,4224]{1,0:T(8,128)(2,1)S(1)} all-gather(bf16[8,4224]{1,0:T(8,128)(2,1)S(1)} %reshape.188), channel_id=1, replica_groups=mesh['zh'=3,'core'=2,'x'=4,'zl'=4,'y'=8] {'zh'}, dimensions={0}, use_global_device_ids=true | all-gather | bytes 270336 | tf_op jit(solution)/shard_map/all_gather | solution.py:69
  36.1 3.2 %collective-permute-start.3 = (bf16[24,4224]{1,0:T(8,128)(2,1)S(1)}, bf16[24,4224]{1,0:T(8,128)(2,1)S(1)}, u32[]{:S(2)}, u32[]{:S(2)}) collective-permute-start(bf16[24,4224]{1,0:T(8,128)(2,1)S(1)} %all_gather.13), channel_id=1, source_target_pairs={{0,1},{1,2},{2,3},{3,4},{4,5},{5,6},{6,7},{7,0},{8,9},{9,10},{10,1... | collective-permute-start | bytes 608264 | tf_op jit(solution)/shard_map/ppermute | solution.py:19
  39.3 3.8 %collective-permute-start = (bf16[24,4224]{1,0:T(8,128)(2,1)S(1)}, bf16[24,4224]{1,0:T(8,128)(2,1)S(1)}, u32[]{:S(2)}, u32[]{:S(2)}) collective-permute-start(bf16[24,4224]{1,0:T(8,128)(2,1)S(1)} %all_gather.13), channel_id=1, source_target_pairs={{0,7},{1,0},{2,1},{3,2},{4,3},{5,4},{6,5},{7,6},{8,15},{9,8},{10,9... | collective-permute-start | bytes 608264 | tf_op jit(solution)/shard_map/ppermute | solution.py:19
  44.1 2.9 %fusion.68 = bf16[200,512]{1,0:T(8,128)(2,1)S(1)} fusion(bf16[24,4224]{1,0:T(8,128)(2,1)S(1)} %all_gather.13, bf16[4096,256]{1,0:T(8,128)(2,1)} %bitcast.95, bf16[4096,256]{1,0:T(8,128)(2,1)} %bitcast.103), kind=kOutput, calls=%fused_computation.63 | convolution fusion | flops 109064192 | bytes 4415488 | tf_op jit(solution)/shard_map/dot_general | solution.py:74
  47.0 3.3 %collective-permute-done.3 = bf16[24,4224]{1,0:T(8,128)(2,1)S(1)} collective-permute-done((bf16[24,4224]{1,0:T(8,128)(2,1)S(1)}, bf16[24,4224]{1,0:T(8,128)(2,1)S(1)}, u32[]{:S(2)}, u32[]{:S(2)}) %collective-permute-start.3) | collective-permute-done | bytes 202784 | tf_op jit(solution)/shard_map/ppermute | solution.py:19
  51.3 2.0 collective-permute-start.4
  53.2 5.4 %collective-permute-start.1 = (bf16[24,4224]{1,0:T(8,128)(2,1)S(1)}, bf16[24,4224]{1,0:T(8,128)(2,1)S(1)}, u32[]{:S(2)}, u32[]{:S(2)}) collective-permute-start(bf16[24,4224]{1,0:T(8,128)(2,1)S(1)} %collective-permute-done), channel_id=1, source_target_pairs={{0,7},{1,0},{2,1},{3,2},{4,3},{5,4},{6,5},{7,6},{8,15},{9,8},{10,9... | collective-permute-start | bytes 608264 | tf_op jit(solution)/shard_map/ppermute | solution.py:19
  58.6 2.9 %fusion.67 = bf16[200,512]{1,0:T(8,128)(2,1)S(1)} fusion(bf16[200,512]{1,0:T(8,128)(2,1)S(1)} %fusion.68, bf16[24,4224]{1,0:T(8,128)(2,1)S(1)} %collective-permute-done, bf16[4096,256]{1,0:T(8,128)(2,1)} %bitcast.96, bf16[4096,256]{1,0:T(8,128)(2,1)} %bitcast.104), kind=kOutput, calls=%fused_computation.61 | convolution fusion | flops 109064192 | bytes 4415488 | tf_op jit(solution)/shard_map/dot_general | solution.py:74
  61.5 3.8 %collective-permute-done.4 = bf16[24,4224]{1,0:T(8,128)(2,1)S(1)} collective-permute-done((bf16[24,4224]{1,0:T(8,128)(2,1)S(1)}, bf16[24,4224]{1,0:T(8,128)(2,1)S(1)}, u32[]{:S(2)}, u32[]{:S(2)}) %collective-permute-start.4) | collective-permute-done | bytes 202784 | tf_op jit(solution)/shard_map/ppermute | solution.py:19
  66.7 2.8 %collective-permute-start.5 = (bf16[24,4224]{1,0:T(8,128)(2,1)S(1)}, bf16[24,4224]{1,0:T(8,128)(2,1)S(1)}, u32[]{:S(2)}, u32[]{:S(2)}) collective-permute-start(bf16[24,4224]{1,0:T(8,128)(2,1)S(1)} %collective-permute-done.4), channel_id=1, source_target_pairs={{0,1},{1,2},{2,3},{3,4},{4,5},{5,6},{6,7},{7,0},{8,9},{9,10},{10,1... | collective-permute-start | bytes 608264 | tf_op jit(solution)/shard_map/ppermute | solution.py:19
  69.5 3.9 %collective-permute-start.2 = (bf16[24,4224]{1,0:T(8,128)(2,1)}, bf16[24,4224]{1,0:T(8,128)(2,1)S(1)}, u32[]{:S(2)}, u32[]{:S(2)}) collective-permute-start(bf16[24,4224]{1,0:T(8,128)(2,1)} %copy-done.17), channel_id=1, source_target_pairs={{0,7},{1,0},{2,1},{3,2},{4,3},{5,4},{6,5},{7,6},{8,15},{9,8},{10,9... | collective-permute-start | bytes 608264 | tf_op jit(solution)/shard_map/ppermute | solution.py:19
  73.4 3.0 %fusion.66 = bf16[200,512]{1,0:T(8,128)(2,1)S(1)} fusion(bf16[200,512]{1,0:T(8,128)(2,1)S(1)} %fusion.67, bf16[24,4224]{1,0:T(8,128)(2,1)} %copy-done.17, bf16[4096,256]{1,0:T(8,128)(2,1)} %bitcast.97, bf16[4096,256]{1,0:T(8,128)(2,1)} %bitcast.105), kind=kOutput, calls=%fused_computation.59 | convolution fusion | flops 109064192 | bytes 4415488 | tf_op jit(solution)/shard_map/dot_general | solution.py:74
  78.5 4.6 %collective-permute-start.7 = (bf16[12,4224]{1,0:T(8,128)(2,1)S(1)}, bf16[12,4224]{1,0:T(8,128)(2,1)S(1)}, u32[]{:S(2)}, u32[]{:S(2)}) collective-permute-start(bf16[12,4224]{1,0:T(8,128)(2,1)S(1)} %slice.163), channel_id=1, source_target_pairs={{0,7},{1,0},{2,1},{3,2},{4,3},{5,4},{6,5},{7,6},{8,15},{9,8},{10,9... | collective-permute-start | bytes 304136 | tf_op jit(solution)/shard_map/ppermute | solution.py:19
  85.2 3.0 %fusion.64 = bf16[200,512]{1,0:T(8,128)(2,1)S(1)} fusion(bf16[200,512]{1,0:T(8,128)(2,1)S(1)} %fusion.65, bf16[12,4224]{1,0:T(8,128)(2,1)S(1)} %collective-permute-done.6, bf16[12,4224]{1,0:T(8,128)(2,1)S(1)} %collective-permute-done.7, bf16[4096,256]{1,0:T(8,128)(2,1)} %bitcast.98, bf16[4096,256]{1,0:T(8,128)(2,1)} %bitcast.106), kind=kOutput, calls=%fused_computation.55 | convolution fusion | flops 109457408 | bytes 4489216 | tf_op jit(solution)/shard_map/dot_general | solution.py:74
  91.0 16.8 %all_gather.14 = bf16[800,512]{1,0:T(8,128)(2,1)S(1)} all-gather(bf16[200,512]{1,0:T(8,128)(2,1)S(1)} %constant_dynamic-update-slice_fusion), channel_id=1, replica_groups=mesh['zh'=3,'core'=2,'x'=4,'zl'=4,'y'=8] {'zl'}, dimensions={0}, use_global_device_ids=true | all-gather | bytes 1024000 | tf_op jit(solution)/shard_map/all_gather | solution.py:86
  107.9 2.1 fusion
  110.0 3.0 %fusion.56 = bf16[256,256]{1,0:T(8,128)(2,1)S(1)} fusion(bf16[1,4096,256]{2,1,0:T(8,128)(2,1)} %param.14, bf16[1,256,4096]{2,1,0:T(8,128)(2,1)} %all-gather.4.cloned.1.call-done, f32[4096]{0:T(1024)S(1)} %bitcast.89, f32[256]{0:T(256)S(1)} %add_rsqrt_fusion), kind=kOutput, calls=%fused_computation.47 | convolution fusion | flops 541130752 | bytes 4342784 | tf_op jit(solution)/shard_map/dot_general | solution.py:91
  113.0 4.2 %collective-permute-start.8 = (bf16[800,512]{1,0:T(8,128)(2,1)S(1)}, bf16[800,512]{1,0:T(8,128)(2,1)}, u32[]{:S(2)}, u32[]{:S(2)}) collective-permute-start(bf16[800,512]{1,0:T(8,128)(2,1)S(1)} %all_gather.14), channel_id=1, source_target_pairs={{0,96},{32,0},{64,32},{96,64},{1,97},{33,1},{65,33},{97,65},{2,98}... | collective-permute-start | bytes 2457608 | tf_op jit(solution)/shard_map/ppermute | solution.py:19
  121.5 2.3 fusion.91
  125.1 3.3 %fusion.24 = f32[4,64,256]{2,1,0:T(8,128)} fusion(bf16[800,4,64]{0,2,1:T(8,128)(2,1)S(1)} %bitcast.83, f32[4,256,800]{1,2,0:T(8,128)} %fusion.91, f32[800]{0:T(1024)S(1)} %mul.72, pred[800]{0:T(1024)(128)(4,1)S(1)} %broadcast_in_dim.69), kind=kOutput, calls=%fused_computation.28 | convolution fusion | flops 107315200 | bytes 3952544 | tf_op jit(solution)/shard_map/hqk,khd->qhd/dot_general | solution.py:53
  129.9 1.9 fusion.87
  131.8 2.0 copy.68
  135.6 5.2 %collective-permute-start.11 = (bf16[400,512]{1,0:T(8,128)(2,1)}, bf16[400,512]{1,0:T(8,128)(2,1)}, u32[]{:S(2)}, u32[]{:S(2)}) collective-permute-start(bf16[400,512]{1,0:T(8,128)(2,1)} %slice.181), channel_id=1, source_target_pairs={{0,96},{32,0},{64,32},{96,64},{1,97},{33,1},{65,33},{97,65},{2,98}... | collective-permute-start | bytes 1228808 | tf_op jit(solution)/shard_map/ppermute | solution.py:19
  145.0 2.1 collective-permute-start.10
  147.1 2.4 fusion.93
  149.8 3.3 %fusion.18 = f32[4,64,256]{2,1,0:T(8,128)} fusion(bf16[800,4,64]{0,2,1:T(8,128)(2,1)S(1)} %bitcast.84, f32[4,256,800]{1,2,0:T(8,128)} %fusion.93, f32[800]{0:T(1024)S(1)} %mul.78, pred[800]{0:T(1024)(128)(4,1)S(1)} %broadcast_in_dim.69), kind=kOutput, calls=%fused_computation.25 | convolution fusion | flops 107315200 | bytes 3952544 | tf_op jit(solution)/shard_map/hqk,khd->qhd/dot_general | solution.py:53
  161.3 2.7 %fusion.5 = (f32[4,256]{1,0:T(4,128)S(1)}, f32[4,256]{1,0:T(4,128)S(1)}, f32[4,256]{1,0:T(4,128)S(1)}, f32[4,256]{1,0:T(4,128)S(1)}, f32[4,256,800]{1,2,0:T(8,128)S(1)}) fusion(f32[800]{0:T(1024)S(1)} %copy-done.14, pred[800]{0:T(1024)(128)(4,1)S(1)} %copy-done.13, f32[4,256,800]{1,2,0:T(8,128)S(1)} %copy-done.1, f32[800]{0:T(1024)S(1)} %copy-done.8, ...), kind=kOutput, calls=%fused_computation.13 | convolution fusion | flops 114683904 | bytes 13677856 | tf_op jit(solution)/shard_map/qhd,khd->hqk/dot_general | solution.py:50
  164.8 2.1 convolution_convert_fusion
  166.9 47.9 %reduce-scatter.2.cloned.1.call-done = bf16[256,512]{1,0:T(8,128)(2,1)} async-done(((bf16[256,4096]{1,0:T(8,128)(2,1)}), bf16[256,512]{1,0:T(8,128)(2,1)}) %reduce-scatter.2.cloned.1.call-update) | async-done | bytes 262160 | tf_op jit(solution)/shard_map/reduce_scatter | solution.py:112
  214.8 12.5 %collective-permute-start.12 = (bf16[256,512]{1,0:T(8,128)(2,1)}, bf16[256,512]{1,0:T(8,128)(2,1)S(1)}, u32[]{:S(2)}, u32[]{:S(2)}) collective-permute-start(bf16[256,512]{1,0:T(8,128)(2,1)} %reduce-scatter.2.cloned.1.call-done), channel_id=1, source_target_pairs={{0,128},{128,256},{256,384},{384,512},{512,640},{640,0},{1,129},{1... | collective-permute-start | bytes 786440 | tf_op jit(solution)/shard_map/ppermute | solution.py:19
  227.4 12.1 %collective-permute-done.12 = bf16[256,512]{1,0:T(8,128)(2,1)S(1)} collective-permute-done((bf16[256,512]{1,0:T(8,128)(2,1)}, bf16[256,512]{1,0:T(8,128)(2,1)S(1)}, u32[]{:S(2)}, u32[]{:S(2)}) %collective-permute-start.12) | collective-permute-done | bytes 262176 | tf_op jit(solution)/shard_map/ppermute | solution.py:19
  (131 shorter events, 36.4 us)
Async XLA Ops:
  6.5 158.3 %copy-start = (bf16[1,256,4096]{2,1,0:T(8,128)(2,1)S(1)}, bf16[1,256,4096]{2,1,0:T(8,128)(2,1)}, u32[]{:S(2)}) copy-start(bf16[1,256,4096]{2,1,0:T(8,128)(2,1)} %param.17) | copy-start | bytes 6291460
  6.5 101.3 %all-gather.4.cloned.1.call-start = ((), (), s32[]{:S(2)}) async-start(), calls=%async_computation.2 | async-start | bytes 2359296 | tf_op jit(solution)/shard_map/all_gather | solution.py:87
  7.3 207.6 %reduce-scatter.2.cloned.1.call-start = ((), (), s32[]{:S(2)}) async-start(), calls=%async_computation.1 | async-start | bytes 2359296 | tf_op jit(solution)/shard_map/reduce_scatter | solution.py:112
  36.1 14.2 %collective-permute-start.3 = (bf16[24,4224]{1,0:T(8,128)(2,1)S(1)}, bf16[24,4224]{1,0:T(8,128)(2,1)S(1)}, u32[]{:S(2)}, u32[]{:S(2)}) collective-permute-start(bf16[24,4224]{1,0:T(8,128)(2,1)S(1)} %all_gather.13), channel_id=1, source_target_pairs={{0,1},{1,2},{2,3},{3,4},{4,5},{5,6},{6,7},{7,0},{8,9},{9,10},{10,1... | collective-permute-start | bytes 608264 | tf_op jit(solution)/shard_map/ppermute | solution.py:19
  39.3 11.8 %collective-permute-start = (bf16[24,4224]{1,0:T(8,128)(2,1)S(1)}, bf16[24,4224]{1,0:T(8,128)(2,1)S(1)}, u32[]{:S(2)}, u32[]{:S(2)}) collective-permute-start(bf16[24,4224]{1,0:T(8,128)(2,1)S(1)} %all_gather.13), channel_id=1, source_target_pairs={{0,7},{1,0},{2,1},{3,2},{4,3},{5,4},{6,5},{7,6},{8,15},{9,8},{10,9... | collective-permute-start | bytes 608264 | tf_op jit(solution)/shard_map/ppermute | solution.py:19
  43.3 106.5 %copy-start.12 = (pred[800]{0:T(1024)(128)(4,1)}, pred[800]{0:T(1024)(128)(4,1)S(1)}, u32[]{:S(2)}) copy-start(pred[800]{0:T(1024)(128)(4,1)S(1)} %broadcast_in_dim.69) | copy-start | bytes 2404
  51.3 14.1 %collective-permute-start.4 = (bf16[24,4224]{1,0:T(8,128)(2,1)S(1)}, bf16[24,4224]{1,0:T(8,128)(2,1)S(1)}, u32[]{:S(2)}, u32[]{:S(2)}) collective-permute-start(bf16[24,4224]{1,0:T(8,128)(2,1)S(1)} %collective-permute-done.3), channel_id=1, source_target_pairs={{0,1},{1,2},{2,3},{3,4},{4,5},{5,6},{6,7},{7,0},{8,9},{9,10},{10,1... | collective-permute-start | bytes 608264 | tf_op jit(solution)/shard_map/ppermute | solution.py:19
  53.2 12.7 %collective-permute-start.1 = (bf16[24,4224]{1,0:T(8,128)(2,1)S(1)}, bf16[24,4224]{1,0:T(8,128)(2,1)S(1)}, u32[]{:S(2)}, u32[]{:S(2)}) collective-permute-start(bf16[24,4224]{1,0:T(8,128)(2,1)S(1)} %collective-permute-done), channel_id=1, source_target_pairs={{0,7},{1,0},{2,1},{3,2},{4,3},{5,4},{6,5},{7,6},{8,15},{9,8},{10,9... | collective-permute-start | bytes 608264 | tf_op jit(solution)/shard_map/ppermute | solution.py:19
  65.4 11.1 %copy-start.15 = (bf16[24,4224]{1,0:T(8,128)(2,1)}, bf16[24,4224]{1,0:T(8,128)(2,1)S(1)}, u32[]{:S(2)}) copy-start(bf16[24,4224]{1,0:T(8,128)(2,1)S(1)} %collective-permute-done.4) | copy-start | bytes 608260
  66.7 16.4 %copy-start.18 = (bf16[1,4096,256]{2,1,0:T(8,128)(2,1)S(1)}, bf16[1,4096,256]{2,1,0:T(8,128)(2,1)}, u32[]{:S(2)}) copy-start(bf16[1,4096,256]{2,1,0:T(8,128)(2,1)} %param.16) | copy-start | bytes 6291460
  66.7 16.4 %copy-start.20 = (bf16[1,4096,256]{2,1,0:T(8,128)(2,1)S(1)}, bf16[1,4096,256]{2,1,0:T(8,128)(2,1)}, u32[]{:S(2)}) copy-start(bf16[1,4096,256]{2,1,0:T(8,128)(2,1)} %param.15) | copy-start | bytes 6291460
  66.7 9.8 %collective-permute-start.5 = (bf16[24,4224]{1,0:T(8,128)(2,1)S(1)}, bf16[24,4224]{1,0:T(8,128)(2,1)S(1)}, u32[]{:S(2)}, u32[]{:S(2)}) collective-permute-start(bf16[24,4224]{1,0:T(8,128)(2,1)S(1)} %collective-permute-done.4), channel_id=1, source_target_pairs={{0,1},{1,2},{2,3},{3,4},{4,5},{5,6},{6,7},{7,0},{8,9},{9,10},{10,1... | collective-permute-start | bytes 608264 | tf_op jit(solution)/shard_map/ppermute | solution.py:19
  69.5 8.9 %collective-permute-start.2 = (bf16[24,4224]{1,0:T(8,128)(2,1)}, bf16[24,4224]{1,0:T(8,128)(2,1)S(1)}, u32[]{:S(2)}, u32[]{:S(2)}) collective-permute-start(bf16[24,4224]{1,0:T(8,128)(2,1)} %copy-done.17), channel_id=1, source_target_pairs={{0,7},{1,0},{2,1},{3,2},{4,3},{5,4},{6,5},{7,6},{8,15},{9,8},{10,9... | collective-permute-start | bytes 608264 | tf_op jit(solution)/shard_map/ppermute | solution.py:19
  76.5 7.5 %collective-permute-start.6 = (bf16[12,4224]{1,0:T(8,128)(2,1)S(1)}, bf16[12,4224]{1,0:T(8,128)(2,1)S(1)}, u32[]{:S(2)}, u32[]{:S(2)}) collective-permute-start(bf16[12,4224]{1,0:T(8,128)(2,1)S(1)} %slice.162), channel_id=1, source_target_pairs={{0,1},{1,2},{2,3},{3,4},{4,5},{5,6},{6,7},{7,0},{8,9},{9,10},{10,1... | collective-permute-start | bytes 304136 | tf_op jit(solution)/shard_map/ppermute | solution.py:19
  78.5 6.5 %collective-permute-start.7 = (bf16[12,4224]{1,0:T(8,128)(2,1)S(1)}, bf16[12,4224]{1,0:T(8,128)(2,1)S(1)}, u32[]{:S(2)}, u32[]{:S(2)}) collective-permute-start(bf16[12,4224]{1,0:T(8,128)(2,1)S(1)} %slice.163), channel_id=1, source_target_pairs={{0,7},{1,0},{2,1},{3,2},{4,3},{5,4},{6,5},{7,6},{8,15},{9,8},{10,9... | collective-permute-start | bytes 304136 | tf_op jit(solution)/shard_map/ppermute | solution.py:19
  85.2 3.1 %copy-start.19 = (bf16[1,4096,256]{2,1,0:T(8,128)(2,1)S(1)}, bf16[1,4096,256]{2,1,0:T(8,128)(2,1)}, u32[]{:S(2)}) copy-start(bf16[1,4096,256]{2,1,0:T(8,128)(2,1)} %param.16) | copy-start | bytes 6291460
  85.2 3.5 %copy-start.21 = (bf16[1,4096,256]{2,1,0:T(8,128)(2,1)S(1)}, bf16[1,4096,256]{2,1,0:T(8,128)(2,1)}, u32[]{:S(2)}) copy-start(bf16[1,4096,256]{2,1,0:T(8,128)(2,1)} %param.15) | copy-start | bytes 6291460
  113.0 15.5 %collective-permute-start.8 = (bf16[800,512]{1,0:T(8,128)(2,1)S(1)}, bf16[800,512]{1,0:T(8,128)(2,1)}, u32[]{:S(2)}, u32[]{:S(2)}) collective-permute-start(bf16[800,512]{1,0:T(8,128)(2,1)S(1)} %all_gather.14), channel_id=1, source_target_pairs={{0,96},{32,0},{64,32},{96,64},{1,97},{33,1},{65,33},{97,65},{2,98}... | collective-permute-start | bytes 2457608 | tf_op jit(solution)/shard_map/ppermute | solution.py:19
  118.2 23.6 %collective-permute-start.9 = (bf16[800,512]{1,0:T(8,128)(2,1)S(1)}, bf16[800,512]{1,0:T(8,128)(2,1)}, u32[]{:S(2)}, u32[]{:S(2)}) collective-permute-start(bf16[800,512]{1,0:T(8,128)(2,1)S(1)} %all_gather.14), channel_id=1, source_target_pairs={{0,32},{32,64},{64,96},{96,0},{1,33},{33,65},{65,97},{97,1},{2,34}... | collective-permute-start | bytes 2457608 | tf_op jit(solution)/shard_map/ppermute | solution.py:19
  123.9 10.0 %copy-start.7 = (f32[800]{0:T(1024)}, f32[800]{0:T(1024)S(1)}, u32[]{:S(2)}) copy-start(f32[800]{0:T(1024)S(1)} %mul.72) | copy-start | bytes 9604
  135.6 20.4 %collective-permute-start.11 = (bf16[400,512]{1,0:T(8,128)(2,1)}, bf16[400,512]{1,0:T(8,128)(2,1)}, u32[]{:S(2)}, u32[]{:S(2)}) collective-permute-start(bf16[400,512]{1,0:T(8,128)(2,1)} %slice.181), channel_id=1, source_target_pairs={{0,96},{32,0},{64,32},{96,64},{1,97},{33,1},{65,33},{97,65},{2,98}... | collective-permute-start | bytes 1228808 | tf_op jit(solution)/shard_map/ppermute | solution.py:19
  145.0 10.0 %collective-permute-start.10 = (bf16[400,512]{1,0:T(8,128)(2,1)S(1)}, bf16[400,512]{1,0:T(8,128)(2,1)}, u32[]{:S(2)}, u32[]{:S(2)}) collective-permute-start(bf16[400,512]{1,0:T(8,128)(2,1)S(1)} %slice.180), channel_id=1, source_target_pairs={{0,32},{32,64},{64,96},{96,0},{1,33},{33,65},{65,97},{97,1},{2,34}... | collective-permute-start | bytes 1228808 | tf_op jit(solution)/shard_map/ppermute | solution.py:19
  149.5 6.5 %copy-start.9 = (f32[800]{0:T(1024)}, f32[800]{0:T(1024)S(1)}, u32[]{:S(2)}) copy-start(f32[800]{0:T(1024)S(1)} %mul.78) | copy-start | bytes 9604
  158.4 2.9 %copy-start.2 = (f32[4,256,800]{1,2,0:T(8,128)S(1)}, f32[4,256,800]{1,2,0:T(8,128)}, u32[]{:S(2)}) copy-start(f32[4,256,800]{1,2,0:T(8,128)} %fusion.93) | copy-start | bytes 9830404
  158.4 2.9 %copy-start.4 = (bf16[800,256]{0,1:T(8,128)(2,1)S(1)}, bf16[800,256]{0,1:T(8,128)(2,1)}, u32[]{:S(2)}) copy-start(bf16[800,256]{0,1:T(8,128)(2,1)} %copy.68) | copy-start | bytes 1228804
  158.4 2.9 %copy-start.8 = (f32[800]{0:T(1024)S(1)}, f32[800]{0:T(1024)}, u32[]{:S(2)}) copy-start(f32[800]{0:T(1024)} %copy-done.7) | copy-start | bytes 9604
  158.4 2.9 %copy-start.10 = (f32[800]{0:T(1024)S(1)}, f32[800]{0:T(1024)}, u32[]{:S(2)}) copy-start(f32[800]{0:T(1024)} %copy-done.9) | copy-start | bytes 9604
  158.4 2.9 %copy-start.14 = (f32[800]{0:T(1024)S(1)}, f32[800]{0:T(1024)}, u32[]{:S(2)}) copy-start(f32[800]{0:T(1024)} %mul.74) | copy-start | bytes 9604
  161.3 2.7 %copy-start.3 = (bf16[800,256]{0,1:T(8,128)(2,1)S(1)}, bf16[800,256]{0,1:T(8,128)(2,1)}, u32[]{:S(2)}) copy-start(bf16[800,256]{0,1:T(8,128)(2,1)} %copy.67) | copy-start | bytes 1228804
  161.3 2.7 %copy-start.5 = (f32[4,64,256]{2,1,0:T(8,128)S(1)}, f32[4,64,256]{2,1,0:T(8,128)}, u32[]{:S(2)}) copy-start(f32[4,64,256]{2,1,0:T(8,128)} %fusion.24) | copy-start | bytes 786436
  161.3 2.7 %copy-start.6 = (f32[4,64,256]{2,1,0:T(8,128)S(1)}, f32[4,64,256]{2,1,0:T(8,128)}, u32[]{:S(2)}) copy-start(f32[4,64,256]{2,1,0:T(8,128)} %fusion.18) | copy-start | bytes 786436
  214.8 24.6 %collective-permute-start.12 = (bf16[256,512]{1,0:T(8,128)(2,1)}, bf16[256,512]{1,0:T(8,128)(2,1)S(1)}, u32[]{:S(2)}, u32[]{:S(2)}) collective-permute-start(bf16[256,512]{1,0:T(8,128)(2,1)} %reduce-scatter.2.cloned.1.call-done), channel_id=1, source_target_pairs={{0,128},{128,256},{256,384},{384,512},{512,640},{640,0},{1,129},{1... | collective-permute-start | bytes 786440 | tf_op jit(solution)/shard_map/ppermute | solution.py:19
  (5 other events, 5.0 us)
Sparse Core Ops, SparseCore 0:
  9.7 56.1 all-gather.3
  167.0 47.7 reduce-scatter.1

commit v9 on v8

--- a/solution.py
+++ b/solution.py
@@ -84,15 +84,14 @@
     flag_rows = flag_rows.at[0, :rows].set(packed[:, 0])
     kv = jnp.concatenate([kv, flag_rows], axis=0)
     kv = lax.all_gather(kv, "zl", axis=0, tiled=True)
-    features = lax.all_gather(hidden[0], HEAD, axis=1, tiled=True)
+    kv_pieces = ring_pieces(kv, "x")
+
+    local, packed = lax.optimization_barrier((hidden[0], packed))
+    features = lax.all_gather(local, HEAD, axis=1, tiled=True)
     widened = features.astype(jnp.float32)
     inverse = lax.rsqrt(jnp.mean(widened * widened, axis=1, keepdims=True) + norm_eps)
     normed = (widened * inverse * gain[0].astype(jnp.float32)[None, :]).astype(jnp.bfloat16)
     query = jnp.dot(normed, w_query[0], preferred_element_type=jnp.float32).astype(jnp.bfloat16)
-
-    kv, query = lax.optimization_barrier((kv, query))
-    kv_pieces = ring_pieces(kv, "x")
-
 
     more_num, more_den = None, None
     for piece in kv_pieces:

time: 248 us -> 244 us (0.984)
  matrix products: 35.8 us -> 31.1 us
    dot_general x4, matrix products: 8.17 us -> 2.89 us  [attend_terms(): jnp.einsum('hqk,khd->qhd', weights.astype(jnp.bfloat16), value_heads, pre...]
    dot_general x8, matrix products: 14.6 us -> 18.2 us  [shards(): jnp.dot(p[:, :model], both, preferred_element_type=jnp.float32)]
    dot_general x4, matrix products: 7.96 us -> 4.52 us  [attend_terms(): jnp.einsum('qhd,khd->hqk', query_heads, key_heads, preferred_element_type...]
    unnamed x52 -> x34, local copies, waits for them, and re-layouts: 4.82 us -> 2.28 us
  transfers between devices with their start and end apart: 15 -> 15, of which waited for: 8 -> 5; matrix products, arithmetic and copies ran while one was open for 19% -> 17% of each run, Pallas kernels for 0% -> 0%
where the time goes in v9:
time: 244 us; the launch traced here: 243 us
  waiting for transfers between devices  70.9 us (29%)
  starting transfers between devices  52.6 us (22%)
  blocking collectives  45.2 us (19%)
  matrix products  31.1 us (13%)
  local copies, waits for them, and re-layouts  24.5 us (10%)
  between operations  13.9 us (6%)
  other arithmetic  4.89 us (2%)
    ppermute x13, starting transfers between devices, shifted(): lax.ppermute(x, axis, [(i, (i + by) % length) for i in range(length)])  52.6 us
    reduce_scatter x1, waiting for transfers between devices, shards(): lax.psum_scatter(partial_terms.astype(jnp.bfloat16), HEAD, scatter_dimens...  47.5 us
    ppermute x13, waiting for transfers between devices, shifted(): lax.ppermute(x, axis, [(i, (i + by) % length) for i in range(length)])  23.3 us
    all_gather x1, blocking collectives, shards(): kv = lax.all_gather(kv, 'zl', axis=0, tiled=True)  19.3 us
    dot_general x8, matrix products, shards(): jnp.dot(p[:, :model], both, preferred_element_type=jnp.float32)  18.2 us
    all_gather x1, blocking collectives, shards(): packed = lax.all_gather(packed, 'zh', axis=0, tiled=True)  14 us
    all_gather x1, blocking collectives, shards(): packed = lax.all_gather(packed, 'core', axis=0, tiled=True)  12 us
    slice x8, local copies, waits for them, and re-layouts, shards(): piece[:, :width]  9.08 us
  transfers between devices with their start and end apart: 15, of which 5 were waited for; matrix products, arithmetic and copies ran while one was open for 17% of the time, Pallas kernels for 0%

profile of v9, /device:TPU:1, one launch (start us, length us, event | category | flops | bytes accessed | tf_op | source)
XLA Modules:
  0.0 243.1 jit_solution(17963156128222462946)
XLA Ops:
  7.2 1.3 fusion.80
  9.4 12.0 %all-gather = bf16[2,4,4224]{2,1,0:T(4,128)(2,1)S(1)} all-gather(bf16[1,4,4224]{2,1,0:T(4,128)(2,1)S(1)} %fusion.79), channel_id=1, replica_groups=mesh['zh'=3,'core'=2,'x'=4,'zl'=4,'y'=8] {'core'}, dimensions={0}, use_global_device_ids=true | all-gather | bytes 101376 | tf_op jit(solution)/shard_map/all_gather | solution.py:68
  21.4 14.0 %all_gather.13 = bf16[24,4224]{1,0:T(8,128)(2,1)S(1)} all-gather(bf16[8,4224]{1,0:T(8,128)(2,1)S(1)} %reshape.186), channel_id=1, replica_groups=mesh['zh'=3,'core'=2,'x'=4,'zl'=4,'y'=8] {'zh'}, dimensions={0}, use_global_device_ids=true | all-gather | bytes 270336 | tf_op jit(solution)/shard_map/all_gather | solution.py:69
  35.4 3.2 %collective-permute-start.3 = (bf16[24,4224]{1,0:T(8,128)(2,1)S(1)}, bf16[24,4224]{1,0:T(8,128)(2,1)S(1)}, u32[]{:S(2)}, u32[]{:S(2)}) collective-permute-start(bf16[24,4224]{1,0:T(8,128)(2,1)S(1)} %all_gather.13), channel_id=1, source_target_pairs={{0,1},{1,2},{2,3},{3,4},{4,5},{5,6},{6,7},{7,0},{8,9},{9,10},{10,1... | collective-permute-start | bytes 608264 | tf_op jit(solution)/shard_map/ppermute | solution.py:19
  38.6 3.8 %collective-permute-start = (bf16[24,4224]{1,0:T(8,128)(2,1)S(1)}, bf16[24,4224]{1,0:T(8,128)(2,1)S(1)}, u32[]{:S(2)}, u32[]{:S(2)}) collective-permute-start(bf16[24,4224]{1,0:T(8,128)(2,1)S(1)} %all_gather.13), channel_id=1, source_target_pairs={{0,7},{1,0},{2,1},{3,2},{4,3},{5,4},{6,5},{7,6},{8,15},{9,8},{10,9... | collective-permute-start | bytes 608264 | tf_op jit(solution)/shard_map/ppermute | solution.py:19
  43.6 1.9 collective-permute-start.4
  45.5 4.6 %collective-permute-start.1 = (bf16[24,4224]{1,0:T(8,128)(2,1)S(1)}, bf16[24,4224]{1,0:T(8,128)(2,1)}, u32[]{:S(2)}, u32[]{:S(2)}) collective-permute-start(bf16[24,4224]{1,0:T(8,128)(2,1)S(1)} %collective-permute-done), channel_id=1, source_target_pairs={{0,7},{1,0},{2,1},{3,2},{4,3},{5,4},{6,5},{7,6},{8,15},{9,8},{10,9... | collective-permute-start | bytes 608264 | tf_op jit(solution)/shard_map/ppermute | solution.py:19
  50.1 3.5 %fusion.67 = bf16[200,512]{1,0:T(8,128)(2,1)} fusion(bf16[24,4224]{1,0:T(8,128)(2,1)S(1)} %all_gather.13, bf16[4096,256]{1,0:T(8,128)(2,1)} %bitcast.88, bf16[4096,256]{1,0:T(8,128)(2,1)} %bitcast.96), kind=kOutput, calls=%fused_computation.62 | convolution fusion | flops 109064192 | bytes 4415488 | tf_op jit(solution)/shard_map/dot_general | solution.py:74
  53.8 2.2 collective-permute-start.5
  56.0 4.6 %collective-permute-start.2 = (bf16[24,4224]{1,0:T(8,128)(2,1)}, bf16[24,4224]{1,0:T(8,128)(2,1)S(1)}, u32[]{:S(2)}, u32[]{:S(2)}) collective-permute-start(bf16[24,4224]{1,0:T(8,128)(2,1)} %collective-permute-done.1), channel_id=1, source_target_pairs={{0,7},{1,0},{2,1},{3,2},{4,3},{5,4},{6,5},{7,6},{8,15},{9,8},{10,9... | collective-permute-start | bytes 608264 | tf_op jit(solution)/shard_map/ppermute | solution.py:19
  60.6 3.6 %fusion.66 = bf16[200,512]{1,0:T(8,128)(2,1)} fusion(bf16[200,512]{1,0:T(8,128)(2,1)} %fusion.67, bf16[24,4224]{1,0:T(8,128)(2,1)} %copy-done.8, bf16[4096,256]{1,0:T(8,128)(2,1)} %bitcast.89, bf16[4096,256]{1,0:T(8,128)(2,1)} %bitcast.97), kind=kOutput, calls=%fused_computation.60 | convolution fusion | flops 109064192 | bytes 4415488 | tf_op jit(solution)/shard_map/dot_general | solution.py:74
  64.2 1.9 collective-permute-start.6
  66.2 4.6 %collective-permute-start.7 = (bf16[12,4224]{1,0:T(8,128)(2,1)S(1)}, bf16[12,4224]{1,0:T(8,128)(2,1)S(1)}, u32[]{:S(2)}, u32[]{:S(2)}) collective-permute-start(bf16[12,4224]{1,0:T(8,128)(2,1)S(1)} %slice.163), channel_id=1, source_target_pairs={{0,7},{1,0},{2,1},{3,2},{4,3},{5,4},{6,5},{7,6},{8,15},{9,8},{10,9... | collective-permute-start | bytes 304136 | tf_op jit(solution)/shard_map/ppermute | solution.py:19
  70.8 2.2 fusion.65
  74.5 3.7 %fusion.64 = bf16[200,512]{1,0:T(8,128)(2,1)} fusion(bf16[200,512]{1,0:T(8,128)(2,1)} %fusion.65, bf16[24,4224]{1,0:T(8,128)(2,1)S(1)} %collective-permute-done.2, bf16[4096,256]{1,0:T(8,128)(2,1)} %bitcast.90, bf16[4096,256]{1,0:T(8,128)(2,1)} %bitcast.98), kind=kOutput, calls=%fused_computation.56 | convolution fusion | flops 109064192 | bytes 4415488 | tf_op jit(solution)/shard_map/dot_general | solution.py:74
  83.9 19.3 %all_gather.14 = bf16[800,512]{1,0:T(8,128)(2,1)S(1)} all-gather(bf16[200,512]{1,0:T(8,128)(2,1)} %constant_dynamic-update-slice_fusion), channel_id=1, replica_groups=mesh['zh'=3,'core'=2,'x'=4,'zl'=4,'y'=8] {'zl'}, dimensions={0}, use_global_device_ids=true | all-gather | bytes 1024000 | tf_op jit(solution)/shard_map/all_gather | solution.py:86
  103.2 4.4 %collective-permute-start.8 = (bf16[800,512]{1,0:T(8,128)(2,1)S(1)}, bf16[800,512]{1,0:T(8,128)(2,1)}, u32[]{:S(2)}, u32[]{:S(2)}) collective-permute-start(bf16[800,512]{1,0:T(8,128)(2,1)S(1)} %all_gather.14), channel_id=1, source_target_pairs={{0,96},{32,0},{64,32},{96,64},{1,97},{33,1},{65,33},{97,65},{2,98}... | collective-permute-start | bytes 2457608 | tf_op jit(solution)/shard_map/ppermute | solution.py:19
  107.6 1.9 collective-permute-start.9
  112.8 5.7 %collective-permute-done.8 = bf16[800,512]{1,0:T(8,128)(2,1)} collective-permute-done((bf16[800,512]{1,0:T(8,128)(2,1)S(1)}, bf16[800,512]{1,0:T(8,128)(2,1)}, u32[]{:S(2)}, u32[]{:S(2)}) %collective-permute-start.8) | collective-permute-done | bytes 819232 | tf_op jit(solution)/shard_map/ppermute | solution.py:19
  119.3 4.4 %collective-permute-done.9 = bf16[800,512]{1,0:T(8,128)(2,1)} collective-permute-done((bf16[800,512]{1,0:T(8,128)(2,1)S(1)}, bf16[800,512]{1,0:T(8,128)(2,1)}, u32[]{:S(2)}, u32[]{:S(2)}) %collective-permute-start.9) | collective-permute-done | bytes 819232 | tf_op jit(solution)/shard_map/ppermute | solution.py:19
  123.7 1.8 slice.182
  125.5 1.9 collective-permute-start.10
  128.6 1.8 slice.183
  130.4 4.7 %collective-permute-start.11 = (bf16[400,512]{1,0:T(8,128)(2,1)}, bf16[400,512]{1,0:T(8,128)(2,1)}, u32[]{:S(2)}, u32[]{:S(2)}) collective-permute-start(bf16[400,512]{1,0:T(8,128)(2,1)} %slice.183), channel_id=1, source_target_pairs={{0,96},{32,0},{64,32},{96,64},{1,97},{33,1},{65,33},{97,65},{2,98}... | collective-permute-start | bytes 1228808 | tf_op jit(solution)/shard_map/ppermute | solution.py:19
  144.3 2.0 copy.64
  147.6 2.1 fusion
  149.7 3.4 %fusion.55 = bf16[256,256]{0,1:T(8,128)(2,1)S(1)} fusion(bf16[1,4096,256]{2,1,0:T(8,128)(2,1)} %param.14, bf16[256,4096]{1,0:T(8,128)(2,1)} %all-gather.3.cloned.1.call-done, f32[4096]{0:T(1024)S(1)} %bitcast.82, f32[256]{0:T(256)S(1)} %add_rsqrt_fusion), kind=kOutput, calls=%fused_computation.46 | convolution fusion | flops 541130752 | bytes 4342784 | tf_op jit(solution)/shard_map/dot_general | solution.py:94
  157.7 2.6 %fusion.5 = (f32[4,256]{1,0:T(4,128)S(1)}, f32[4,256]{1,0:T(4,128)S(1)}, f32[4,256]{1,0:T(4,128)S(1)}, f32[4,256]{1,0:T(4,128)S(1)}, f32[4,256,800]{1,2,0:T(8,128)S(1)}) fusion(f32[800]{0:T(1024)S(1)} %mul.74, pred[800]{0:T(1024)(128)(4,1)S(1)} %broadcast_in_dim.69, f32[4,256,800]{1,2,0:T(8,128)S(1)} %fusion.90, f32[800]{0:T(1024)S(1)} %mul.72, ...), kind=kOutput, calls=%fused_computation.13 | convolution fusion | flops 114683904 | bytes 13677856 | tf_op jit(solution)/shard_map/qhd,khd->hqk/dot_general | solution.py:50
  161.1 2.1 convolution_convert_fusion
  163.2 47.5 %reduce-scatter.2.cloned.1.call-done = bf16[256,512]{1,0:T(8,128)(2,1)} async-done(((bf16[256,4096]{1,0:T(8,128)(2,1)}), bf16[256,512]{1,0:T(8,128)(2,1)}) %reduce-scatter.2.cloned.1.call-update) | async-done | bytes 262160 | tf_op jit(solution)/shard_map/reduce_scatter | solution.py:111
  210.7 12.9 %collective-permute-start.12 = (bf16[256,512]{1,0:T(8,128)(2,1)}, bf16[256,512]{1,0:T(8,128)(2,1)S(1)}, u32[]{:S(2)}, u32[]{:S(2)}) collective-permute-start(bf16[256,512]{1,0:T(8,128)(2,1)} %reduce-scatter.2.cloned.1.call-done), channel_id=1, source_target_pairs={{0,128},{128,256},{256,384},{384,512},{512,640},{640,0},{1,129},{1... | collective-permute-start | bytes 786440 | tf_op jit(solution)/shard_map/ppermute | solution.py:19
  223.6 12.0 %collective-permute-done.12 = bf16[256,512]{1,0:T(8,128)(2,1)S(1)} collective-permute-done((bf16[256,512]{1,0:T(8,128)(2,1)}, bf16[256,512]{1,0:T(8,128)(2,1)S(1)}, u32[]{:S(2)}, u32[]{:S(2)}) %collective-permute-start.12) | collective-permute-done | bytes 262176 | tf_op jit(solution)/shard_map/ppermute | solution.py:19
  (112 shorter events, 31.6 us)
Async XLA Ops:
  6.5 154.5 %copy-start = (bf16[1,256,4096]{2,1,0:T(8,128)(2,1)S(1)}, bf16[1,256,4096]{2,1,0:T(8,128)(2,1)}, u32[]{:S(2)}) copy-start(bf16[1,256,4096]{2,1,0:T(8,128)(2,1)} %param.17) | copy-start | bytes 6291460
  6.5 141.1 %all-gather.3.cloned.1.call-start = ((), (), s32[]{:S(2)}) async-start(), calls=%async_computation.1 | async-start | bytes 2359296 | tf_op jit(solution)/shard_map/all_gather | solution.py:90
  35.4 8.2 %collective-permute-start.3 = (bf16[24,4224]{1,0:T(8,128)(2,1)S(1)}, bf16[24,4224]{1,0:T(8,128)(2,1)S(1)}, u32[]{:S(2)}, u32[]{:S(2)}) collective-permute-start(bf16[24,4224]{1,0:T(8,128)(2,1)S(1)} %all_gather.13), channel_id=1, source_target_pairs={{0,1},{1,2},{2,3},{3,4},{4,5},{5,6},{6,7},{7,0},{8,9},{9,10},{10,1... | collective-permute-start | bytes 608264 | tf_op jit(solution)/shard_map/ppermute | solution.py:19
  38.6 6.9 %collective-permute-start = (bf16[24,4224]{1,0:T(8,128)(2,1)S(1)}, bf16[24,4224]{1,0:T(8,128)(2,1)S(1)}, u32[]{:S(2)}, u32[]{:S(2)}) collective-permute-start(bf16[24,4224]{1,0:T(8,128)(2,1)S(1)} %all_gather.13), channel_id=1, source_target_pairs={{0,7},{1,0},{2,1},{3,2},{4,3},{5,4},{6,5},{7,6},{8,15},{9,8},{10,9... | collective-permute-start | bytes 608264 | tf_op jit(solution)/shard_map/ppermute | solution.py:19
  43.6 10.2 %collective-permute-start.4 = (bf16[24,4224]{1,0:T(8,128)(2,1)S(1)}, bf16[24,4224]{1,0:T(8,128)(2,1)S(1)}, u32[]{:S(2)}, u32[]{:S(2)}) collective-permute-start(bf16[24,4224]{1,0:T(8,128)(2,1)S(1)} %collective-permute-done.3), channel_id=1, source_target_pairs={{0,1},{1,2},{2,3},{3,4},{4,5},{5,6},{6,7},{7,0},{8,9},{9,10},{10,1... | collective-permute-start | bytes 608264 | tf_op jit(solution)/shard_map/ppermute | solution.py:19
  45.5 8.2 %copy-start.8 = (bf16[24,4224]{1,0:T(8,128)(2,1)}, bf16[24,4224]{1,0:T(8,128)(2,1)S(1)}, u32[]{:S(2)}) copy-start(bf16[24,4224]{1,0:T(8,128)(2,1)S(1)} %collective-permute-done) | copy-start | bytes 608260
  45.5 10.5 %collective-permute-start.1 = (bf16[24,4224]{1,0:T(8,128)(2,1)S(1)}, bf16[24,4224]{1,0:T(8,128)(2,1)}, u32[]{:S(2)}, u32[]{:S(2)}) collective-permute-start(bf16[24,4224]{1,0:T(8,128)(2,1)S(1)} %collective-permute-done), channel_id=1, source_target_pairs={{0,7},{1,0},{2,1},{3,2},{4,3},{5,4},{6,5},{7,6},{8,15},{9,8},{10,9... | collective-permute-start | bytes 608264 | tf_op jit(solution)/shard_map/ppermute | solution.py:19
  53.8 17.0 %copy-start.9 = (bf16[1,4096,256]{2,1,0:T(8,128)(2,1)S(1)}, bf16[1,4096,256]{2,1,0:T(8,128)(2,1)}, u32[]{:S(2)}) copy-start(bf16[1,4096,256]{2,1,0:T(8,128)(2,1)} %param.16) | copy-start | bytes 6291460
  53.8 17.0 %copy-start.11 = (bf16[1,4096,256]{2,1,0:T(8,128)(2,1)S(1)}, bf16[1,4096,256]{2,1,0:T(8,128)(2,1)}, u32[]{:S(2)}) copy-start(bf16[1,4096,256]{2,1,0:T(8,128)(2,1)} %param.15) | copy-start | bytes 6291460
  53.8 10.4 %collective-permute-start.5 = (bf16[24,4224]{1,0:T(8,128)(2,1)S(1)}, bf16[24,4224]{1,0:T(8,128)(2,1)S(1)}, u32[]{:S(2)}, u32[]{:S(2)}) collective-permute-start(bf16[24,4224]{1,0:T(8,128)(2,1)S(1)} %collective-permute-done.4), channel_id=1, source_target_pairs={{0,1},{1,2},{2,3},{3,4},{4,5},{5,6},{6,7},{7,0},{8,9},{9,10},{10,1... | collective-permute-start | bytes 608264 | tf_op jit(solution)/shard_map/ppermute | solution.py:19
  56.0 10.2 %collective-permute-start.2 = (bf16[24,4224]{1,0:T(8,128)(2,1)}, bf16[24,4224]{1,0:T(8,128)(2,1)S(1)}, u32[]{:S(2)}, u32[]{:S(2)}) collective-permute-start(bf16[24,4224]{1,0:T(8,128)(2,1)} %collective-permute-done.1), channel_id=1, source_target_pairs={{0,7},{1,0},{2,1},{3,2},{4,3},{5,4},{6,5},{7,6},{8,15},{9,8},{10,9... | collective-permute-start | bytes 608264 | tf_op jit(solution)/shard_map/ppermute | solution.py:19
  64.2 9.9 %collective-permute-start.6 = (bf16[12,4224]{1,0:T(8,128)(2,1)S(1)}, bf16[12,4224]{1,0:T(8,128)(2,1)S(1)}, u32[]{:S(2)}, u32[]{:S(2)}) collective-permute-start(bf16[12,4224]{1,0:T(8,128)(2,1)S(1)} %slice.162), channel_id=1, source_target_pairs={{0,1},{1,2},{2,3},{3,4},{4,5},{5,6},{6,7},{7,0},{8,9},{9,10},{10,1... | collective-permute-start | bytes 304136 | tf_op jit(solution)/shard_map/ppermute | solution.py:19
  66.2 7.9 %collective-permute-start.7 = (bf16[12,4224]{1,0:T(8,128)(2,1)S(1)}, bf16[12,4224]{1,0:T(8,128)(2,1)S(1)}, u32[]{:S(2)}, u32[]{:S(2)}) collective-permute-start(bf16[12,4224]{1,0:T(8,128)(2,1)S(1)} %slice.163), channel_id=1, source_target_pairs={{0,7},{1,0},{2,1},{3,2},{4,3},{5,4},{6,5},{7,6},{8,15},{9,8},{10,9... | collective-permute-start | bytes 304136 | tf_op jit(solution)/shard_map/ppermute | solution.py:19
  74.4 136.3 %reduce-scatter.2.cloned.1.call-start = ((), (), s32[]{:S(2)}) async-start(), calls=%async_computation.2 | async-start | bytes 2359296 | tf_op jit(solution)/shard_map/reduce_scatter | solution.py:111
  74.4 3.7 %copy-start.10 = (bf16[1,4096,256]{2,1,0:T(8,128)(2,1)S(1)}, bf16[1,4096,256]{2,1,0:T(8,128)(2,1)}, u32[]{:S(2)}) copy-start(bf16[1,4096,256]{2,1,0:T(8,128)(2,1)} %param.16) | copy-start | bytes 6291460
  74.4 3.7 %copy-start.12 = (bf16[1,4096,256]{2,1,0:T(8,128)(2,1)S(1)}, bf16[1,4096,256]{2,1,0:T(8,128)(2,1)}, u32[]{:S(2)}) copy-start(bf16[1,4096,256]{2,1,0:T(8,128)(2,1)} %param.15) | copy-start | bytes 6291460
  82.0 27.6 %copy-start.7 = (bf16[1,4096]{1,0:T(2,128)(2,1)S(1)}, bf16[1,4096]{1,0:T(2,128)(2,1)}, u32[]{:S(2)}) copy-start(bf16[1,4096]{1,0:T(2,128)(2,1)} %param.13) | copy-start | bytes 24580
  103.2 15.4 %collective-permute-start.8 = (bf16[800,512]{1,0:T(8,128)(2,1)S(1)}, bf16[800,512]{1,0:T(8,128)(2,1)}, u32[]{:S(2)}, u32[]{:S(2)}) collective-permute-start(bf16[800,512]{1,0:T(8,128)(2,1)S(1)} %all_gather.14), channel_id=1, source_target_pairs={{0,96},{32,0},{64,32},{96,64},{1,97},{33,1},{65,33},{97,65},{2,98}... | collective-permute-start | bytes 2457608 | tf_op jit(solution)/shard_map/ppermute | solution.py:19
  107.6 16.1 %collective-permute-start.9 = (bf16[800,512]{1,0:T(8,128)(2,1)S(1)}, bf16[800,512]{1,0:T(8,128)(2,1)}, u32[]{:S(2)}, u32[]{:S(2)}) collective-permute-start(bf16[800,512]{1,0:T(8,128)(2,1)S(1)} %all_gather.14), channel_id=1, source_target_pairs={{0,32},{32,64},{64,96},{96,0},{1,33},{33,65},{65,97},{97,1},{2,34}... | collective-permute-start | bytes 2457608 | tf_op jit(solution)/shard_map/ppermute | solution.py:19
  125.5 15.7 %collective-permute-start.10 = (bf16[400,512]{1,0:T(8,128)(2,1)}, bf16[400,512]{1,0:T(8,128)(2,1)}, u32[]{:S(2)}, u32[]{:S(2)}) collective-permute-start(bf16[400,512]{1,0:T(8,128)(2,1)} %slice.182), channel_id=1, source_target_pairs={{0,32},{32,64},{64,96},{96,0},{1,33},{33,65},{65,97},{97,1},{2,34}... | collective-permute-start | bytes 1228808 | tf_op jit(solution)/shard_map/ppermute | solution.py:19
  130.4 11.8 %collective-permute-start.11 = (bf16[400,512]{1,0:T(8,128)(2,1)}, bf16[400,512]{1,0:T(8,128)(2,1)}, u32[]{:S(2)}, u32[]{:S(2)}) collective-permute-start(bf16[400,512]{1,0:T(8,128)(2,1)} %slice.183), channel_id=1, source_target_pairs={{0,96},{32,0},{64,32},{96,64},{1,97},{33,1},{65,33},{97,65},{2,98}... | collective-permute-start | bytes 1228808 | tf_op jit(solution)/shard_map/ppermute | solution.py:19
  149.7 3.5 %copy-start.4 = (bf16[800,256]{0,1:T(8,128)(2,1)S(1)}, bf16[800,256]{0,1:T(8,128)(2,1)}, u32[]{:S(2)}) copy-start(bf16[800,256]{0,1:T(8,128)(2,1)} %copy.64) | copy-start | bytes 1228804
  153.1 1.0 copy-start.3
  153.2 1.6 copy-start.1
  154.8 1.4 copy-start.2
  156.2 1.5 copy-start.6
  157.7 2.6 %copy-start.5 = (bf16[800,256]{0,1:T(8,128)(2,1)S(1)}, bf16[800,256]{0,1:T(8,128)(2,1)}, u32[]{:S(2)}) copy-start(bf16[800,256]{0,1:T(8,128)(2,1)} %copy.60) | copy-start | bytes 1228804
  210.7 24.9 %collective-permute-start.12 = (bf16[256,512]{1,0:T(8,128)(2,1)}, bf16[256,512]{1,0:T(8,128)(2,1)S(1)}, u32[]{:S(2)}, u32[]{:S(2)}) collective-permute-start(bf16[256,512]{1,0:T(8,128)(2,1)} %reduce-scatter.2.cloned.1.call-done), channel_id=1, source_target_pairs={{0,128},{128,256},{256,384},{384,512},{512,640},{640,0},{1,129},{1... | collective-permute-start | bytes 786440 | tf_op jit(solution)/shard_map/ppermute | solution.py:19
Sparse Core Ops, SparseCore 0:
  74.5 45.0 all-gather.2
  163.3 47.3 reduce-scatter.1

commit v10 on v7

--- a/solution.py
+++ b/solution.py
@@ -69,14 +69,20 @@
     packed = lax.all_gather(packed, "zh", axis=0, tiled=True)
     both = jnp.concatenate([w_key[0], w_value[0]], axis=1)
     pieces = ring_pieces(packed, HEAD)
+    length = len(pieces)
+    groups = [[pieces[0]]] + [
+        [pieces[r], pieces[-r % length]] if r != length - r else [pieces[r]]
+        for r in range(1, length // 2 + 1)
+    ]
+    groups = [jnp.concatenate(g, axis=0) if len(g) > 1 else g[0] for g in groups]
     kv = jnp.concatenate(
         [
-            jnp.dot(p[:, :model], both, preferred_element_type=jnp.float32).astype(jnp.bfloat16)
-            for p in pieces
+            jnp.dot(g[:, :model], both, preferred_element_type=jnp.float32).astype(jnp.bfloat16)
+            for g in groups
         ],
         axis=0,
     )
-    packed = jnp.concatenate([p[:, model:model + 1] for p in pieces], axis=0)
+    packed = jnp.concatenate([g[:, model:model + 1] for g in groups], axis=0)
     key_rows = kv
     width = w_key.shape[2]
     rows = key_rows.shape[0]

time: 234 us -> 238 us (1.017)
  waiting for transfers between devices: 76.8 us -> 83.6 us
  matrix products: 24.3 us -> 20.6 us
    ppermute x13, waiting for transfers between devices: 30.3 us -> 34.1 us  [shifted(): lax.ppermute(x, axis, [(i, (i + by) % length) for i in range(length)])]
    dot_general x8 -> x5, matrix products: 14.6 us -> 10.9 us  [shards(): jnp.dot(g[:, :model], both, preferred_element_type=jnp.float32)]
    reduce_scatter x1, waiting for transfers between devices: 46.5 us -> 49.4 us  [shards(): lax.psum_scatter(partial_terms.astype(jnp.bfloat16), HEAD, scatter_dimens...]
    unnamed x31 -> x32, local copies, waits for them, and re-layouts: 7.58 us -> 8.83 us
  transfers between devices with their start and end apart: 15 -> 15, of which waited for: 7 -> 8; matrix products, arithmetic and copies ran while one was open for 11% -> 10% of each run, Pallas kernels for 0% -> 0%
where the time goes in v10:
time: 238 us; the launch traced here: 237 us
  waiting for transfers between devices  83.6 us (35%)
  starting transfers between devices  52.2 us (22%)
  blocking collectives  46.7 us (20%)
  matrix products  20.6 us (9%)
  local copies, waits for them, and re-layouts  15.5 us (7%)
  between operations  13.8 us (6%)
  other arithmetic  4.89 us (2%)
    ppermute x13, starting transfers between devices, shifted(): lax.ppermute(x, axis, [(i, (i + by) % length) for i in range(length)])  52.2 us
    reduce_scatter x1, waiting for transfers between devices, shards(): lax.psum_scatter(partial_terms.astype(jnp.bfloat16), HEAD, scatter_dimens...  49.4 us
    ppermute x13, waiting for transfers between devices, shifted(): lax.ppermute(x, axis, [(i, (i + by) % length) for i in range(length)])  34.1 us
    all_gather x1, blocking collectives, shards(): kv = lax.all_gather(kv, 'zl', axis=0, tiled=True)  20.7 us
    all_gather x1, blocking collectives, shards(): packed = lax.all_gather(packed, 'zh', axis=0, tiled=True)  14 us
    all_gather x1, blocking collectives, shards(): packed = lax.all_gather(packed, 'core', axis=0, tiled=True)  12 us
    dot_general x5, matrix products, shards(): jnp.dot(g[:, :model], both, preferred_element_type=jnp.float32)  10.9 us
    unnamed x32, local copies, waits for them, and re-layouts  8.83 us
  transfers between devices with their start and end apart: 15, of which 8 were waited for; matrix products, arithmetic and copies ran while one was open for 10% of the time, Pallas kernels for 0%

profile of v10, /device:TPU:1, one launch (start us, length us, event | category | flops | bytes accessed | tf_op | source)
XLA Modules:
  0.0 237.3 jit_solution(18406314986329373180)
XLA Ops:
  9.4 12.0 %all-gather = bf16[2,4,4224]{2,1,0:T(4,128)(2,1)S(1)} all-gather(bf16[1,4,4224]{2,1,0:T(4,128)(2,1)S(1)} %fusion.41), channel_id=1, replica_groups=mesh['zh'=3,'core'=2,'x'=4,'zl'=4,'y'=8] {'core'}, dimensions={0}, use_global_device_ids=true | all-gather | bytes 101376 | tf_op jit(solution)/shard_map/all_gather | solution.py:68
  21.4 14.0 %all_gather.13 = bf16[24,4224]{1,0:T(8,128)(2,1)S(1)} all-gather(bf16[8,4224]{1,0:T(8,128)(2,1)S(1)} %reshape.105), channel_id=1, replica_groups=mesh['zh'=3,'core'=2,'x'=4,'zl'=4,'y'=8] {'zh'}, dimensions={0}, use_global_device_ids=true | all-gather | bytes 270336 | tf_op jit(solution)/shard_map/all_gather | solution.py:69
  35.4 3.2 %collective-permute-start.1 = (bf16[24,4224]{1,0:T(8,128)(2,1)S(1)}, bf16[24,4224]{1,0:T(8,128)(2,1)S(1)}, u32[]{:S(2)}, u32[]{:S(2)}) collective-permute-start(bf16[24,4224]{1,0:T(8,128)(2,1)S(1)} %all_gather.13), channel_id=1, source_target_pairs={{0,1},{1,2},{2,3},{3,4},{4,5},{5,6},{6,7},{7,0},{8,9},{9,10},{10,1... | collective-permute-start | bytes 608264 | tf_op jit(solution)/shard_map/ppermute | solution.py:19
  38.6 3.8 %collective-permute-start = (bf16[24,4224]{1,0:T(8,128)(2,1)S(1)}, bf16[24,4224]{1,0:T(8,128)(2,1)S(1)}, u32[]{:S(2)}, u32[]{:S(2)}) collective-permute-start(bf16[24,4224]{1,0:T(8,128)(2,1)S(1)} %all_gather.13), channel_id=1, source_target_pairs={{0,7},{1,0},{2,1},{3,2},{4,3},{5,4},{6,5},{7,6},{8,15},{9,8},{10,9... | collective-permute-start | bytes 608264 | tf_op jit(solution)/shard_map/ppermute | solution.py:19
  42.5 2.9 %fusion.32 = bf16[200,512]{1,0:T(8,128)(2,1)S(1)} fusion(bf16[24,4224]{1,0:T(8,128)(2,1)S(1)} %all_gather.13, bf16[4096,256]{1,0:T(8,128)(2,1)} %bitcast.47, bf16[4096,256]{1,0:T(8,128)(2,1)} %bitcast.52), kind=kOutput, calls=%fused_computation.30 | convolution fusion | flops 109064192 | bytes 4415488 | tf_op jit(solution)/shard_map/dot_general | solution.py:80
  46.3 2.8 %collective-permute-start.3 = (bf16[24,4224]{1,0:T(8,128)(2,1)S(1)}, bf16[24,4224]{1,0:T(8,128)(2,1)S(1)}, u32[]{:S(2)}, u32[]{:S(2)}) collective-permute-start(bf16[24,4224]{1,0:T(8,128)(2,1)S(1)} %collective-permute-done.1), channel_id=1, source_target_pairs={{0,1},{1,2},{2,3},{3,4},{4,5},{5,6},{6,7},{7,0},{8,9},{9,10},{10,1... | collective-permute-start | bytes 608264 | tf_op jit(solution)/shard_map/ppermute | solution.py:19
  49.2 3.7 %collective-permute-start.2 = (bf16[24,4224]{1,0:T(8,128)(2,1)S(1)}, bf16[24,4224]{1,0:T(8,128)(2,1)S(1)}, u32[]{:S(2)}, u32[]{:S(2)}) collective-permute-start(bf16[24,4224]{1,0:T(8,128)(2,1)S(1)} %collective-permute-done), channel_id=1, source_target_pairs={{0,7},{1,0},{2,1},{3,2},{4,3},{5,4},{6,5},{7,6},{8,15},{9,8},{10,9... | collective-permute-start | bytes 608264 | tf_op jit(solution)/shard_map/ppermute | solution.py:19
  52.9 3.2 %fusion.30 = bf16[200,512]{1,0:T(8,128)(2,1)S(1)} fusion(bf16[200,512]{1,0:T(8,128)(2,1)S(1)} %fusion.32, bf16[48,4224]{1,0:T(8,128)(2,1)} %copy-done.4, bf16[4096,256]{1,0:T(8,128)(2,1)} %bitcast.48, bf16[4096,256]{1,0:T(8,128)(2,1)} %bitcast.53), kind=kOutput, calls=%fused_computation.26 | convolution fusion | flops 209739776 | bytes 4636672 | tf_op jit(solution)/shard_map/dot_general | solution.py:80
  56.8 3.7 %collective-permute-start.4 = (bf16[24,4224]{1,0:T(8,128)(2,1)S(1)}, bf16[24,4224]{1,0:T(8,128)(2,1)S(1)}, u32[]{:S(2)}, u32[]{:S(2)}) collective-permute-start(bf16[24,4224]{1,0:T(8,128)(2,1)S(1)} %collective-permute-done.2), channel_id=1, source_target_pairs={{0,7},{1,0},{2,1},{3,2},{4,3},{5,4},{6,5},{7,6},{8,15},{9,8},{10,9... | collective-permute-start | bytes 608264 | tf_op jit(solution)/shard_map/ppermute | solution.py:19
  60.6 2.4 %collective-permute-start.5 = (bf16[24,4224]{1,0:T(8,128)(2,1)S(1)}, bf16[24,4224]{1,0:T(8,128)(2,1)S(1)}, u32[]{:S(2)}, u32[]{:S(2)}) collective-permute-start(bf16[24,4224]{1,0:T(8,128)(2,1)S(1)} %collective-permute-done.3), channel_id=1, source_target_pairs={{0,1},{1,2},{2,3},{3,4},{4,5},{5,6},{6,7},{7,0},{8,9},{9,10},{10,1... | collective-permute-start | bytes 608264 | tf_op jit(solution)/shard_map/ppermute | solution.py:19
  63.9 4.4 %collective-permute-done.5 = bf16[24,4224]{1,0:T(8,128)(2,1)S(1)} collective-permute-done((bf16[24,4224]{1,0:T(8,128)(2,1)S(1)}, bf16[24,4224]{1,0:T(8,128)(2,1)S(1)}, u32[]{:S(2)}, u32[]{:S(2)}) %collective-permute-start.5) | collective-permute-done | bytes 202784 | tf_op jit(solution)/shard_map/ppermute | solution.py:19
  70.3 4.6 %collective-permute-start.7 = (bf16[12,4224]{1,0:T(8,128)(2,1)S(1)}, bf16[12,4224]{1,0:T(8,128)(2,1)S(1)}, u32[]{:S(2)}, u32[]{:S(2)}) collective-permute-start(bf16[12,4224]{1,0:T(8,128)(2,1)S(1)} %slice.107), channel_id=1, source_target_pairs={{0,7},{1,0},{2,1},{3,2},{4,3},{5,4},{6,5},{7,6},{8,15},{9,8},{10,9... | collective-permute-start | bytes 304136 | tf_op jit(solution)/shard_map/ppermute | solution.py:19
  77.2 3.3 %fusion.29 = bf16[200,512]{1,0:T(8,128)(2,1)S(1)} fusion(bf16[200,512]{1,0:T(8,128)(2,1)S(1)} %fusion.30, bf16[48,4224]{1,0:T(8,128)(2,1)} %copy-done.3, bf16[4096,256]{1,0:T(8,128)(2,1)} %bitcast.49, bf16[4096,256]{1,0:T(8,128)(2,1)} %bitcast.54), kind=kOutput, calls=%fused_computation.24 | convolution fusion | flops 209739776 | bytes 4636672 | tf_op jit(solution)/shard_map/dot_general | solution.py:80
  82.4 20.7 %all_gather.14 = bf16[800,512]{1,0:T(8,128)(2,1)S(1)} all-gather(bf16[200,512]{1,0:T(8,128)(2,1)S(1)} %constant_dynamic-update-slice_fusion.6), channel_id=1, replica_groups=mesh['zh'=3,'core'=2,'x'=4,'zl'=4,'y'=8] {'zl'}, dimensions={0}, use_global_device_ids=true | all-gather | bytes 1024000 | tf_op jit(solution)/shard_map/all_gather | solution.py:92
  103.1 3.1 %collective-permute-start.9 = (bf16[800,512]{1,0:T(8,128)(2,1)S(1)}, bf16[800,512]{1,0:T(8,128)(2,1)S(1)}, u32[]{:S(2)}, u32[]{:S(2)}) collective-permute-start(bf16[800,512]{1,0:T(8,128)(2,1)S(1)} %all_gather.14), channel_id=1, source_target_pairs={{0,32},{32,64},{64,96},{96,0},{1,33},{33,65},{65,97},{97,1},{2,34}... | collective-permute-start | bytes 2457608 | tf_op jit(solution)/shard_map/ppermute | solution.py:19
  106.2 3.4 %collective-permute-start.8 = (bf16[800,512]{1,0:T(8,128)(2,1)S(1)}, bf16[800,512]{1,0:T(8,128)(2,1)S(1)}, u32[]{:S(2)}, u32[]{:S(2)}) collective-permute-start(bf16[800,512]{1,0:T(8,128)(2,1)S(1)} %all_gather.14), channel_id=1, source_target_pairs={{0,96},{32,0},{64,32},{96,64},{1,97},{33,1},{65,33},{97,65},{2,98}... | collective-permute-start | bytes 2457608 | tf_op jit(solution)/shard_map/ppermute | solution.py:19
  109.6 10.3 %collective-permute-done.9 = bf16[800,512]{1,0:T(8,128)(2,1)S(1)} collective-permute-done((bf16[800,512]{1,0:T(8,128)(2,1)S(1)}, bf16[800,512]{1,0:T(8,128)(2,1)S(1)}, u32[]{:S(2)}, u32[]{:S(2)}) %collective-permute-start.9) | collective-permute-done | bytes 819232 | tf_op jit(solution)/shard_map/ppermute | solution.py:19
  119.9 1.9 collective-permute-start.10
  121.9 4.8 %collective-permute-start.11 = (bf16[400,512]{1,0:T(8,128)(2,1)S(1)}, bf16[400,512]{1,0:T(8,128)(2,1)S(1)}, u32[]{:S(2)}, u32[]{:S(2)}) collective-permute-start(bf16[400,512]{1,0:T(8,128)(2,1)S(1)} %slice.115), channel_id=1, source_target_pairs={{0,96},{32,0},{64,32},{96,64},{1,97},{33,1},{65,33},{97,65},{2,98}... | collective-permute-start | bytes 1228808 | tf_op jit(solution)/shard_map/ppermute | solution.py:19
  126.8 3.7 %collective-permute-done.10 = bf16[400,512]{1,0:T(8,128)(2,1)S(1)} collective-permute-done((bf16[400,512]{1,0:T(8,128)(2,1)S(1)}, bf16[400,512]{1,0:T(8,128)(2,1)S(1)}, u32[]{:S(2)}, u32[]{:S(2)}) %collective-permute-start.10) | collective-permute-done | bytes 409632 | tf_op jit(solution)/shard_map/ppermute | solution.py:19
  132.5 2.0 slice.116
  134.6 3.8 %fusion.47 = (bf16[3072,256]{1,0:T(8,128)(2,1)}, bf16[3072,256]{1,0:T(8,128)(2,1)}) fusion(bf16[3072,512]{1,0:T(8,128)(2,1)} %bitcast.35), kind=kLoop, calls=%fused_computation.64 | loop fusion | bytes 6291456 | tf_op jit(solution)/shard_map/slice | solution.py:106
  138.5 2.6 %copy.28 = bf16[3072,256]{0,1:T(8,128)(2,1)} copy(bf16[3072,256]{1,0:T(8,128)(2,1)} %get-tuple-element.31) | data formatting | bytes 3145728
  141.1 2.6 %copy.27 = bf16[3072,256]{0,1:T(8,128)(2,1)} copy(bf16[3072,256]{1,0:T(8,128)(2,1)} %get-tuple-element.32) | data formatting | bytes 3145728
  143.7 2.1 fusion.5
  145.8 3.5 %fusion.17 = bf16[256,256]{0,1:T(8,128)(2,1)S(1)} fusion(bf16[1,4096,256]{2,1,0:T(8,128)(2,1)} %param.14, bf16[256,4096]{1,0:T(8,128)(2,1)} %all-gather.3.cloned.1.call-done, f32[4096]{0:T(1024)S(1)} %bitcast.44, f32[256]{0:T(256)S(1)} %add_rsqrt_fusion), kind=kOutput, calls=%fused_computation.18 | convolution fusion | flops 541130752 | bytes 4342784 | tf_op jit(solution)/shard_map/dot_general | solution.py:103
  149.3 2.1 fusion
  151.4 2.0 fusion.25
  153.4 2.1 convolution_convert_fusion
  155.5 49.4 %reduce-scatter.2.cloned.1.call-done = bf16[256,512]{1,0:T(8,128)(2,1)} async-done(((bf16[256,4096]{1,0:T(8,128)(2,1)}), bf16[256,512]{1,0:T(8,128)(2,1)}) %reduce-scatter.2.cloned.1.call-update) | async-done | bytes 262160 | tf_op jit(solution)/shard_map/reduce_scatter | solution.py:111
  205.0 12.8 %collective-permute-start.12 = (bf16[256,512]{1,0:T(8,128)(2,1)}, bf16[256,512]{1,0:T(8,128)(2,1)S(1)}, u32[]{:S(2)}, u32[]{:S(2)}) collective-permute-start(bf16[256,512]{1,0:T(8,128)(2,1)} %reduce-scatter.2.cloned.1.call-done), channel_id=1, source_target_pairs={{0,128},{128,256},{256,384},{384,512},{512,640},{640,0},{1,129},{1... | collective-permute-start | bytes 786440 | tf_op jit(solution)/shard_map/ppermute | solution.py:19
  217.7 12.0 %collective-permute-done.12 = bf16[256,512]{1,0:T(8,128)(2,1)S(1)} collective-permute-done((bf16[256,512]{1,0:T(8,128)(2,1)}, bf16[256,512]{1,0:T(8,128)(2,1)S(1)}, u32[]{:S(2)}, u32[]{:S(2)}) %collective-permute-start.12) | collective-permute-done | bytes 262176 | tf_op jit(solution)/shard_map/ppermute | solution.py:19
  (74 shorter events, 14.5 us)
Async XLA Ops:
  6.5 146.9 %copy-start = (bf16[1,256,4096]{2,1,0:T(8,128)(2,1)S(1)}, bf16[1,256,4096]{2,1,0:T(8,128)(2,1)}, u32[]{:S(2)}) copy-start(bf16[1,256,4096]{2,1,0:T(8,128)(2,1)} %param.17) | copy-start | bytes 6291460
  6.5 137.1 %all-gather.3.cloned.1.call-start = ((), (), s32[]{:S(2)}) async-start(), calls=%async_computation.1 | async-start | bytes 2359296 | tf_op jit(solution)/shard_map/all_gather | solution.py:99
  35.4 10.1 %collective-permute-start.1 = (bf16[24,4224]{1,0:T(8,128)(2,1)S(1)}, bf16[24,4224]{1,0:T(8,128)(2,1)S(1)}, u32[]{:S(2)}, u32[]{:S(2)}) collective-permute-start(bf16[24,4224]{1,0:T(8,128)(2,1)S(1)} %all_gather.13), channel_id=1, source_target_pairs={{0,1},{1,2},{2,3},{3,4},{4,5},{5,6},{6,7},{7,0},{8,9},{9,10},{10,1... | collective-permute-start | bytes 608264 | tf_op jit(solution)/shard_map/ppermute | solution.py:19
  38.6 6.8 %collective-permute-start = (bf16[24,4224]{1,0:T(8,128)(2,1)S(1)}, bf16[24,4224]{1,0:T(8,128)(2,1)S(1)}, u32[]{:S(2)}, u32[]{:S(2)}) collective-permute-start(bf16[24,4224]{1,0:T(8,128)(2,1)S(1)} %all_gather.13), channel_id=1, source_target_pairs={{0,7},{1,0},{2,1},{3,2},{4,3},{5,4},{6,5},{7,6},{8,15},{9,8},{10,9... | collective-permute-start | bytes 608264 | tf_op jit(solution)/shard_map/ppermute | solution.py:19
  45.5 0.8 copy-start.4
  46.3 14.3 %collective-permute-start.3 = (bf16[24,4224]{1,0:T(8,128)(2,1)S(1)}, bf16[24,4224]{1,0:T(8,128)(2,1)S(1)}, u32[]{:S(2)}, u32[]{:S(2)}) collective-permute-start(bf16[24,4224]{1,0:T(8,128)(2,1)S(1)} %collective-permute-done.1), channel_id=1, source_target_pairs={{0,1},{1,2},{2,3},{3,4},{4,5},{5,6},{6,7},{7,0},{8,9},{9,10},{10,1... | collective-permute-start | bytes 608264 | tf_op jit(solution)/shard_map/ppermute | solution.py:19
  49.2 7.7 %collective-permute-start.2 = (bf16[24,4224]{1,0:T(8,128)(2,1)S(1)}, bf16[24,4224]{1,0:T(8,128)(2,1)S(1)}, u32[]{:S(2)}, u32[]{:S(2)}) collective-permute-start(bf16[24,4224]{1,0:T(8,128)(2,1)S(1)} %collective-permute-done), channel_id=1, source_target_pairs={{0,7},{1,0},{2,1},{3,2},{4,3},{5,4},{6,5},{7,6},{8,15},{9,8},{10,9... | collective-permute-start | bytes 608264 | tf_op jit(solution)/shard_map/ppermute | solution.py:19
  56.8 13.4 %collective-permute-start.4 = (bf16[24,4224]{1,0:T(8,128)(2,1)S(1)}, bf16[24,4224]{1,0:T(8,128)(2,1)S(1)}, u32[]{:S(2)}, u32[]{:S(2)}) collective-permute-start(bf16[24,4224]{1,0:T(8,128)(2,1)S(1)} %collective-permute-done.2), channel_id=1, source_target_pairs={{0,7},{1,0},{2,1},{3,2},{4,3},{5,4},{6,5},{7,6},{8,15},{9,8},{10,9... | collective-permute-start | bytes 608264 | tf_op jit(solution)/shard_map/ppermute | solution.py:19
  60.6 7.7 %collective-permute-start.5 = (bf16[24,4224]{1,0:T(8,128)(2,1)S(1)}, bf16[24,4224]{1,0:T(8,128)(2,1)S(1)}, u32[]{:S(2)}, u32[]{:S(2)}) collective-permute-start(bf16[24,4224]{1,0:T(8,128)(2,1)S(1)} %collective-permute-done.3), channel_id=1, source_target_pairs={{0,1},{1,2},{2,3},{3,4},{4,5},{5,6},{6,7},{7,0},{8,9},{9,10},{10,1... | collective-permute-start | bytes 608264 | tf_op jit(solution)/shard_map/ppermute | solution.py:19
  63.1 0.8 copy-start.3
  68.3 7.5 %collective-permute-start.6 = (bf16[12,4224]{1,0:T(8,128)(2,1)S(1)}, bf16[12,4224]{1,0:T(8,128)(2,1)S(1)}, u32[]{:S(2)}, u32[]{:S(2)}) collective-permute-start(bf16[12,4224]{1,0:T(8,128)(2,1)S(1)} %slice.106), channel_id=1, source_target_pairs={{0,1},{1,2},{2,3},{3,4},{4,5},{5,6},{6,7},{7,0},{8,9},{9,10},{10,1... | collective-permute-start | bytes 304136 | tf_op jit(solution)/shard_map/ppermute | solution.py:19
  70.3 6.5 %collective-permute-start.7 = (bf16[12,4224]{1,0:T(8,128)(2,1)S(1)}, bf16[12,4224]{1,0:T(8,128)(2,1)S(1)}, u32[]{:S(2)}, u32[]{:S(2)}) collective-permute-start(bf16[12,4224]{1,0:T(8,128)(2,1)S(1)} %slice.107), channel_id=1, source_target_pairs={{0,7},{1,0},{2,1},{3,2},{4,3},{5,4},{6,5},{7,6},{8,15},{9,8},{10,9... | collective-permute-start | bytes 304136 | tf_op jit(solution)/shard_map/ppermute | solution.py:19
  74.9 0.7 copy-start.5
  77.1 3.4 %copy-start.6 = (bf16[48,4224]{1,0:T(8,128)(2,1)S(1)}, bf16[48,4224]{1,0:T(8,128)(2,1)}, u32[]{:S(2)}) copy-start(bf16[48,4224]{1,0:T(8,128)(2,1)} %copy-done.5) | copy-start | bytes 1216516
  77.1 127.9 %reduce-scatter.2.cloned.1.call-start = ((), (), s32[]{:S(2)}) async-start(), calls=%async_computation.2 | async-start | bytes 2359296 | tf_op jit(solution)/shard_map/reduce_scatter | solution.py:111
  77.1 3.4 %copy-start.8 = (bf16[1,4096,256]{2,1,0:T(8,128)(2,1)S(1)}, bf16[1,4096,256]{2,1,0:T(8,128)(2,1)}, u32[]{:S(2)}) copy-start(bf16[1,4096,256]{2,1,0:T(8,128)(2,1)} %param.16) | copy-start | bytes 6291460
  77.1 3.7 %copy-start.9 = (bf16[1,4096,256]{2,1,0:T(8,128)(2,1)S(1)}, bf16[1,4096,256]{2,1,0:T(8,128)(2,1)}, u32[]{:S(2)}) copy-start(bf16[1,4096,256]{2,1,0:T(8,128)(2,1)} %param.15) | copy-start | bytes 6291460
  81.7 45.0 %copy-start.7 = (bf16[1,4096]{1,0:T(2,128)(2,1)S(1)}, bf16[1,4096]{1,0:T(2,128)(2,1)}, u32[]{:S(2)}) copy-start(bf16[1,4096]{1,0:T(2,128)(2,1)} %param.13) | copy-start | bytes 24580
  103.1 16.8 %collective-permute-start.9 = (bf16[800,512]{1,0:T(8,128)(2,1)S(1)}, bf16[800,512]{1,0:T(8,128)(2,1)S(1)}, u32[]{:S(2)}, u32[]{:S(2)}) collective-permute-start(bf16[800,512]{1,0:T(8,128)(2,1)S(1)} %all_gather.14), channel_id=1, source_target_pairs={{0,32},{32,64},{64,96},{96,0},{1,33},{33,65},{65,97},{97,1},{2,34}... | collective-permute-start | bytes 2457608 | tf_op jit(solution)/shard_map/ppermute | solution.py:19
  106.2 15.7 %collective-permute-start.8 = (bf16[800,512]{1,0:T(8,128)(2,1)S(1)}, bf16[800,512]{1,0:T(8,128)(2,1)S(1)}, u32[]{:S(2)}, u32[]{:S(2)}) collective-permute-start(bf16[800,512]{1,0:T(8,128)(2,1)S(1)} %all_gather.14), channel_id=1, source_target_pairs={{0,96},{32,0},{64,32},{96,64},{1,97},{33,1},{65,33},{97,65},{2,98}... | collective-permute-start | bytes 2457608 | tf_op jit(solution)/shard_map/ppermute | solution.py:19
  119.9 10.6 %collective-permute-start.10 = (bf16[400,512]{1,0:T(8,128)(2,1)S(1)}, bf16[400,512]{1,0:T(8,128)(2,1)S(1)}, u32[]{:S(2)}, u32[]{:S(2)}) collective-permute-start(bf16[400,512]{1,0:T(8,128)(2,1)S(1)} %slice.114), channel_id=1, source_target_pairs={{0,32},{32,64},{64,96},{96,0},{1,33},{33,65},{65,97},{97,1},{2,34}... | collective-permute-start | bytes 1228808 | tf_op jit(solution)/shard_map/ppermute | solution.py:19
  121.9 10.5 %collective-permute-start.11 = (bf16[400,512]{1,0:T(8,128)(2,1)S(1)}, bf16[400,512]{1,0:T(8,128)(2,1)S(1)}, u32[]{:S(2)}, u32[]{:S(2)}) collective-permute-start(bf16[400,512]{1,0:T(8,128)(2,1)S(1)} %slice.115), channel_id=1, source_target_pairs={{0,96},{32,0},{64,32},{96,64},{1,97},{33,1},{65,33},{97,65},{2,98}... | collective-permute-start | bytes 1228808 | tf_op jit(solution)/shard_map/ppermute | solution.py:19
  145.7 3.5 %copy-start.1 = (bf16[3072,256]{0,1:T(8,128)(2,1)S(1)}, bf16[3072,256]{0,1:T(8,128)(2,1)}, u32[]{:S(2)}) copy-start(bf16[3072,256]{0,1:T(8,128)(2,1)} %copy.28) | copy-start | bytes 4718596
  149.3 2.1 copy-start.2
  205.0 24.8 %collective-permute-start.12 = (bf16[256,512]{1,0:T(8,128)(2,1)}, bf16[256,512]{1,0:T(8,128)(2,1)S(1)}, u32[]{:S(2)}, u32[]{:S(2)}) collective-permute-start(bf16[256,512]{1,0:T(8,128)(2,1)} %reduce-scatter.2.cloned.1.call-done), channel_id=1, source_target_pairs={{0,128},{128,256},{256,384},{384,512},{512,640},{640,0},{1,129},{1... | collective-permute-start | bytes 786440 | tf_op jit(solution)/shard_map/ppermute | solution.py:19
Sparse Core Ops, SparseCore 0:
  77.2 47.9 all-gather.2
  155.7 49.2 reduce-scatter.1
